TPU v7x, 32 devices: a whole 2x2x4 slice. The times are simulated.
32 devices in a mesh: groups: 2 (over y), space: 16 (over z, x, core).
Axes of the slice: x: 2, y: 2, z: 4, core: 2. Of those that a mesh axis runs over, the one named last changes fastest.
Arguments:
- field: float32 [64, 40, 8, 256], P(('groups', 'space')), parts along dimension 0, may hold values from -6 to 6
- grad_out: float32 [64, 40, 8, 256], P(('groups', 'space')), parts along dimension 0, may hold values from -6 to 6
- weight: float32 [256, 27, 256], P('space'), may hold values from -0.078125 to 0.078125
- bias: float32 [256], replicated, may hold values from -3 to 3
- land_bias: float32 [256], replicated, may hold values from -3 to 3
- level_gain: float32 [4, 256], replicated, may hold values from 0.5 to 1.5
- land_mask: int32 [32, 40], P('space'), may hold values 0 or 1
- level_index: int32 [8], replicated, may hold values from 0 to 3, as said below
Outputs:
- grad_field: float32 [64, 40, 8, 256], P(('groups', 'space')), parts along dimension 0
- grad_weight: float32 [512, 27, 256], P(('groups', 'space')), parts along dimension 0
- grad_bias: float32 [512], P('groups'), parts along dimension 0
- grad_land: float32 [512], P('groups'), parts along dimension 0
- grad_gain: float32 [8, 256], P('groups'), parts along dimension 0
There are 2 independent parts, one for each index of `groups`. A program takes and returns all parts, laid end to end along the dimension named above; an argument that names none is the same for every part. Nothing has to cross between parts.
Inputs may be any that keep to these rules, and one draw needn't show every extreme that they name: `level_index`: a gain table row for each level; every row of the table is used by some level.
All inputs are finite; a program needn't handle non-finite values. No bound on the sum of `land_mask` on one device may be relied on, other than what follows from the above.
Results may differ from a plain program's by a relative error of at most 0.00011.
Values sent between devices are 32-bit elements; how exact they have to be, the bound alone decides.
No kernel may reach another device: no remote copies, remote signals or barrier semaphores. Data moves between devices by JAX's collectives and lax.ppermute only.
A program may use at most 128 MiB of HBM per device.

v0:
```python
import jax
import jax.numpy as jnp
from jax import lax
from jax.sharding import PartitionSpec as P

highest = lax.Precision.HIGHEST


def with_halo(array, sides, width):
    for axis, dim in sides:
        count, length = (lax.axis_size(axis), array.shape[dim])
        up = [(i, (i + 1) % count) for i in range(count - 1)]
        down = [(j, i) for i, j in up]
        last = lax.slice_in_dim(array, length - width, length, axis=dim)
        leading = lax.slice_in_dim(array, 0, width, axis=dim)
        before = lax.ppermute(last, axis, up)
        after = lax.ppermute(leading, axis, down)
        array = jnp.concatenate([before, array, after], axis=dim)
    return array


def wrap_levels(field):
    wrapped = jnp.concatenate([field[:, -1:], field, field[:, :1]], axis=1)
    return jnp.pad(wrapped, ((0, 0), (0, 0), (1, 1), (0, 0)))


def window_table(grid, out_rows, flipped):
    lon_n = grid.shape[1] - 2
    lev_n = grid.shape[2] - 2
    chans = grid.shape[3]
    windows = []
    for offset in range(27):
        lat_off, remainder = divmod(offset, 9)
        lon_off, lev_off = divmod(remainder, 3)
        if flipped:
            lat_off, lon_off, lev_off = (2 - lat_off, 2 - lon_off, 2 - lev_off)
        window = grid[
            lat_off : lat_off + out_rows, lon_off : lon_off + lon_n, lev_off : lev_off + lev_n
        ]
        windows.append(window.reshape(-1, chans))
    return jnp.stack(windows, axis=1)


def conv_piece(table, piece):
    return jnp.einsum("rop,poc->rc", table, piece, precision=highest)


def back_piece(table, piece):
    return jnp.einsum("roc,qoc->rq", table, piece, precision=highest)


def per_device(field, grad_out, weight, bias, land_bias, level_gain, land_mask, level_index):
    rows, lon_n, lev_n, chans = field.shape
    land_float = land_mask.astype(jnp.float32)
    one_hot = (
        level_index[:, None] == jnp.arange(level_gain.shape[0], dtype=jnp.int32)[None, :]
    ).astype(jnp.float32)
    gains = jnp.dot(one_hot, level_gain, precision=highest)
    full_weight = lax.all_gather(weight, "space", axis=0, tiled=True)
    grid_pre = wrap_levels(with_halo(field, (("space", 0),), 1))
    table_pre = window_table(grid_pre, rows, False)
    conv = conv_piece(table_pre, full_weight)
    conv = conv.reshape(rows, lon_n, lev_n, chans)
    pre = conv + bias + land_float[:, :, None, None] * land_bias
    sigma = jax.nn.sigmoid(pre)
    active = pre * sigma
    delta = grad_out * gains * sigma * (1.0 + pre * (1.0 - sigma))
    delta_pad = with_halo(delta, (("space", 0),), 1)
    delta_table = window_table(wrap_levels(delta_pad), rows, True)
    back = back_piece(delta_table, full_weight)
    grad_field = grad_out + back.reshape(rows, lon_n, lev_n, chans)
    delta_flat = delta.reshape(-1, chans)
    grad_weight = lax.psum_scatter(
        jnp.einsum("rop,rq->poq", table_pre, delta_flat, precision=highest),
        "space",
        scatter_dimension=0,
        tiled=True,
    )
    local_bias = jnp.sum(delta, axis=(0, 1, 2))
    local_land = jnp.sum(land_float[:, :, None, None] * delta, axis=(0, 1, 2))
    per_level = jnp.sum(grad_out * active, axis=(0, 1))
    local_gain = jnp.dot(one_hot.T, per_level, precision=highest)
    grad_bias, grad_land, grad_gain = lax.psum((local_bias, local_land, local_gain), "space")
    return (grad_field, grad_weight, grad_bias, grad_land, grad_gain)


def solution(mesh):
    in_specs = (
        P(("groups", "space"), None, None, None),
        P(("groups", "space"), None, None, None),
        P("space", None, None),
        P(),
        P(),
        P(),
        P("space", None),
        P(),
    )
    out_specs = (
        P(("groups", "space"), None, None, None),
        P(("groups", "space"), None, None),
        P("groups"),
        P("groups"),
        P("groups", None),
    )
    return jax.shard_map(
        per_device, mesh=mesh, in_specs=in_specs, out_specs=out_specs, check_vma=False
    )
```

profile of v0, /device:TPU:0, one launch (start us, length us, event | category | flops | bytes accessed | tf_op | source)
XLA Modules:
  0.0 242.6 jit_solution(7508774460025754964)
XLA Ops:
  10.4 3.1 %collective-permute-start = (f32[1,40,8,256]{3,2,1,0:T(8,128)S(1)}, f32[1,40,8,256]{3,2,1,0:T(8,128)S(1)}, u32[]{:S(2)}, u32[]{:S(2)}) collective-permute-start(f32[1,40,8,256]{3,2,1,0:T(8,128)S(1)} %get-tuple-element.87), channel_id=1, source_target_pairs={{0,1},{1,2},{2,3},{3,4},{4,5},{5,6},{6,7},{7,8},{8,9},{9,10},{10,1... | collective-permute-start | bytes 983048 | tf_op jit(solution)/shard_map/ppermute | solution.py:16
  15.8 2.7 %pad_maximum_fusion.4 = (f32[2,40,8,256]{3,2,1,0:T(8,128)}, f32[4,40,8,256]{3,2,1,0:T(8,128)S(1)}, f32[2,40,8,256]{3,2,1,0:T(8,128)}) fusion(f32[1,40,8,256]{3,2,1,0:T(8,128)S(1)} %collective-permute-done.1, f32[2,40,8,256]{3,2,1,0:T(8,128)} %param.8, f32[4,40,8,256]{3,2,1,0:T(8,128)S(1)} %constant_dynamic-update-slice_fusion.2, ...), kind=kLoop, calls=%fused_computation.27 | loop fusion | flops 327680 | bytes 3276800 | tf_op jit(solution)/shard_map/concatenate | solution.py:18
  20.1 4.5 %fusion.10 = (f32[2,40,8,256]{3,2,1,0:T(8,128)}, f32[2,40,8,256]{3,2,1,0:T(8,128)}, f32[2,40,8,256]{3,2,1,0:T(8,128)}, f32[2,40,8,256]{3,2,1,0:T(8,128)}, f32[2,...) fusion(f32[4,42,10,256]{3,2,1,0:T(8,128)S(1)} %select_maximum_f, ...), kind=kLoop, calls=%fused_computation.102 | loop fusion | bytes 23592960 | tf_op jit(solution)/shard_map/slice | solution.py:37
  24.6 2.1 constant_dynamic-update-slice_fusion.29
  26.8 2.8 %pad_maximum_fusion.3 = (f32[2,40,8,256]{3,2,1,0:T(8,128)S(1)}, f32[2,40,8,256]{3,2,1,0:T(8,128)S(1)}, f32[2,40,8,256]{3,2,1,0:T(8,128)S(1)}, f32[2,40,8,256]{3,...) fusion(f32[4,1,8,256]{3,2,1,0:T(8,128)} %copy-done.35, f32[4,40,8,256]{3,2,1,0:T(8,128)} %copy-done.2, ...), kind=kLoop, calls=%fused_computation.26 | loop fusion | flops 983040 | bytes 5308416 | tf_op jit(solution)/shard_map/concatenate | solution.py:23
  30.5 2.0 constant_dynamic-update-slice_fusion.27
  32.4 2.0 constant_dynamic-update-slice_fusion.26
  34.4 2.0 constant_dynamic-update-slice_fusion.25
  36.4 2.0 constant_dynamic-update-slice_fusion.24
  38.4 2.0 constant_dynamic-update-slice_fusion.23
  41.2 2.0 constant_dynamic-update-slice_fusion.21
  43.2 2.2 constant_dynamic-update-slice_fusion.20
  60.7 18.9 %all-gather.2.cloned.1.call-done = f32[256,27,256]{2,0,1:T(8,128)} async-done(((f32[16,27,256]{2,0,1:T(8,128)}), f32[256,27,256]{2,0,1:T(8,128)}) %all-gather.2.cloned.1.call-update) | async-done | bytes 7077904 | tf_op jit(solution)/shard_map/all_gather | solution.py:59
  79.6 17.7 %fusion.16 = f32[640,256,1]{1,0,2:T(8,128)S(1)} fusion(f32[640,27,256]{2,0,1:T(8,128)} %constant_dynamic-update-slice_fusion.3, f32[256,27,256]{2,0,1:T(8,128)} %all-gather.2.cloned.1.call-done), kind=kOutput, calls=%fused_computation.108 | convolution fusion | flops 13589544960 | bytes 25427968 | tf_op jit(solution)/shard_map/rop,poc->rc/dot_general | solution.py:45
  97.7 22.4 %convolution_bitcast_fusion = f32[256,27,256]{0,2,1:T(8,128)} fusion(f32[640,256,1]{1,0,2:T(8,128)S(1)} %bitcast.73, f32[640,27,256]{2,0,1:T(8,128)} %constant_dynamic-update-slice_fusion.3), kind=kOutput, calls=%fused_computation.2 | convolution fusion | flops 13589544960 | bytes 25427968 | tf_op jit(solution)/shard_map/rop,rq->poq/dot_general | solution.py:74
  120.1 10.3 %copy.16 = f32[256,27,256]{2,1,0:T(8,128)} copy(f32[256,27,256]{0,2,1:T(8,128)} %convolution_bitcast_fusion) | data formatting | bytes 14155776 | tf_op jit(solution)/shard_map/rop,rq->poq/transpose | solution.py:74
  130.5 2.2 collective-permute-start.2
  134.3 33.4 %all-reduce.2 = (f32[256]{0:T(256)}, f32[256]{0:T(256)}, f32[4,256]{1,0:T(4,128)}) all-reduce(f32[256]{0:T(256)S(1)} %get-tuple-element.16, f32[256]{0:T(256)S(1)} %get-tuple-element.15, f32[4,256]{1,0:T(4,128)S(1)} %fusion.5), channel_id=1, replica_groups=mesh['groups'=2,'space'=16] {'space'}, use_global_device_ids=true, to_apply=%region_2.3 | all-reduce | flops 1536 | bytes 12288 | tf_op jit(solution)/shard_map/psum | solution.py:83
  170.2 4.4 %fusion.9 = (f32[2,40,8,256]{3,2,1,0:T(8,128)}, f32[2,40,8,256]{3,2,1,0:T(8,128)}, f32[2,40,8,256]{3,2,1,0:T(8,128)}, f32[2,40,8,256]{3,2,1,0:T(8,128)}, f32[2,4...) fusion(f32[4,42,10,256]{3,2,1,0:T(8,128)S(1)} %select_maximum_f, ...), kind=kLoop, calls=%fused_computation.101 | loop fusion | bytes 23592960 | tf_op jit(solution)/shard_map/slice | solution.py:37
  176.0 2.0 maximum_maximum_fusion
  179.8 1.8 constant_dynamic-update-slice_fusion.53
  185.2 14.4 %fusion.17 = f32[640,256,1]{1,0,2:T(8,128)S(1)} fusion(f32[640,27,256]{2,0,1:T(8,128)S(1)} %constant_dynamic-update-slice_fusion.30, f32[256,27,256]{2,0,1:T(8,128)S(1)} %bitcast.76), kind=kOutput, calls=%fused_computation.109 | convolution fusion | flops 13589544960 | bytes 25427968 | tf_op jit(solution)/shard_map/roc,qoc->rq/dot_general | solution.py:49
  200.5 33.2 %reduce-scatter.2.cloned.1.call-done = f32[16,27,256]{2,1,0:T(8,128)} async-done(((f32[256,27,256]{2,1,0:T(8,128)}), f32[16,27,256]{2,1,0:T(8,128)}) %reduce-scatter.2.cloned.1.call-update) | async-done | bytes 442384 | tf_op jit(solution)/shard_map/reduce_scatter | solution.py:73
  233.7 2.1 copy.17
  (152 shorter events, 36.0 us)
Async XLA Ops:
  7.2 72.4 %all-gather.2.cloned.1.call-start = ((), (), s32[]{:S(2)}) async-start(), calls=%async_computation.1 | async-start | bytes 7520256 | tf_op jit(solution)/shard_map/all_gather | solution.py:59
  7.9 225.8 %reduce-scatter.2.cloned.1.call-start = ((), (), s32[]{:S(2)}) async-start(), calls=%async_computation.2 | async-start | bytes 8912896 | tf_op jit(solution)/shard_map/reduce_scatter | solution.py:73
  9.1 6.7 %collective-permute-start.1 = (f32[1,40,8,256]{3,2,1,0:T(8,128)S(1)}, f32[1,40,8,256]{3,2,1,0:T(8,128)S(1)}, u32[]{:S(2)}, u32[]{:S(2)}) collective-permute-start(f32[1,40,8,256]{3,2,1,0:T(8,128)S(1)} %get-tuple-element.86), channel_id=1, source_target_pairs={{1,0},{2,1},{3,2},{4,3},{5,4},{6,5},{7,6},{8,7},{9,8},{10,9},{11,1... | collective-permute-start | bytes 983048 | tf_op jit(solution)/shard_map/ppermute | solution.py:17
  10.4 5.4 %collective-permute-start = (f32[1,40,8,256]{3,2,1,0:T(8,128)S(1)}, f32[1,40,8,256]{3,2,1,0:T(8,128)S(1)}, u32[]{:S(2)}, u32[]{:S(2)}) collective-permute-start(f32[1,40,8,256]{3,2,1,0:T(8,128)S(1)} %get-tuple-element.87), channel_id=1, source_target_pairs={{0,1},{1,2},{2,3},{3,4},{4,5},{5,6},{6,7},{7,8},{8,9},{9,10},{10,1... | collective-permute-start | bytes 983048 | tf_op jit(solution)/shard_map/ppermute | solution.py:16
  20.1 28.1 %copy-start.3 = (f32[2,40,8,256]{3,2,1,0:T(8,128)S(1)}, f32[2,40,8,256]{3,2,1,0:T(8,128)}, u32[]{:S(2)}) copy-start(f32[2,40,8,256]{3,2,1,0:T(8,128)} %param.8) | copy-start | bytes 1966084
  24.5 21.8 %copy-start.29 = (f32[2,40,8,256]{3,2,1,0:T(8,128)S(1)}, f32[2,40,8,256]{3,2,1,0:T(8,128)}, u32[]{:S(2)}) copy-start(f32[2,40,8,256]{3,2,1,0:T(8,128)} %get-tuple-element.49) | copy-start | bytes 1966084
  24.5 22.7 %copy-start.28 = (f32[2,40,8,256]{3,2,1,0:T(8,128)S(1)}, f32[2,40,8,256]{3,2,1,0:T(8,128)}, u32[]{:S(2)}) copy-start(f32[2,40,8,256]{3,2,1,0:T(8,128)} %get-tuple-element.48) | copy-start | bytes 1966084
  24.5 24.5 %copy-start.25 = (f32[2,40,8,256]{3,2,1,0:T(8,128)S(1)}, f32[2,40,8,256]{3,2,1,0:T(8,128)}, u32[]{:S(2)}) copy-start(f32[2,40,8,256]{3,2,1,0:T(8,128)} %get-tuple-element.47) | copy-start | bytes 1966084
  24.6 25.4 %copy-start.24 = (f32[2,40,8,256]{3,2,1,0:T(8,128)S(1)}, f32[2,40,8,256]{3,2,1,0:T(8,128)}, u32[]{:S(2)}) copy-start(f32[2,40,8,256]{3,2,1,0:T(8,128)} %get-tuple-element.46) | copy-start | bytes 1966084
  24.6 27.2 %copy-start.21 = (f32[2,40,8,256]{3,2,1,0:T(8,128)S(1)}, f32[2,40,8,256]{3,2,1,0:T(8,128)}, u32[]{:S(2)}) copy-start(f32[2,40,8,256]{3,2,1,0:T(8,128)} %get-tuple-element.45) | copy-start | bytes 1966084
  24.6 28.0 %copy-start.20 = (f32[2,40,8,256]{3,2,1,0:T(8,128)S(1)}, f32[2,40,8,256]{3,2,1,0:T(8,128)}, u32[]{:S(2)}) copy-start(f32[2,40,8,256]{3,2,1,0:T(8,128)} %get-tuple-element.44) | copy-start | bytes 1966084
  24.6 29.8 %copy-start.17 = (f32[2,40,8,256]{3,2,1,0:T(8,128)S(1)}, f32[2,40,8,256]{3,2,1,0:T(8,128)}, u32[]{:S(2)}) copy-start(f32[2,40,8,256]{3,2,1,0:T(8,128)} %get-tuple-element.43) | copy-start | bytes 1966084
  24.6 30.7 %copy-start.16 = (f32[2,40,8,256]{3,2,1,0:T(8,128)S(1)}, f32[2,40,8,256]{3,2,1,0:T(8,128)}, u32[]{:S(2)}) copy-start(f32[2,40,8,256]{3,2,1,0:T(8,128)} %get-tuple-element.42) | copy-start | bytes 1966084
  24.6 31.6 %copy-start.34 = (f32[2,40,8,256]{3,2,1,0:T(8,128)S(1)}, f32[2,40,8,256]{3,2,1,0:T(8,128)}, u32[]{:S(2)}) copy-start(f32[2,40,8,256]{3,2,1,0:T(8,128)} %get-tuple-element.83) | copy-start | bytes 1966084
  24.6 32.5 %copy-start.13 = (f32[2,40,8,256]{3,2,1,0:T(8,128)S(1)}, f32[2,40,8,256]{3,2,1,0:T(8,128)}, u32[]{:S(2)}) copy-start(f32[2,40,8,256]{3,2,1,0:T(8,128)} %get-tuple-element.41) | copy-start | bytes 1966084
  26.8 31.2 %copy-start.12 = (f32[2,40,8,256]{3,2,1,0:T(8,128)S(1)}, f32[2,40,8,256]{3,2,1,0:T(8,128)}, u32[]{:S(2)}) copy-start(f32[2,40,8,256]{3,2,1,0:T(8,128)} %get-tuple-element.40) | copy-start | bytes 1966084
  29.6 30.3 %copy-start.9 = (f32[2,40,8,256]{3,2,1,0:T(8,128)S(1)}, f32[2,40,8,256]{3,2,1,0:T(8,128)}, u32[]{:S(2)}) copy-start(f32[2,40,8,256]{3,2,1,0:T(8,128)} %get-tuple-element.39) | copy-start | bytes 1966084
  53.5 43.8 %copy-start.32 = (f32[2,40,8,256]{3,2,1,0:T(8,128)S(1)}, f32[2,40,8,256]{3,2,1,0:T(8,128)}, u32[]{:S(2)}) copy-start(f32[2,40,8,256]{3,2,1,0:T(8,128)} %param.9) | copy-start | bytes 1966084
  53.5 43.8 %copy-start.36 = (f32[256]{0:T(256)S(1)}, f32[256]{0:T(256)}, u32[]{:S(2)}) copy-start(f32[256]{0:T(256)} %param.11) | copy-start | bytes 3076
  120.1 13.9 %copy-start.37 = (s32[8]{0:T(128)S(1)}, s32[8]{0:T(128)}, u32[]{:S(2)}) copy-start(s32[8]{0:T(128)} %param.15) | copy-start | bytes 100
  130.5 37.1 %collective-permute-start.2 = (f32[1,40,8,256]{3,2,1,0:T(8,128)S(1)}, f32[1,40,8,256]{3,2,1,0:T(8,128)S(1)}, u32[]{:S(2)}, u32[]{:S(2)}) collective-permute-start(f32[1,40,8,256]{3,2,1,0:T(8,128)S(1)} %get-tuple-element.81), channel_id=1, source_target_pairs={{0,1},{1,2},{2,3},{3,4},{4,5},{5,6},{6,7},{7,8},{8,9},{9,10},{10,1... | collective-permute-start | bytes 983048 | tf_op jit(solution)/shard_map/ppermute | solution.py:16
  132.7 34.9 %collective-permute-start.3 = (f32[1,40,8,256]{3,2,1,0:T(8,128)S(1)}, f32[1,40,8,256]{3,2,1,0:T(8,128)S(1)}, u32[]{:S(2)}, u32[]{:S(2)}) collective-permute-start(f32[1,40,8,256]{3,2,1,0:T(8,128)S(1)} %get-tuple-element.82), channel_id=1, source_target_pairs={{1,0},{2,1},{3,2},{4,3},{5,4},{6,5},{7,6},{8,7},{9,8},{10,9},{11,1... | collective-permute-start | bytes 983048 | tf_op jit(solution)/shard_map/ppermute | solution.py:17
  183.8 15.8 %copy-start.33 = (f32[2,40,8,256]{3,2,1,0:T(8,128)S(1)}, f32[2,40,8,256]{3,2,1,0:T(8,128)}, u32[]{:S(2)}) copy-start(f32[2,40,8,256]{3,2,1,0:T(8,128)} %param.9) | copy-start | bytes 1966084
  183.9 51.9 %copy-start.1 = (f32[4,256]{1,0:T(4,128)S(1)}, f32[4,256]{1,0:T(4,128)}, u32[]{:S(2)}) copy-start(f32[4,256]{1,0:T(4,128)} %param.13) | copy-start | bytes 12292
  (22 other events, 131.9 us)
Sparse Core Ops, SparseCore 0:
  10.2 69.3 all-gather.1
  130.6 103.0 reduce-scatter.1
where the time goes:
time: 244 us; the launch traced here: 243 us
  local copies, waits for them, and re-layouts  64.6 us (26%)
  matrix products  55.5 us (23%)
  waiting for transfers between devices  52.8 us (22%)
  blocking collectives  33.4 us (14%)
  between operations  14.8 us (6%)
  other arithmetic  13.6 us (6%)
  starting transfers between devices  7.9 us (3%)
    unnamed x134, local copies, waits for them, and re-layouts  42.9 us
    psum x1, blocking collectives, per_device(): lax.psum((local_bias, local_land, local_gain), 'space')  33.4 us
    reduce_scatter x1, waiting for transfers between devices, per_device(): lax.psum_scatter(jnp.einsum('rop,rq->poq', table_pre, delta_flat, precisi...  33.2 us
    dot_general x1, matrix products, per_device(): jnp.einsum('rop,rq->poq', table_pre, delta_flat, precision=highest)  22.4 us
    all_gather x1, waiting for transfers between devices, per_device(): full_weight = lax.all_gather(weight, 'space', axis=0, tiled=True)  18.9 us
    dot_general x1, matrix products, conv_piece(): return jnp.einsum('rop,poc->rc', table, piece, precision=highest)  17.7 us
    dot_general x1, matrix products, back_piece(): return jnp.einsum('roc,qoc->rq', table, piece, precision=highest)  14.4 us
    transpose x1, local copies, waits for them, and re-layouts, per_device(): jnp.einsum('rop,rq->poq', table_pre, delta_flat, precision=highest)  10.3 us
  transfers between devices with their start and end apart: 6, of which 2 were waited for; matrix products, arithmetic and copies ran while one was open for 32% of the time, Pallas kernels for 0%

commit v1 on v0

v1 whole, which is shorter than its diff:
```python
import jax
import jax.numpy as jnp
from jax import lax
from jax.sharding import Mesh
from jax.sharding import PartitionSpec as P

highest = lax.Precision.HIGHEST
SPACE = ("chip", "core")


def with_halo(array):
    count = lax.axis_size(SPACE)
    up = [(i, i + 1) for i in range(count - 1)]
    down = [(j, i) for i, j in up]
    before = lax.ppermute(array[-1:], SPACE, up)
    after = lax.ppermute(array[:1], SPACE, down)
    return jnp.concatenate([before, array, after], axis=0)


def wrap_lon(grid):
    return jnp.concatenate([grid[:, -1:], grid, grid[:, :1]], axis=1)


def to_local_order(x, q, n_chip):
    lead = x.shape[:-1]
    blk = x.shape[-1] // (2 * n_chip)
    xt = jnp.swapaxes(x.reshape(lead + (n_chip, 2, blk)), -3, -2)
    xt = jnp.where(q == 0, xt, xt[..., ::-1, :, :])
    return xt.reshape(x.shape)


def from_local_order(x, q, n_chip):
    lead = x.shape[:-1]
    blk = x.shape[-1] // (2 * n_chip)
    xt = x.reshape(lead + (2, n_chip, blk))
    xt = jnp.where(q == 0, xt, xt[..., ::-1, :, :])
    return jnp.swapaxes(xt, -3, -2).reshape(x.shape)


def conv3(grid, kernel, rhs_spec):
    return lax.conv_general_dilated(
        grid[None],
        kernel,
        (1, 1, 1),
        [(0, 0), (0, 0), (1, 1)],
        dimension_numbers=("NDHWC", rhs_spec, "NDHWC"),
        precision=highest,
    )[0]


def all_sum(x):
    count = lax.axis_size(SPACE)
    if count & (count - 1):
        return lax.psum(x, SPACE)
    bit = 1
    while bit < count:
        pairs = [(i, i ^ bit) for i in range(count)]
        x = x + lax.ppermute(x, SPACE, pairs)
        bit *= 2
    return x


def per_device(field, grad_out, weight, bias, land_bias, level_gain, land_mask, level_index):
    rows, lon_n, lev_n, chans = field.shape
    n_chip = lax.axis_size("chip")
    q = lax.axis_index("core")
    swap = [(0, 1), (1, 0)]
    land_float = land_mask.astype(jnp.float32)
    one_hot = (
        level_index[:, None] == jnp.arange(level_gain.shape[0], dtype=jnp.int32)[None, :]
    ).astype(jnp.float32)
    gains = jnp.dot(one_hot, level_gain, precision=highest)

    mine_w = lax.all_gather(weight, "chip", axis=0, tiled=True)
    other_w = lax.ppermute(mine_w, "core", swap)
    kernel = jnp.concatenate([mine_w, other_w], axis=0).reshape(chans, 3, 3, 3, chans)

    grid = to_local_order(wrap_lon(with_halo(field)), q, n_chip)

    def forward_conv(k):
        return conv3(grid, k, "IDHWO")

    conv, weight_pullback = jax.vjp(forward_conv, kernel)
    pre = conv + bias + land_float[:, :, None, None] * land_bias
    sigma = jax.nn.sigmoid(pre)
    active = pre * sigma
    delta = grad_out * gains * sigma * (1.0 + pre * (1.0 - sigma))

    local_bias = jnp.sum(delta, axis=(0, 1, 2))
    local_land = jnp.sum(land_float[:, :, None, None] * delta, axis=(0, 1, 2))
    per_level = jnp.sum(grad_out * active, axis=(0, 1))
    local_gain = jnp.dot(one_hot.T, per_level, precision=highest)
    sums = all_sum(jnp.concatenate([local_bias[None], local_land[None], local_gain], axis=0))

    delta_grid = wrap_lon(with_halo(delta))
    back = conv3(delta_grid, lax.rev(kernel, (1, 2, 3)), "ODHWI")
    grad_field = grad_out + from_local_order(back, q, n_chip)

    (dk,) = weight_pullback(delta)
    dk = dk.reshape(chans, 27, chans)
    half = chans // 2
    chip_sum = dk[:half] + lax.ppermute(dk[half:], "core", swap)
    grad_weight = lax.psum_scatter(chip_sum, "chip", scatter_dimension=0, tiled=True)
    return (grad_field, grad_weight, sums[0], sums[1], sums[2:])


def solution(mesh):
    groups, space = mesh.devices.shape
    split = Mesh(mesh.devices.reshape(groups, space // 2, 2), ("groups",) + SPACE)
    cells = P(("groups",) + SPACE, None, None, None)
    in_specs = (
        cells,
        cells,
        P(SPACE, None, None),
        P(),
        P(),
        P(),
        P(SPACE, None),
        P(),
    )
    out_specs = (
        cells,
        P(("groups",) + SPACE, None, None),
        P("groups"),
        P("groups"),
        P("groups", None),
    )
    return jax.shard_map(
        per_device, mesh=split, in_specs=in_specs, out_specs=out_specs, check_vma=False
    )
```

time: 244 us -> 435 us (1.78)
  matrix products: 55.5 us -> 264 us
  local copies, waits for them, and re-layouts: 64.6 us -> 22.3 us
  waiting for transfers between devices: 52.8 us -> 89.4 us
  blocking collectives: 33.4 us -> 0 us
  starting transfers between devices: 7.9 us -> 25.1 us
    conv_general_dilated x0 -> x3, matrix products: none -> 263 us  [conv3(): lax.conv_general_dilated(grid[None], kernel, (1, 1, 1), [(0, 0), (0, 0),...]
    dot_general x3 -> x0, matrix products: 54.4 us -> none  [the longest x1 22.4 us: per_device(): jnp.einsum('rop,rq->poq', table_pre, delta_flat, precision=highest)]
    all_gather x1, waiting for transfers between devices: 18.9 us -> 70.2 us  [per_device(): mine_w = lax.all_gather(weight, 'chip', axis=0, tiled=True)]
    unnamed x134 -> x38, local copies, waits for them, and re-layouts: 42.9 us -> 4.48 us
    psum x1 -> x0, blocking collectives: 33.4 us -> none  [per_device(): lax.psum((local_bias, local_land, local_gain), 'space')]
    reduce_scatter x1, waiting for transfers between devices: 33.2 us -> 0.01 us  [per_device(): lax.psum_scatter(chip_sum, 'chip', scatter_dimension=0, tiled=True)]
    ppermute x4 -> x10, waiting for transfers between devices: 0.01 us -> 18.5 us  [the longest x4 11.5 us: all_sum(): x = x + lax.ppermute(x, SPACE, pairs)]
    ppermute x4 -> x10, starting transfers between devices: 7.82 us -> 25 us  [the longest x4 12.2 us: all_sum(): x = x + lax.ppermute(x, SPACE, pairs)]
  transfers between devices with their start and end apart: 6 -> 12, of which waited for: 2 -> 7; matrix products, arithmetic and copies ran while one was open for 32% -> 29% of each run, Pallas kernels for 0% -> 0%
where the time goes in v1:
time: 435 us; the launch traced here: 432 us
  matrix products  264 us (61%)
  waiting for transfers between devices  89.4 us (21%)
  starting transfers between devices  25.1 us (6%)
  local copies, waits for them, and re-layouts  22.3 us (5%)
  other arithmetic  17 us (4%)
  between operations  14.6 us (3%)
    conv_general_dilated x3, matrix products, conv3(): lax.conv_general_dilated(grid[None], kernel, (1, 1, 1), [(0, 0), (0, 0),...  263 us
    all_gather x1, waiting for transfers between devices, per_device(): mine_w = lax.all_gather(weight, 'chip', axis=0, tiled=True)  70.2 us
    ppermute x4, starting transfers between devices, all_sum(): x = x + lax.ppermute(x, SPACE, pairs)  12.2 us
    ppermute x4, waiting for transfers between devices, all_sum(): x = x + lax.ppermute(x, SPACE, pairs)  11.5 us
  transfers between devices with their start and end apart: 12, of which 7 were waited for; matrix products, arithmetic and copies ran while one was open for 29% of the time, Pallas kernels for 0%

profile of v1, /device:TPU:0, one launch (start us, length us, event | category | flops | bytes accessed | tf_op | source)
XLA Modules:
  0.0 432.2 jit_solution(5359489900424984357)
XLA Ops:
  8.0 70.2 %all-gather.2.cloned.1.call-done = f32[128,27,256]{2,0,1:T(8,128)} async-done(((f32[16,27,256]{2,0,1:T(8,128)}), f32[128,27,256]{2,0,1:T(8,128)}) %all-gather.2.cloned.1.call-update) | async-done | bytes 3538960 | tf_op jit(solution)/shard_map/all_gather | solution.py:74
  79.3 2.4 collective-permute-start
  85.4 2.7 copy.29
  88.1 4.2 reverse_select_fusion
  92.3 2.6 copy.30
  94.9 5.9 %copy.31 = f32[1,4,42,8,256]{4,0,3,2,1:T(1,128)} copy(f32[1,4,42,8,256]{2,4,3,1,0:T(8,128)} %bitcast.36) | data formatting | bytes 2752512 | tf_op jit(solution)/shard_map/jvp()/broadcast_in_dim;reshape | solution.py:42
  100.7 2.9 pad_maximum_fusion
  103.7 104.0 %fusion.20 = f32[1,2,40,8,256]{4,0,3,2,1:T(1,128)S(1)} fusion(f32[1,4,42,8,256]{4,0,3,2,1:T(1,128)S(1)} %copy-done.7, f32[256,3,3,3,256]{4,0,3,2,1:T(8,128)S(1)} %bitcast.38), kind=kOutput, calls=%fused_computation.41 | convolution fusion | flops 12457082880 | bytes 9109504 | tf_op jit(solution)/shard_map/jvp()/conv_general_dilated | solution.py:41
  208.7 64.8 %fusion.7 = f32[256,3,3,3,256]{4,0,3,2,1:T(8,128)S(1)} fusion(f32[1,4,42,8,256]{4,0,3,2,1:T(1,128)S(1)} %copy-done.7, f32[1,2,40,8,256]{4,3,2,1,0:T(8,128)S(1)} %bitcast.40), kind=kOutput, calls=%fused_computation.18 | convolution fusion | flops 12457082880 | bytes 9109504 | tf_op jit(solution)/shard_map/transpose(jvp())/conv_general_dilated | solution.py:41
  274.3 5.1 %collective-permute-start.5 = (f32[128,27,256]{2,0,1:T(8,128)S(1)}, f32[128,27,256]{2,0,1:T(8,128)S(1)}, u32[]{:S(2)}, u32[]{:S(2)}) collective-permute-start(f32[128,27,256]{2,0,1:T(8,128)S(1)} %bitcast.41), channel_id=1, source_target_pairs={{0,1},{1,0},{2,3},{3,2},{4,5},{5,4},{6,7},{7,6},{8,9},{9,8},{10,11... | collective-permute-start | bytes 10616840 | tf_op jit(solution)/shard_map/ppermute | solution.py:102
  279.4 5.8 %collective-permute-done.5 = f32[128,27,256]{2,0,1:T(8,128)S(1)} collective-permute-done((f32[128,27,256]{2,0,1:T(8,128)S(1)}, f32[128,27,256]{2,0,1:T(8,128)S(1)}, u32[]{:S(2)}, u32[]{:S(2)}) %collective-permute-start.5) | collective-permute-done | bytes 3538976 | tf_op jit(solution)/shard_map/ppermute | solution.py:102
  285.3 2.6 bitcast_add_fusion
  290.2 2.8 collective-permute-start.3
  294.3 4.6 %collective-permute-start.7 = (f32[6,256]{1,0:T(8,128)S(1)}, f32[6,256]{1,0:T(8,128)S(1)}, u32[]{:S(2)}, u32[]{:S(2)}) collective-permute-start(f32[6,256]{1,0:T(8,128)S(1)} %fusion.13), channel_id=1, source_target_pairs={{0,2},{1,3},{2,0},{3,1},{4,6},{5,7},{6,4},{7,5},{8,10},{9,11},{10,... | collective-permute-start | bytes 18440 | tf_op jit(solution)/shard_map/ppermute | solution.py:58
  298.9 7.1 %collective-permute-done.7 = f32[6,256]{1,0:T(8,128)S(1)} collective-permute-done((f32[6,256]{1,0:T(8,128)S(1)}, f32[6,256]{1,0:T(8,128)S(1)}, u32[]{:S(2)}, u32[]{:S(2)}) %collective-permute-start.7) | collective-permute-done | bytes 6176 | tf_op jit(solution)/shard_map/ppermute | solution.py:58
  306.0 5.0 %collective-permute-start.8 = (f32[6,256]{1,0:T(8,128)S(1)}, f32[6,256]{1,0:T(8,128)S(1)}, u32[]{:S(2)}, u32[]{:S(2)}) collective-permute-start(f32[6,256]{1,0:T(8,128)S(1)} %add.51), channel_id=1, source_target_pairs={{0,4},{1,5},{2,6},{3,7},{4,0},{5,1},{6,2},{7,3},{8,12},{9,13},{10,... | collective-permute-start | bytes 18440 | tf_op jit(solution)/shard_map/ppermute | solution.py:58
  311.0 2.5 collective-permute-done.8
  313.4 2.1 collective-permute-start.9
  316.2 1.9 collective-permute-done.9
  320.6 94.6 %fusion.4 = f32[1,2,40,8,256]{4,0,3,2,1:T(1,128)S(1)} fusion(f32[256,3,3,3,256]{4,0,3,2,1:T(8,128)} %bitcast.39, f32[1,4,42,8,256]{4,3,2,1,0:T(8,128)S(1)} %fusion.2), kind=kOutput, calls=%fused_computation.14 | convolution fusion | flops 12457082880 | bytes 9109504 | tf_op jit(solution)/shard_map/conv_general_dilated | solution.py:41
  415.2 2.5 copy.33
  417.7 2.5 fusion
  420.5 1.7 bitcast_add_fusion.1
  422.1 3.0 copy.38
  (72 shorter events, 14.3 us)
Async XLA Ops:
  7.2 76.6 %copy-start = (f32[4,256]{1,0:T(4,128)S(1)}, f32[4,256]{1,0:T(4,128)}, u32[]{:S(2)}) copy-start(f32[4,256]{1,0:T(4,128)} %param.13) | copy-start | bytes 12292
  7.2 77.3 %copy-start.4 = (f32[2,40,8,256]{3,2,1,0:T(8,128)S(1)}, f32[2,40,8,256]{3,2,1,0:T(8,128)}, u32[]{:S(2)}) copy-start(f32[2,40,8,256]{3,2,1,0:T(8,128)} %param.8) | copy-start | bytes 1966084
  7.2 75.8 %copy-start.14 = (s32[2,40]{1,0:T(2,128)S(1)}, s32[2,40]{1,0:T(2,128)}, u32[]{:S(2)}) copy-start(s32[2,40]{1,0:T(2,128)} %param.14) | copy-start | bytes 964
  7.2 75.8 %copy-start.12 = (f32[256]{0:T(256)S(1)}, f32[256]{0:T(256)}, u32[]{:S(2)}) copy-start(f32[256]{0:T(256)} %param.12) | copy-start | bytes 3076
  7.2 76.6 %copy-start.15 = (s32[8]{0:T(128)S(1)}, s32[8]{0:T(128)}, u32[]{:S(2)}) copy-start(s32[8]{0:T(128)} %param.15) | copy-start | bytes 100
  7.2 70.9 %all-gather.2.cloned.1.call-start = ((), (), s32[]{:S(2)}) async-start(), calls=%async_computation.1 | async-start | bytes 3981312 | tf_op jit(solution)/shard_map/all_gather | solution.py:74
  8.0 417.2 %reduce-scatter.2.cloned.1.call-start = ((), (), s32[]{:S(2)}) async-start(), calls=%async_computation.2 | async-start | bytes 3981312 | tf_op jit(solution)/shard_map/reduce_scatter | solution.py:103
  78.2 22.6 %collective-permute-start.2 = (f32[128,27,256]{2,0,1:T(8,128)}, f32[128,27,256]{2,0,1:T(8,128)}, u32[]{:S(2)}, u32[]{:S(2)}) collective-permute-start(f32[128,27,256]{2,0,1:T(8,128)} %all-gather.2.cloned.1.call-done), channel_id=1, source_target_pairs={{0,1},{1,0},{2,3},{3,2},{4,5},{5,4},{6,7},{7,6},{8,9},{9,8},{10,11... | collective-permute-start | bytes 10616840 | tf_op jit(solution)/shard_map/ppermute | solution.py:75
  79.3 5.2 %collective-permute-start = (f32[1,40,8,256]{3,2,1,0:T(8,128)S(1)}, f32[1,40,8,256]{3,2,1,0:T(8,128)S(1)}, u32[]{:S(2)}, u32[]{:S(2)}) collective-permute-start(f32[1,40,8,256]{3,2,1,0:T(8,128)S(1)} %get-tuple-element.26), channel_id=1, source_target_pairs={{0,1},{1,2},{2,3},{3,4},{4,5},{5,6},{6,7},{7,8},{8,9},{9,10},{10,1... | collective-permute-start | bytes 983048 | tf_op jit(solution)/shard_map/ppermute | solution.py:15
  81.7 3.5 collective-permute-start.1
  94.9 5.9 %copy-start.3 = (f32[128,27,256]{2,0,1:T(8,128)S(1)}, f32[128,27,256]{2,0,1:T(8,128)}, u32[]{:S(2)}) copy-start(f32[128,27,256]{2,0,1:T(8,128)} %all-gather.2.cloned.1.call-done) | copy-start | bytes 10616836
  103.6 104.1 %copy-start.2 = (f32[256,27,256]{2,0,1:T(8,128)}, f32[256,27,256]{2,0,1:T(8,128)S(1)}, u32[]{:S(2)}) copy-start(f32[256,27,256]{2,0,1:T(8,128)S(1)} %pad_maximum_fusion) | copy-start | bytes 21233668
  103.6 104.1 %copy-start.5 = (f32[2,40,8,256]{3,2,1,0:T(8,128)S(1)}, f32[2,40,8,256]{3,2,1,0:T(8,128)}, u32[]{:S(2)}) copy-start(f32[2,40,8,256]{3,2,1,0:T(8,128)} %param.9) | copy-start | bytes 1966084
  103.6 104.1 %copy-start.8 = (f32[2,40,256]{2,1,0:T(8,128)S(1)}, f32[2,40,256]{2,1,0:T(8,128)}, u32[]{:S(2)}) copy-start(f32[2,40,256]{2,1,0:T(8,128)} %broadcast_multiply_fusion) | copy-start | bytes 245764
  103.7 104.1 %copy-start.13 = (f32[256]{0:T(256)S(1)}, f32[256]{0:T(256)}, u32[]{:S(2)}) copy-start(f32[256]{0:T(256)} %param.11) | copy-start | bytes 3076
  274.3 10.9 %collective-permute-start.5 = (f32[128,27,256]{2,0,1:T(8,128)S(1)}, f32[128,27,256]{2,0,1:T(8,128)S(1)}, u32[]{:S(2)}, u32[]{:S(2)}) collective-permute-start(f32[128,27,256]{2,0,1:T(8,128)S(1)} %bitcast.41), channel_id=1, source_target_pairs={{0,1},{1,0},{2,3},{3,2},{4,5},{5,4},{6,7},{7,6},{8,9},{9,8},{10,11... | collective-permute-start | bytes 10616840 | tf_op jit(solution)/shard_map/ppermute | solution.py:102
  287.9 27.6 %copy-start.6 = (f32[2,40,8,256]{3,2,1,0:T(8,128)S(1)}, f32[2,40,8,256]{3,2,1,0:T(8,128)}, u32[]{:S(2)}) copy-start(f32[2,40,8,256]{3,2,1,0:T(8,128)} %param.9) | copy-start | bytes 1966084
  288.9 5.4 %collective-permute-start.6 = (f32[6,256]{1,0:T(8,128)S(1)}, f32[6,256]{1,0:T(8,128)S(1)}, u32[]{:S(2)}, u32[]{:S(2)}) collective-permute-start(f32[6,256]{1,0:T(8,128)S(1)} %pad_maximum_fusion.6), channel_id=1, source_target_pairs={{0,1},{1,0},{2,3},{3,2},{4,5},{5,4},{6,7},{7,6},{8,9},{9,8},{10,11... | collective-permute-start | bytes 18440 | tf_op jit(solution)/shard_map/ppermute | solution.py:58
  290.2 29.1 %collective-permute-start.3 = (f32[1,40,8,256]{3,2,1,0:T(8,128)}, f32[1,40,8,256]{3,2,1,0:T(8,128)}, u32[]{:S(2)}, u32[]{:S(2)}) collective-permute-start(f32[1,40,8,256]{3,2,1,0:T(8,128)} %get-tuple-element.23), channel_id=1, source_target_pairs={{0,1},{1,2},{2,3},{3,4},{4,5},{5,6},{6,7},{7,8},{8,9},{9,10},{10,1... | collective-permute-start | bytes 983048 | tf_op jit(solution)/shard_map/ppermute | solution.py:15
  292.9 26.4 %collective-permute-start.4 = (f32[1,40,8,256]{3,2,1,0:T(8,128)}, f32[1,40,8,256]{3,2,1,0:T(8,128)}, u32[]{:S(2)}, u32[]{:S(2)}) collective-permute-start(f32[1,40,8,256]{3,2,1,0:T(8,128)} %get-tuple-element.24), channel_id=1, source_target_pairs={{1,0},{2,1},{3,2},{4,3},{5,4},{6,5},{7,6},{8,7},{9,8},{10,9},{11,1... | collective-permute-start | bytes 983048 | tf_op jit(solution)/shard_map/ppermute | solution.py:16
  294.3 11.7 %collective-permute-start.7 = (f32[6,256]{1,0:T(8,128)S(1)}, f32[6,256]{1,0:T(8,128)S(1)}, u32[]{:S(2)}, u32[]{:S(2)}) collective-permute-start(f32[6,256]{1,0:T(8,128)S(1)} %fusion.13), channel_id=1, source_target_pairs={{0,2},{1,3},{2,0},{3,1},{4,6},{5,7},{6,4},{7,5},{8,10},{9,11},{10,... | collective-permute-start | bytes 18440 | tf_op jit(solution)/shard_map/ppermute | solution.py:58
  306.0 7.5 %collective-permute-start.8 = (f32[6,256]{1,0:T(8,128)S(1)}, f32[6,256]{1,0:T(8,128)S(1)}, u32[]{:S(2)}, u32[]{:S(2)}) collective-permute-start(f32[6,256]{1,0:T(8,128)S(1)} %add.51), channel_id=1, source_target_pairs={{0,4},{1,5},{2,6},{3,7},{4,0},{5,1},{6,2},{7,3},{8,12},{9,13},{10,... | collective-permute-start | bytes 18440 | tf_op jit(solution)/shard_map/ppermute | solution.py:58
  313.4 4.7 %collective-permute-start.9 = (f32[6,256]{1,0:T(8,128)S(1)}, f32[6,256]{1,0:T(8,128)S(1)}, u32[]{:S(2)}, u32[]{:S(2)}) collective-permute-start(f32[6,256]{1,0:T(8,128)S(1)} %add.52), channel_id=1, source_target_pairs={{0,8},{1,9},{2,10},{3,11},{4,12},{5,13},{6,14},{7,15},{8,0},{9,1},... | collective-permute-start | bytes 18440 | tf_op jit(solution)/shard_map/ppermute | solution.py:58
  420.5 4.7 %copy-start.1 = (f32[4,256]{1,0:T(4,128)S(1)}, f32[4,256]{1,0:T(4,128)}, u32[]{:S(2)}) copy-start(f32[4,256]{1,0:T(4,128)} %param.13) | copy-start | bytes 12292
  (5 other events, 6.2 us)
Sparse Core Ops, SparseCore 0:
  10.2 67.8 all-gather.1
  288.0 83.2 reduce-scatter.1

commit v2 on v0

--- a/solution.py
+++ b/solution.py
@@ -4,6 +4,7 @@
 from jax.sharding import PartitionSpec as P
 
 highest = lax.Precision.HIGHEST
+high = lax.Precision.HIGH
 
 
 def with_halo(array, sides, width):
@@ -42,11 +43,11 @@
 
 
 def conv_piece(table, piece):
-    return jnp.einsum("rop,poc->rc", table, piece, precision=highest)
+    return jnp.einsum("rop,poc->rc", table, piece, precision=high)
 
 
 def back_piece(table, piece):
-    return jnp.einsum("roc,qoc->rq", table, piece, precision=highest)
+    return jnp.einsum("roc,qoc->rq", table, piece, precision=high)
 
 
 def per_device(field, grad_out, weight, bias, land_bias, level_gain, land_mask, level_index):
@@ -69,19 +70,19 @@
     delta_table = window_table(wrap_levels(delta_pad), rows, True)
     back = back_piece(delta_table, full_weight)
     grad_field = grad_out + back.reshape(rows, lon_n, lev_n, chans)
-    delta_flat = delta.reshape(-1, chans)
+    local_bias = jnp.sum(delta, axis=(0, 1, 2))
+    local_land = jnp.sum(land_float[:, :, None, None] * delta, axis=(0, 1, 2))
+    per_level = jnp.sum(grad_out * active, axis=(0, 1))
+    local_gain = jnp.dot(one_hot.T, per_level, precision=highest)
+    sums = lax.psum(jnp.concatenate([local_bias[None], local_land[None], local_gain], axis=0), "space")
+    sums, delta_flat = lax.optimization_barrier((sums, delta.reshape(-1, chans)))
     grad_weight = lax.psum_scatter(
-        jnp.einsum("rop,rq->poq", table_pre, delta_flat, precision=highest),
+        jnp.einsum("rop,rq->poq", table_pre, delta_flat, precision=high),
         "space",
         scatter_dimension=0,
         tiled=True,
     )
-    local_bias = jnp.sum(delta, axis=(0, 1, 2))
-    local_land = jnp.sum(land_float[:, :, None, None] * delta, axis=(0, 1, 2))
-    per_level = jnp.sum(grad_out * active, axis=(0, 1))
-    local_gain = jnp.dot(one_hot.T, per_level, precision=highest)
-    grad_bias, grad_land, grad_gain = lax.psum((local_bias, local_land, local_gain), "space")
-    return (grad_field, grad_weight, grad_bias, grad_land, grad_gain)
+    return (grad_field, grad_weight, sums[0], sums[1], sums[2:])
 
 
 def solution(mesh):

time: 244 us -> 263 us (1.078)
  local copies, waits for them, and re-layouts: 64.6 us -> 87.6 us
  waiting for transfers between devices: 52.8 us -> 68.2 us
  matrix products: 55.5 us -> 40.8 us
    unnamed x134, local copies, waits for them, and re-layouts: 42.9 us -> 63.1 us
    dot_general x3, matrix products: 54.4 us -> 39.7 us  [the longest x1 15.3 us: per_device(): jnp.einsum('rop,rq->poq', table_pre, delta_flat, precision=high)]
    reduce_scatter x1, waiting for transfers between devices: 33.2 us -> 47.3 us  [per_device(): lax.psum_scatter(jnp.einsum('rop,rq->poq', table_pre, delta_flat, precisi...]
  transfers between devices with their start and end apart: 6 -> 6, of which waited for: 2 -> 3; matrix products, arithmetic and copies ran while one was open for 32% -> 37% of each run, Pallas kernels for 0% -> 0%
where the time goes in v2:
time: 263 us; the launch traced here: 262 us
  local copies, waits for them, and re-layouts  87.6 us (33%)
  waiting for transfers between devices  68.2 us (26%)
  matrix products  40.8 us (16%)
  blocking collectives  31.9 us (12%)
  between operations  14.5 us (6%)
  other arithmetic  12.2 us (5%)
  starting transfers between devices  7.24 us (3%)
    unnamed x134, local copies, waits for them, and re-layouts  63.1 us
    reduce_scatter x1, waiting for transfers between devices, per_device(): lax.psum_scatter(jnp.einsum('rop,rq->poq', table_pre, delta_flat, precisi...  47.3 us
    psum x1, blocking collectives, per_device(): lax.psum(jnp.concatenate([local_bias[None], local_land[None], local_gain]...  31.9 us
    all_gather x1, waiting for transfers between devices, per_device(): full_weight = lax.all_gather(weight, 'space', axis=0, tiled=True)  19.4 us
    dot_general x1, matrix products, per_device(): jnp.einsum('rop,rq->poq', table_pre, delta_flat, precision=high)  15.3 us
    dot_general x1, matrix products, conv_piece(): return jnp.einsum('rop,poc->rc', table, piece, precision=high)  13.7 us
    dot_general x1, matrix products, back_piece(): return jnp.einsum('roc,qoc->rq', table, piece, precision=high)  10.7 us
    transpose x1, local copies, waits for them, and re-layouts, per_device(): jnp.einsum('rop,rq->poq', table_pre, delta_flat, precision=high)  10.3 us
  transfers between devices with their start and end apart: 6, of which 3 were waited for; matrix products, arithmetic and copies ran while one was open for 37% of the time, Pallas kernels for 0%

profile of v2, /device:TPU:0, one launch (start us, length us, event | category | flops | bytes accessed | tf_op | source)
XLA Modules:
  0.0 262.4 jit_solution(12044902150029803068)
XLA Ops:
  10.4 3.1 %collective-permute-start = (f32[1,40,8,256]{3,2,1,0:T(8,128)S(1)}, f32[1,40,8,256]{3,2,1,0:T(8,128)S(1)}, u32[]{:S(2)}, u32[]{:S(2)}) collective-permute-start(f32[1,40,8,256]{3,2,1,0:T(8,128)S(1)} %get-tuple-element.88), channel_id=1, source_target_pairs={{0,1},{1,2},{2,3},{3,4},{4,5},{5,6},{6,7},{7,8},{8,9},{9,10},{10,1... | collective-permute-start | bytes 983048 | tf_op jit(solution)/shard_map/ppermute | solution.py:17
  15.8 2.5 pad_maximum_fusion.4
  19.9 4.5 %fusion.12 = (f32[2,40,8,256]{3,2,1,0:T(8,128)}, f32[2,40,8,256]{3,2,1,0:T(8,128)}, f32[2,40,8,256]{3,2,1,0:T(8,128)}, f32[2,40,8,256]{3,2,1,0:T(8,128)}, f32[2,...) fusion(f32[4,42,10,256]{3,2,1,0:T(8,128)S(1)} %select_maximum_f, ...), kind=kLoop, calls=%fused_computation.105 | loop fusion | bytes 23592960 | tf_op jit(solution)/shard_map/slice | solution.py:38
  24.4 2.1 constant_dynamic-update-slice_fusion.29
  26.6 2.6 %pad_maximum_fusion.3 = (f32[2,40,8,256]{3,2,1,0:T(8,128)S(1)}, f32[2,40,8,256]{3,2,1,0:T(8,128)S(1)}, f32[2,40,8,256]{3,2,1,0:T(8,128)S(1)}, f32[2,40,8,256]{3,...) fusion(f32[4,1,8,256]{3,2,1,0:T(8,128)} %copy-done.35, f32[4,40,8,256]{3,2,1,0:T(8,128)} %copy-done.2, ...), kind=kLoop, calls=%fused_computation.26 | loop fusion | flops 983040 | bytes 5308416 | tf_op jit(solution)/shard_map/concatenate | solution.py:24
  30.1 2.0 constant_dynamic-update-slice_fusion.27
  32.1 2.0 constant_dynamic-update-slice_fusion.26
  34.1 2.0 constant_dynamic-update-slice_fusion.25
  38.0 2.0 constant_dynamic-update-slice_fusion.23
  40.9 2.0 constant_dynamic-update-slice_fusion.21
  42.9 2.0 constant_dynamic-update-slice_fusion.20
  60.2 19.4 %all-gather.2.cloned.1.call-done = f32[256,27,256]{2,0,1:T(8,128)} async-done(((f32[16,27,256]{2,0,1:T(8,128)}), f32[256,27,256]{2,0,1:T(8,128)}) %all-gather.2.cloned.1.call-update) | async-done | bytes 7077904 | tf_op jit(solution)/shard_map/all_gather | solution.py:60
  79.6 13.7 %fusion.19 = f32[640,256,1]{1,0,2:T(8,128)S(1)} fusion(f32[640,27,256]{2,0,1:T(8,128)} %constant_dynamic-update-slice_fusion.3, f32[256,27,256]{2,0,1:T(8,128)} %all-gather.2.cloned.1.call-done), kind=kOutput, calls=%fused_computation.112 | convolution fusion | flops 6794772480 | bytes 25427968 | tf_op jit(solution)/shard_map/rop,poc->rc/dot_general | solution.py:46
  94.0 31.9 %psum.7 = f32[6,256]{1,0:T(8,128)S(1)} all-reduce(f32[6,256]{1,0:T(8,128)S(1)} %pad_maximum_fusion.10), channel_id=1, replica_groups=mesh['groups'=2,'space'=16] {'space'}, use_global_device_ids=true, to_apply=%region_3.4 | all-reduce | flops 1536 | bytes 12288 | tf_op jit(solution)/shard_map/psum | solution.py:77
  125.9 15.3 %convolution_bitcast_fusion = f32[256,27,256]{0,2,1:T(8,128)} fusion(f32[640,27,256]{2,0,1:T(8,128)} %constant_dynamic-update-slice_fusion.3, f32[640,256]{1,0:T(8,128)S(1)} %bitcast.77), kind=kOutput, calls=%fused_computation.2 | convolution fusion | flops 6794772480 | bytes 25427968 | tf_op jit(solution)/shard_map/rop,rq->poq/dot_general | solution.py:80
  141.2 10.3 %copy.16 = f32[256,27,256]{2,1,0:T(8,128)} copy(f32[256,27,256]{0,2,1:T(8,128)} %convolution_bitcast_fusion) | data formatting | bytes 14155776 | tf_op jit(solution)/shard_map/rop,rq->poq/transpose | solution.py:80
  157.8 5.0 %fusion.11 = (f32[2,40,8,256]{3,2,1,0:T(8,128)}, f32[2,40,8,256]{3,2,1,0:T(8,128)}, f32[2,40,8,256]{3,2,1,0:T(8,128)}, f32[2,40,8,256]{3,2,1,0:T(8,128)}, f32[2,...) fusion(f32[4,42,10,256]{3,2,1,0:T(8,128)S(1)} %select_maximum_f, ...), kind=kLoop, calls=%fused_computation.104 | loop fusion | bytes 23592960 | tf_op jit(solution)/shard_map/slice | solution.py:38
  162.9 2.2 constant_dynamic-update-slice_fusion.56
  165.1 2.0 maximum_maximum_fusion
  168.5 2.2 constant_dynamic-update-slice_fusion.54
  170.7 2.0 constant_dynamic-update-slice_fusion.53
  194.6 10.7 %fusion.20 = f32[640,256,1]{1,0,2:T(8,128)S(1)} fusion(f32[640,27,256]{2,0,1:T(8,128)} %constant_dynamic-update-slice_fusion.30, f32[256,27,256]{2,0,1:T(8,128)S(1)} %bitcast.80), kind=kOutput, calls=%fused_computation.113 | convolution fusion | flops 6794772480 | bytes 25427968 | tf_op jit(solution)/shard_map/roc,qoc->rq/dot_general | solution.py:50
  206.2 47.3 %reduce-scatter.2.cloned.1.call-done = f32[16,27,256]{2,1,0:T(8,128)} async-done(((f32[256,27,256]{2,1,0:T(8,128)}), f32[16,27,256]{2,1,0:T(8,128)}) %reduce-scatter.2.cloned.1.call-update) | async-done | bytes 442384 | tf_op jit(solution)/shard_map/reduce_scatter | solution.py:79
  253.5 2.1 copy.17
  (155 shorter events, 57.1 us)
Async XLA Ops:
  7.2 72.4 %all-gather.2.cloned.1.call-start = ((), (), s32[]{:S(2)}) async-start(), calls=%async_computation.1 | async-start | bytes 7520256 | tf_op jit(solution)/shard_map/all_gather | solution.py:60
  7.9 245.6 %reduce-scatter.2.cloned.1.call-start = ((), (), s32[]{:S(2)}) async-start(), calls=%async_computation.2 | async-start | bytes 8912896 | tf_op jit(solution)/shard_map/reduce_scatter | solution.py:79
  9.1 6.7 %collective-permute-start.1 = (f32[1,40,8,256]{3,2,1,0:T(8,128)S(1)}, f32[1,40,8,256]{3,2,1,0:T(8,128)S(1)}, u32[]{:S(2)}, u32[]{:S(2)}) collective-permute-start(f32[1,40,8,256]{3,2,1,0:T(8,128)S(1)} %get-tuple-element.87), channel_id=1, source_target_pairs={{1,0},{2,1},{3,2},{4,3},{5,4},{6,5},{7,6},{8,7},{9,8},{10,9},{11,1... | collective-permute-start | bytes 983048 | tf_op jit(solution)/shard_map/ppermute | solution.py:18
  10.4 5.4 %collective-permute-start = (f32[1,40,8,256]{3,2,1,0:T(8,128)S(1)}, f32[1,40,8,256]{3,2,1,0:T(8,128)S(1)}, u32[]{:S(2)}, u32[]{:S(2)}) collective-permute-start(f32[1,40,8,256]{3,2,1,0:T(8,128)S(1)} %get-tuple-element.88), channel_id=1, source_target_pairs={{0,1},{1,2},{2,3},{3,4},{4,5},{5,6},{6,7},{7,8},{8,9},{9,10},{10,1... | collective-permute-start | bytes 983048 | tf_op jit(solution)/shard_map/ppermute | solution.py:17
  19.8 27.8 %copy-start.3 = (f32[2,40,8,256]{3,2,1,0:T(8,128)S(1)}, f32[2,40,8,256]{3,2,1,0:T(8,128)}, u32[]{:S(2)}) copy-start(f32[2,40,8,256]{3,2,1,0:T(8,128)} %param.8) | copy-start | bytes 1966084
  24.4 24.2 %copy-start.25 = (f32[2,40,8,256]{3,2,1,0:T(8,128)S(1)}, f32[2,40,8,256]{3,2,1,0:T(8,128)}, u32[]{:S(2)}) copy-start(f32[2,40,8,256]{3,2,1,0:T(8,128)} %get-tuple-element.48) | copy-start | bytes 1966084
  24.4 25.1 %copy-start.24 = (f32[2,40,8,256]{3,2,1,0:T(8,128)S(1)}, f32[2,40,8,256]{3,2,1,0:T(8,128)}, u32[]{:S(2)}) copy-start(f32[2,40,8,256]{3,2,1,0:T(8,128)} %get-tuple-element.47) | copy-start | bytes 1966084
  24.4 26.8 %copy-start.21 = (f32[2,40,8,256]{3,2,1,0:T(8,128)S(1)}, f32[2,40,8,256]{3,2,1,0:T(8,128)}, u32[]{:S(2)}) copy-start(f32[2,40,8,256]{3,2,1,0:T(8,128)} %get-tuple-element.46) | copy-start | bytes 1966084
  24.4 27.7 %copy-start.20 = (f32[2,40,8,256]{3,2,1,0:T(8,128)S(1)}, f32[2,40,8,256]{3,2,1,0:T(8,128)}, u32[]{:S(2)}) copy-start(f32[2,40,8,256]{3,2,1,0:T(8,128)} %get-tuple-element.45) | copy-start | bytes 1966084
  24.4 29.5 %copy-start.17 = (f32[2,40,8,256]{3,2,1,0:T(8,128)S(1)}, f32[2,40,8,256]{3,2,1,0:T(8,128)}, u32[]{:S(2)}) copy-start(f32[2,40,8,256]{3,2,1,0:T(8,128)} %get-tuple-element.44) | copy-start | bytes 1966084
  24.4 30.4 %copy-start.16 = (f32[2,40,8,256]{3,2,1,0:T(8,128)S(1)}, f32[2,40,8,256]{3,2,1,0:T(8,128)}, u32[]{:S(2)}) copy-start(f32[2,40,8,256]{3,2,1,0:T(8,128)} %get-tuple-element.43) | copy-start | bytes 1966084
  24.4 31.3 %copy-start.34 = (f32[2,40,8,256]{3,2,1,0:T(8,128)S(1)}, f32[2,40,8,256]{3,2,1,0:T(8,128)}, u32[]{:S(2)}) copy-start(f32[2,40,8,256]{3,2,1,0:T(8,128)} %get-tuple-element.84) | copy-start | bytes 1966084
  24.4 32.1 %copy-start.13 = (f32[2,40,8,256]{3,2,1,0:T(8,128)S(1)}, f32[2,40,8,256]{3,2,1,0:T(8,128)}, u32[]{:S(2)}) copy-start(f32[2,40,8,256]{3,2,1,0:T(8,128)} %get-tuple-element.42) | copy-start | bytes 1966084
  26.6 30.9 %copy-start.12 = (f32[2,40,8,256]{3,2,1,0:T(8,128)S(1)}, f32[2,40,8,256]{3,2,1,0:T(8,128)}, u32[]{:S(2)}) copy-start(f32[2,40,8,256]{3,2,1,0:T(8,128)} %get-tuple-element.41) | copy-start | bytes 1966084
  29.2 30.1 %copy-start.9 = (f32[2,40,8,256]{3,2,1,0:T(8,128)S(1)}, f32[2,40,8,256]{3,2,1,0:T(8,128)}, u32[]{:S(2)}) copy-start(f32[2,40,8,256]{3,2,1,0:T(8,128)} %get-tuple-element.40) | copy-start | bytes 1966084
  55.7 37.6 %copy-start.32 = (f32[2,40,8,256]{3,2,1,0:T(8,128)S(1)}, f32[2,40,8,256]{3,2,1,0:T(8,128)}, u32[]{:S(2)}) copy-start(f32[2,40,8,256]{3,2,1,0:T(8,128)} %param.9) | copy-start | bytes 1966084
  55.7 37.7 %copy-start.36 = (f32[256]{0:T(256)S(1)}, f32[256]{0:T(256)}, u32[]{:S(2)}) copy-start(f32[256]{0:T(256)} %param.11) | copy-start | bytes 3076
  57.5 36.3 %copy-start.37 = (s32[8]{0:T(128)S(1)}, s32[8]{0:T(128)}, u32[]{:S(2)}) copy-start(s32[8]{0:T(128)} %param.15) | copy-start | bytes 100
  151.7 4.0 %collective-permute-start.2 = (f32[1,40,8,256]{3,2,1,0:T(8,128)S(1)}, f32[1,40,8,256]{3,2,1,0:T(8,128)S(1)}, u32[]{:S(2)}, u32[]{:S(2)}) collective-permute-start(f32[1,40,8,256]{3,2,1,0:T(8,128)S(1)} %get-tuple-element.82), channel_id=1, source_target_pairs={{0,1},{1,2},{2,3},{3,4},{4,5},{5,6},{6,7},{7,8},{8,9},{9,10},{10,1... | collective-permute-start | bytes 983048 | tf_op jit(solution)/shard_map/ppermute | solution.py:17
  153.0 3.5 %collective-permute-start.3 = (f32[1,40,8,256]{3,2,1,0:T(8,128)S(1)}, f32[1,40,8,256]{3,2,1,0:T(8,128)S(1)}, u32[]{:S(2)}, u32[]{:S(2)}) collective-permute-start(f32[1,40,8,256]{3,2,1,0:T(8,128)S(1)} %get-tuple-element.83), channel_id=1, source_target_pairs={{1,0},{2,1},{3,2},{4,3},{5,4},{6,5},{7,6},{8,7},{9,8},{10,9},{11,1... | collective-permute-start | bytes 983048 | tf_op jit(solution)/shard_map/ppermute | solution.py:18
  167.5 24.4 %copy-start.7 = (f32[2,40,8,256]{3,2,1,0:T(8,128)S(1)}, f32[2,40,8,256]{3,2,1,0:T(8,128)}, u32[]{:S(2)}) copy-start(f32[2,40,8,256]{3,2,1,0:T(8,128)} %get-tuple-element.23) | copy-start | bytes 1966084
  167.6 26.2 %copy-start.6 = (f32[2,40,8,256]{3,2,1,0:T(8,128)S(1)}, f32[2,40,8,256]{3,2,1,0:T(8,128)}, u32[]{:S(2)}) copy-start(f32[2,40,8,256]{3,2,1,0:T(8,128)} %get-tuple-element.22) | copy-start | bytes 1966084
  168.5 26.2 %slice-start = ((s8[7077888]{0:T(1024)(128)(4,1)}), s8[4194304]{0:T(1024)(128)(4,1)S(1)}, s32[]{:S(2)}) async-start(s8[7077888]{0:T(1024)(128)(4,1)} %bitcast.79), calls=%async_computation.3 | async-start | bytes 8388608
  191.9 63.7 %copy-start.1 = (f32[4,256]{1,0:T(4,128)S(1)}, f32[4,256]{1,0:T(4,128)}, u32[]{:S(2)}) copy-start(f32[4,256]{1,0:T(4,128)} %param.13) | copy-start | bytes 12292
  (22 other events, 323.1 us)
Sparse Core Ops, SparseCore 0:
  10.2 69.3 all-gather.1
  151.7 101.7 reduce-scatter.1

commit v3 on v2

--- a/solution.py
+++ b/solution.py
@@ -74,15 +74,17 @@
     local_land = jnp.sum(land_float[:, :, None, None] * delta, axis=(0, 1, 2))
     per_level = jnp.sum(grad_out * active, axis=(0, 1))
     local_gain = jnp.dot(one_hot.T, per_level, precision=highest)
-    sums = lax.psum(jnp.concatenate([local_bias[None], local_land[None], local_gain], axis=0), "space")
-    sums, delta_flat = lax.optimization_barrier((sums, delta.reshape(-1, chans)))
+    partial = jnp.concatenate([local_bias[None], local_land[None], local_gain], axis=0)
+    partial = jnp.pad(partial, ((0, 64 - partial.shape[0]), (0, 0)))
+    sums = jnp.sum(lax.all_gather(partial, "space", axis=0, tiled=False), axis=0)
+    delta_flat = delta.reshape(-1, chans)
     grad_weight = lax.psum_scatter(
-        jnp.einsum("rop,rq->poq", table_pre, delta_flat, precision=high),
+        jnp.einsum("rq,rop->poq", delta_flat, table_pre, precision=high),
         "space",
         scatter_dimension=0,
         tiled=True,
     )
-    return (grad_field, grad_weight, sums[0], sums[1], sums[2:])
+    return (grad_field, grad_weight, sums[0], sums[1], sums[2 : 2 + local_gain.shape[0]])
 
 
 def solution(mesh):

time: 263 us -> 236 us (0.90)
  blocking collectives: 31.9 us -> 0 us
  local copies, waits for them, and re-layouts: 87.6 us -> 74.3 us
  waiting for transfers between devices: 68.2 us -> 78.7 us
  matrix products: 40.8 us -> 45.4 us
    psum x1 -> x0, blocking collectives: 31.9 us -> none  [per_device(): lax.psum(jnp.concatenate([local_bias[None], local_land[None], local_gain]...]
    transpose x1 -> x0, local copies, waits for them, and re-layouts: 10.3 us -> none  [per_device(): jnp.einsum('rop,rq->poq', table_pre, delta_flat, precision=high)]
    reduce_scatter x1, waiting for transfers between devices: 47.3 us -> 56.6 us  [per_device(): lax.psum_scatter(jnp.einsum('rq,rop->poq', delta_flat, table_pre, precisi...]
    dot_general x1, matrix products: 15.3 us -> 19.6 us  [per_device(): jnp.einsum('rq,rop->poq', delta_flat, table_pre, precision=high)]
    unnamed x134 -> x133, local copies, waits for them, and re-layouts: 63.1 us -> 60.9 us
  transfers between devices with their start and end apart: 6 -> 7, of which waited for: 3 -> 3; matrix products, arithmetic and copies ran while one was open for 37% -> 50% of each run, Pallas kernels for 0% -> 0%
where the time goes in v3:
time: 236 us; the launch traced here: 235 us
  waiting for transfers between devices  78.7 us (33%)
  local copies, waits for them, and re-layouts  74.3 us (31%)
  matrix products  45.4 us (19%)
  between operations  14.2 us (6%)
  other arithmetic  14 us (6%)
  starting transfers between devices  8.34 us (4%)
    unnamed x133, local copies, waits for them, and re-layouts  60.9 us
    reduce_scatter x1, waiting for transfers between devices, per_device(): lax.psum_scatter(jnp.einsum('rq,rop->poq', delta_flat, table_pre, precisi...  56.6 us
    dot_general x1, matrix products, per_device(): jnp.einsum('rq,rop->poq', delta_flat, table_pre, precision=high)  19.6 us
    all_gather x1, waiting for transfers between devices, per_device(): full_weight = lax.all_gather(weight, 'space', axis=0, tiled=True)  19.4 us
    dot_general x1, matrix products, conv_piece(): return jnp.einsum('rop,poc->rc', table, piece, precision=high)  13.7 us
    dot_general x1, matrix products, back_piece(): return jnp.einsum('roc,qoc->rq', table, piece, precision=high)  11 us
    slice x3, local copies, waits for them, and re-layouts, window_table(): grid[lat_off:lat_off + out_rows, lon_off:lon_off + lon_n, lev_off:lev_off...  9.23 us
    concatenate x4, other arithmetic, wrap_levels(): wrapped = jnp.concatenate([field[:, -1:], field, field[:, :1]], axis=1)  5.3 us
  transfers between devices with their start and end apart: 7, of which 3 were waited for; matrix products, arithmetic and copies ran while one was open for 50% of the time, Pallas kernels for 0%

profile of v3, /device:TPU:0, one launch (start us, length us, event | category | flops | bytes accessed | tf_op | source)
XLA Modules:
  0.0 235.0 jit_solution(17449935497202735239)
XLA Ops:
  10.4 3.1 %collective-permute-start = (f32[1,40,8,256]{3,2,1,0:T(8,128)S(1)}, f32[1,40,8,256]{3,2,1,0:T(8,128)S(1)}, u32[]{:S(2)}, u32[]{:S(2)}) collective-permute-start(f32[1,40,8,256]{3,2,1,0:T(8,128)S(1)} %get-tuple-element.74), channel_id=1, source_target_pairs={{0,1},{1,2},{2,3},{3,4},{4,5},{5,6},{6,7},{7,8},{8,9},{9,10},{10,1... | collective-permute-start | bytes 983048 | tf_op jit(solution)/shard_map/ppermute | solution.py:17
  15.8 2.5 %pad_maximum_fusion.4 = (f32[2,40,8,256]{3,2,1,0:T(8,128)}, f32[4,40,8,256]{3,2,1,0:T(8,128)S(1)}, f32[2,40,8,256]{3,2,1,0:T(8,128)}) fusion(f32[1,40,8,256]{3,2,1,0:T(8,128)S(1)} %collective-permute-done.1, f32[2,40,8,256]{3,2,1,0:T(8,128)} %param.8, f32[4,40,8,256]{3,2,1,0:T(8,128)S(1)} %constant_dynamic-update-slice_fusion.2, ...), kind=kLoop, calls=%fused_computation.27 | loop fusion | flops 327680 | bytes 3276800 | tf_op jit(solution)/shard_map/concatenate | solution.py:19
  19.9 4.4 %fusion.11 = (f32[2,40,8,256]{3,2,1,0:T(8,128)}, f32[2,40,8,256]{3,2,1,0:T(8,128)}, f32[2,40,8,256]{3,2,1,0:T(8,128)}, f32[2,40,8,256]{3,2,1,0:T(8,128)}, f32[2,...) fusion(f32[4,42,10,256]{3,2,1,0:T(8,128)S(1)} %select_maximum_f, ...), kind=kLoop, calls=%fused_computation.106 | loop fusion | bytes 23592960 | tf_op jit(solution)/shard_map/slice | solution.py:38
  24.4 2.1 constant_dynamic-update-slice_fusion.29
  26.5 2.7 %pad_maximum_fusion.3 = (f32[2,40,8,256]{3,2,1,0:T(8,128)S(1)}, f32[2,40,8,256]{3,2,1,0:T(8,128)S(1)}, f32[2,40,8,256]{3,2,1,0:T(8,128)S(1)}, f32[2,40,8,256]{3,...) fusion(f32[4,1,8,256]{3,2,1,0:T(8,128)} %copy-done.35, f32[4,40,8,256]{3,2,1,0:T(8,128)} %copy-done.2, ...), kind=kLoop, calls=%fused_computation.26 | loop fusion | flops 983040 | bytes 5308416 | tf_op jit(solution)/shard_map/concatenate | solution.py:24
  30.1 2.0 constant_dynamic-update-slice_fusion.27
  32.1 2.0 constant_dynamic-update-slice_fusion.26
  34.1 2.0 constant_dynamic-update-slice_fusion.25
  36.0 2.0 constant_dynamic-update-slice_fusion.24
  38.0 2.0 constant_dynamic-update-slice_fusion.23
  40.9 2.0 constant_dynamic-update-slice_fusion.21
  42.9 2.0 constant_dynamic-update-slice_fusion.20
  60.2 19.4 %all-gather.4.cloned.1.call-done = f32[256,27,256]{2,0,1:T(8,128)} async-done(((f32[16,27,256]{2,0,1:T(8,128)}), f32[256,27,256]{2,0,1:T(8,128)}) %all-gather.4.cloned.1.call-update) | async-done | bytes 7077904 | tf_op jit(solution)/shard_map/all_gather | solution.py:60
  79.6 13.7 %fusion.18 = f32[640,256,1]{1,0,2:T(8,128)S(1)} fusion(f32[640,27,256]{2,0,1:T(8,128)} %constant_dynamic-update-slice_fusion.3, f32[256,27,256]{2,0,1:T(8,128)} %all-gather.4.cloned.1.call-done), kind=kOutput, calls=%fused_computation.113 | convolution fusion | flops 6794772480 | bytes 25427968 | tf_op jit(solution)/shard_map/rop,poc->rc/dot_general | solution.py:46
  94.9 19.6 %convolution_bitcast_fusion = f32[256,27,256]{2,0,1:T(8,128)} fusion(f32[640,27,256]{2,0,1:T(8,128)} %constant_dynamic-update-slice_fusion.3, f32[640,256,1]{1,0,2:T(8,128)S(1)} %bitcast.78), kind=kOutput, calls=%fused_computation.2 | convolution fusion | flops 6794772480 | bytes 25427968 | tf_op jit(solution)/shard_map/rq,rop->poq/dot_general | solution.py:82
  114.6 2.2 collective-permute-start.2
  118.3 2.0 collective-permute-done.3
  121.6 4.4 %fusion.10 = (f32[2,40,8,256]{3,2,1,0:T(8,128)}, f32[2,40,8,256]{3,2,1,0:T(8,128)}, f32[2,40,8,256]{3,2,1,0:T(8,128)}, f32[2,40,8,256]{3,2,1,0:T(8,128)}, f32[2,...) fusion(f32[4,42,10,256]{3,2,1,0:T(8,128)S(1)} %select_maximum_f, ...), kind=kLoop, calls=%fused_computation.105 | loop fusion | bytes 23592960 | tf_op jit(solution)/shard_map/slice | solution.py:38
  126.1 2.1 constant_dynamic-update-slice_fusion.56
  128.3 1.6 maximum_maximum_fusion
  131.2 2.1 constant_dynamic-update-slice_fusion.54
  133.3 2.0 constant_dynamic-update-slice_fusion.53
  157.2 11.0 %fusion.19 = f32[640,256,1]{1,0,2:T(8,128)S(1)} fusion(f32[640,27,256]{2,0,1:T(8,128)} %constant_dynamic-update-slice_fusion.30, f32[256,27,256]{2,0,1:T(8,128)S(1)} %bitcast.81), kind=kOutput, calls=%fused_computation.114 | convolution fusion | flops 6794772480 | bytes 25427968 | tf_op jit(solution)/shard_map/roc,qoc->rq/dot_general | solution.py:50
  171.8 56.6 %reduce-scatter.2.cloned.1.call-done = f32[16,27,256]{2,0,1:T(8,128)} async-done(((f32[256,27,256]{2,0,1:T(8,128)}), f32[16,27,256]{2,0,1:T(8,128)}) %reduce-scatter.2.cloned.1.call-update) | async-done | bytes 442384 | tf_op jit(solution)/shard_map/reduce_scatter | solution.py:81
  (156 shorter events, 55.4 us)
Async XLA Ops:
  7.2 72.4 %all-gather.4.cloned.1.call-start = ((), (), s32[]{:S(2)}) async-start(), calls=%async_computation.1 | async-start | bytes 7520256 | tf_op jit(solution)/shard_map/all_gather | solution.py:60
  7.9 161.2 %all-gather.6.cloned.1.call-start = ((), (), s32[]{:S(2)}) async-start(), calls=%async_computation.3 | async-start | bytes 1114112 | tf_op jit(solution)/shard_map/all_gather | solution.py:79
  9.1 6.7 %collective-permute-start.1 = (f32[1,40,8,256]{3,2,1,0:T(8,128)S(1)}, f32[1,40,8,256]{3,2,1,0:T(8,128)S(1)}, u32[]{:S(2)}, u32[]{:S(2)}) collective-permute-start(f32[1,40,8,256]{3,2,1,0:T(8,128)S(1)} %get-tuple-element.73), channel_id=1, source_target_pairs={{1,0},{2,1},{3,2},{4,3},{5,4},{6,5},{7,6},{8,7},{9,8},{10,9},{11,1... | collective-permute-start | bytes 983048 | tf_op jit(solution)/shard_map/ppermute | solution.py:18
  10.4 5.4 %collective-permute-start = (f32[1,40,8,256]{3,2,1,0:T(8,128)S(1)}, f32[1,40,8,256]{3,2,1,0:T(8,128)S(1)}, u32[]{:S(2)}, u32[]{:S(2)}) collective-permute-start(f32[1,40,8,256]{3,2,1,0:T(8,128)S(1)} %get-tuple-element.74), channel_id=1, source_target_pairs={{0,1},{1,2},{2,3},{3,4},{4,5},{5,6},{6,7},{7,8},{8,9},{9,10},{10,1... | collective-permute-start | bytes 983048 | tf_op jit(solution)/shard_map/ppermute | solution.py:17
  19.9 27.8 %copy-start.3 = (f32[2,40,8,256]{3,2,1,0:T(8,128)S(1)}, f32[2,40,8,256]{3,2,1,0:T(8,128)}, u32[]{:S(2)}) copy-start(f32[2,40,8,256]{3,2,1,0:T(8,128)} %param.8) | copy-start | bytes 1966084
  24.3 25.1 %copy-start.24 = (f32[2,40,8,256]{3,2,1,0:T(8,128)S(1)}, f32[2,40,8,256]{3,2,1,0:T(8,128)}, u32[]{:S(2)}) copy-start(f32[2,40,8,256]{3,2,1,0:T(8,128)} %get-tuple-element.33) | copy-start | bytes 1966084
  24.3 26.8 %copy-start.21 = (f32[2,40,8,256]{3,2,1,0:T(8,128)S(1)}, f32[2,40,8,256]{3,2,1,0:T(8,128)}, u32[]{:S(2)}) copy-start(f32[2,40,8,256]{3,2,1,0:T(8,128)} %get-tuple-element.32) | copy-start | bytes 1966084
  24.4 27.7 %copy-start.20 = (f32[2,40,8,256]{3,2,1,0:T(8,128)S(1)}, f32[2,40,8,256]{3,2,1,0:T(8,128)}, u32[]{:S(2)}) copy-start(f32[2,40,8,256]{3,2,1,0:T(8,128)} %get-tuple-element.31) | copy-start | bytes 1966084
  24.4 29.5 %copy-start.17 = (f32[2,40,8,256]{3,2,1,0:T(8,128)S(1)}, f32[2,40,8,256]{3,2,1,0:T(8,128)}, u32[]{:S(2)}) copy-start(f32[2,40,8,256]{3,2,1,0:T(8,128)} %get-tuple-element.30) | copy-start | bytes 1966084
  24.4 30.4 %copy-start.16 = (f32[2,40,8,256]{3,2,1,0:T(8,128)S(1)}, f32[2,40,8,256]{3,2,1,0:T(8,128)}, u32[]{:S(2)}) copy-start(f32[2,40,8,256]{3,2,1,0:T(8,128)} %get-tuple-element.29) | copy-start | bytes 1966084
  24.4 31.3 %copy-start.34 = (f32[2,40,8,256]{3,2,1,0:T(8,128)S(1)}, f32[2,40,8,256]{3,2,1,0:T(8,128)}, u32[]{:S(2)}) copy-start(f32[2,40,8,256]{3,2,1,0:T(8,128)} %get-tuple-element.70) | copy-start | bytes 1966084
  24.4 32.2 %copy-start.13 = (f32[2,40,8,256]{3,2,1,0:T(8,128)S(1)}, f32[2,40,8,256]{3,2,1,0:T(8,128)}, u32[]{:S(2)}) copy-start(f32[2,40,8,256]{3,2,1,0:T(8,128)} %get-tuple-element.28) | copy-start | bytes 1966084
  26.5 30.9 %copy-start.12 = (f32[2,40,8,256]{3,2,1,0:T(8,128)S(1)}, f32[2,40,8,256]{3,2,1,0:T(8,128)}, u32[]{:S(2)}) copy-start(f32[2,40,8,256]{3,2,1,0:T(8,128)} %get-tuple-element.27) | copy-start | bytes 1966084
  29.2 30.0 %copy-start.9 = (f32[2,40,8,256]{3,2,1,0:T(8,128)S(1)}, f32[2,40,8,256]{3,2,1,0:T(8,128)}, u32[]{:S(2)}) copy-start(f32[2,40,8,256]{3,2,1,0:T(8,128)} %get-tuple-element.26) | copy-start | bytes 1966084
  55.7 37.6 %copy-start.32 = (f32[2,40,8,256]{3,2,1,0:T(8,128)S(1)}, f32[2,40,8,256]{3,2,1,0:T(8,128)}, u32[]{:S(2)}) copy-start(f32[2,40,8,256]{3,2,1,0:T(8,128)} %param.9) | copy-start | bytes 1966084
  55.7 37.6 %copy-start.36 = (f32[256]{0:T(256)S(1)}, f32[256]{0:T(256)}, u32[]{:S(2)}) copy-start(f32[256]{0:T(256)} %param.11) | copy-start | bytes 3076
  57.5 36.3 %copy-start.37 = (s32[8]{0:T(128)S(1)}, s32[8]{0:T(128)}, u32[]{:S(2)}) copy-start(s32[8]{0:T(128)} %param.15) | copy-start | bytes 100
  94.7 133.8 %reduce-scatter.2.cloned.1.call-start = ((), (), s32[]{:S(2)}) async-start(), calls=%async_computation.2 | async-start | bytes 7520256 | tf_op jit(solution)/shard_map/reduce_scatter | solution.py:81
  114.6 3.7 %collective-permute-start.2 = (f32[1,40,8,256]{3,2,1,0:T(8,128)S(1)}, f32[1,40,8,256]{3,2,1,0:T(8,128)S(1)}, u32[]{:S(2)}, u32[]{:S(2)}) collective-permute-start(f32[1,40,8,256]{3,2,1,0:T(8,128)S(1)} %get-tuple-element.68), channel_id=1, source_target_pairs={{0,1},{1,2},{2,3},{3,4},{4,5},{5,6},{6,7},{7,8},{8,9},{9,10},{10,1... | collective-permute-start | bytes 983048 | tf_op jit(solution)/shard_map/ppermute | solution.py:17
  116.8 3.5 %collective-permute-start.3 = (f32[1,40,8,256]{3,2,1,0:T(8,128)S(1)}, f32[1,40,8,256]{3,2,1,0:T(8,128)S(1)}, u32[]{:S(2)}, u32[]{:S(2)}) collective-permute-start(f32[1,40,8,256]{3,2,1,0:T(8,128)S(1)} %get-tuple-element.69), channel_id=1, source_target_pairs={{1,0},{2,1},{3,2},{4,3},{5,4},{6,5},{7,6},{8,7},{9,8},{10,9},{11,1... | collective-permute-start | bytes 983048 | tf_op jit(solution)/shard_map/ppermute | solution.py:18
  130.3 24.2 %copy-start.7 = (f32[2,40,8,256]{3,2,1,0:T(8,128)S(1)}, f32[2,40,8,256]{3,2,1,0:T(8,128)}, u32[]{:S(2)}) copy-start(f32[2,40,8,256]{3,2,1,0:T(8,128)} %get-tuple-element.9) | copy-start | bytes 1966084
  130.3 26.0 %copy-start.6 = (f32[2,40,8,256]{3,2,1,0:T(8,128)S(1)}, f32[2,40,8,256]{3,2,1,0:T(8,128)}, u32[]{:S(2)}) copy-start(f32[2,40,8,256]{3,2,1,0:T(8,128)} %get-tuple-element.8) | copy-start | bytes 1966084
  131.2 26.0 %slice-start = ((s8[7077888]{0:T(1024)(128)(4,1)}), s8[4194304]{0:T(1024)(128)(4,1)S(1)}, s32[]{:S(2)}) async-start(s8[7077888]{0:T(1024)(128)(4,1)} %bitcast.80), calls=%async_computation.4 | async-start | bytes 8388608
  154.5 73.9 %copy-start.1 = (f32[4,256]{1,0:T(4,128)S(1)}, f32[4,256]{1,0:T(4,128)}, u32[]{:S(2)}) copy-start(f32[4,256]{1,0:T(4,128)} %param.13) | copy-start | bytes 12292
  (23 other events, 342.9 us)
Sparse Core Ops, SparseCore 0:
  10.2 69.3 all-gather.3
  94.8 40.0 all-gather.5
  139.5 88.8 reduce-scatter.1

commit v4 on v3

--- a/solution.py
+++ b/solution.py
@@ -50,6 +50,17 @@
     return jnp.einsum("roc,qoc->rq", table, piece, precision=high)
 
 
+def all_sum(x):
+    count = lax.axis_size("space")
+    if count & (count - 1):
+        return lax.psum(x, "space")
+    bit = 1
+    while bit < count:
+        x = x + lax.ppermute(x, "space", [(i, i ^ bit) for i in range(count)])
+        bit *= 2
+    return x
+
+
 def per_device(field, grad_out, weight, bias, land_bias, level_gain, land_mask, level_index):
     rows, lon_n, lev_n, chans = field.shape
     land_float = land_mask.astype(jnp.float32)
@@ -74,9 +85,7 @@
     local_land = jnp.sum(land_float[:, :, None, None] * delta, axis=(0, 1, 2))
     per_level = jnp.sum(grad_out * active, axis=(0, 1))
     local_gain = jnp.dot(one_hot.T, per_level, precision=highest)
-    partial = jnp.concatenate([local_bias[None], local_land[None], local_gain], axis=0)
-    partial = jnp.pad(partial, ((0, 64 - partial.shape[0]), (0, 0)))
-    sums = jnp.sum(lax.all_gather(partial, "space", axis=0, tiled=False), axis=0)
+    sums = all_sum(jnp.concatenate([local_bias[None], local_land[None], local_gain], axis=0))
     delta_flat = delta.reshape(-1, chans)
     grad_weight = lax.psum_scatter(
         jnp.einsum("rq,rop->poq", delta_flat, table_pre, precision=high),

time: 236 us -> 209 us (0.89)
  waiting for transfers between devices: 78.7 us -> 45.4 us
  starting transfers between devices: 8.34 us -> 16.6 us
    reduce_scatter x1, waiting for transfers between devices: 56.6 us -> 17.1 us  [per_device(): lax.psum_scatter(jnp.einsum('rq,rop->poq', delta_flat, table_pre, precisi...]
    ppermute x0 -> x4, waiting for transfers between devices: none -> 8.53 us  [all_sum(): x = x + lax.ppermute(x, 'space', [(i, i ^ bit) for i in range(count)])]
    ppermute x0 -> x4, starting transfers between devices: none -> 8.5 us  [all_sum(): x = x + lax.ppermute(x, 'space', [(i, i ^ bit) for i in range(count)])]
  transfers between devices with their start and end apart: 7 -> 10, of which waited for: 3 -> 5; matrix products, arithmetic and copies ran while one was open for 50% -> 46% of each run, Pallas kernels for 0% -> 0%
where the time goes in v4:
time: 209 us
  local copies, waits for them, and re-layouts  74.8 us (36%)
  waiting for transfers between devices  45.4 us (22%)
  matrix products  45.1 us (22%)
  starting transfers between devices  16.6 us (8%)
  between operations  14.5 us (7%)
  other arithmetic  12.4 us (6%)
    unnamed x133, local copies, waits for them, and re-layouts  61.3 us
    dot_general x1, matrix products, per_device(): jnp.einsum('rq,rop->poq', delta_flat, table_pre, precision=high)  19.6 us
    all_gather x1, waiting for transfers between devices, per_device(): full_weight = lax.all_gather(weight, 'space', axis=0, tiled=True)  19.1 us
    reduce_scatter x1, waiting for transfers between devices, per_device(): lax.psum_scatter(jnp.einsum('rq,rop->poq', delta_flat, table_pre, precisi...  17.1 us
    dot_general x1, matrix products, conv_piece(): return jnp.einsum('rop,poc->rc', table, piece, precision=high)  13.7 us
    dot_general x1, matrix products, back_piece(): return jnp.einsum('roc,qoc->rq', table, piece, precision=high)  10.7 us
    slice x3, local copies, waits for them, and re-layouts, window_table(): grid[lat_off:lat_off + out_rows, lon_off:lon_off + lon_n, lev_off:lev_off...  9.27 us
    ppermute x4, waiting for transfers between devices, all_sum(): x = x + lax.ppermute(x, 'space', [(i, i ^ bit) for i in range(count)])  8.53 us
  transfers between devices with their start and end apart: 10, of which 5 were waited for; matrix products, arithmetic and copies ran while one was open for 46% of the time, Pallas kernels for 0%

profile of v4, /device:TPU:0, one launch (start us, length us, event | category | flops | bytes accessed | tf_op | source)
XLA Modules:
  0.0 208.8 jit_solution(12286144815160069324)
XLA Ops:
  10.4 3.1 %collective-permute-start = (f32[1,40,8,256]{3,2,1,0:T(8,128)S(1)}, f32[1,40,8,256]{3,2,1,0:T(8,128)S(1)}, u32[]{:S(2)}, u32[]{:S(2)}) collective-permute-start(f32[1,40,8,256]{3,2,1,0:T(8,128)S(1)} %get-tuple-element.74), channel_id=1, source_target_pairs={{0,1},{1,2},{2,3},{3,4},{4,5},{5,6},{6,7},{7,8},{8,9},{9,10},{10,1... | collective-permute-start | bytes 983048 | tf_op jit(solution)/shard_map/ppermute | solution.py:17
  15.8 2.6 %pad_maximum_fusion.4 = (f32[2,40,8,256]{3,2,1,0:T(8,128)}, f32[4,40,8,256]{3,2,1,0:T(8,128)S(1)}, f32[2,40,8,256]{3,2,1,0:T(8,128)}) fusion(f32[1,40,8,256]{3,2,1,0:T(8,128)S(1)} %collective-permute-done.1, f32[2,40,8,256]{3,2,1,0:T(8,128)} %param.8, f32[4,40,8,256]{3,2,1,0:T(8,128)S(1)} %constant_dynamic-update-slice_fusion.2, ...), kind=kLoop, calls=%fused_computation.27 | loop fusion | flops 327680 | bytes 3276800 | tf_op jit(solution)/shard_map/concatenate | solution.py:19
  20.0 4.5 %fusion.12 = (f32[2,40,8,256]{3,2,1,0:T(8,128)}, f32[2,40,8,256]{3,2,1,0:T(8,128)}, f32[2,40,8,256]{3,2,1,0:T(8,128)}, f32[2,40,8,256]{3,2,1,0:T(8,128)}, f32[2,...) fusion(f32[4,42,10,256]{3,2,1,0:T(8,128)S(1)} %select_maximum_f, ...), kind=kLoop, calls=%fused_computation.105 | loop fusion | bytes 23592960 | tf_op jit(solution)/shard_map/slice | solution.py:38
  24.6 2.1 %constant_dynamic-update-slice_fusion.29 = f32[640,27,256]{2,0,1:T(8,128)} fusion(f32[640,1,256]{2,0,1:T(8,128)} %bitcast.118), kind=kLoop, calls=%fused_computation.64 | loop fusion | bytes 1310720
  26.7 2.7 %pad_maximum_fusion.3 = (f32[2,40,8,256]{3,2,1,0:T(8,128)S(1)}, f32[2,40,8,256]{3,2,1,0:T(8,128)S(1)}, f32[2,40,8,256]{3,2,1,0:T(8,128)S(1)}, f32[2,40,8,256]{3,...) fusion(f32[4,1,8,256]{3,2,1,0:T(8,128)} %copy-done.35, f32[4,40,8,256]{3,2,1,0:T(8,128)} %copy-done.2, ...), kind=kLoop, calls=%fused_computation.26 | loop fusion | flops 983040 | bytes 5308416 | tf_op jit(solution)/shard_map/concatenate | solution.py:24
  30.3 2.0 constant_dynamic-update-slice_fusion.27
  32.2 2.0 constant_dynamic-update-slice_fusion.26
  38.2 2.0 constant_dynamic-update-slice_fusion.23
  43.0 2.1 %constant_dynamic-update-slice_fusion.20 = f32[640,27,256]{2,0,1:T(8,128)} fusion(f32[640,27,256]{2,0,1:T(8,128)} %constant_dynamic-update-slice_fusion.21, f32[640,1,256]{2,0,1:T(8,128)} %bitcast.110), kind=kLoop, calls=%fused_computation.55 | loop fusion | bytes 1310720
  60.5 19.1 %all-gather.2.cloned.1.call-done = f32[256,27,256]{2,0,1:T(8,128)} async-done(((f32[16,27,256]{2,0,1:T(8,128)}), f32[256,27,256]{2,0,1:T(8,128)}) %all-gather.2.cloned.1.call-update) | async-done | bytes 7077904 | tf_op jit(solution)/shard_map/all_gather | solution.py:71
  79.6 13.7 %fusion.19 = f32[640,256,1]{1,0,2:T(8,128)S(1)} fusion(f32[640,27,256]{2,0,1:T(8,128)} %constant_dynamic-update-slice_fusion.3, f32[256,27,256]{2,0,1:T(8,128)} %all-gather.2.cloned.1.call-done), kind=kOutput, calls=%fused_computation.112 | convolution fusion | flops 6794772480 | bytes 25427968 | tf_op jit(solution)/shard_map/rop,poc->rc/dot_general | solution.py:46
  93.8 19.6 %convolution_bitcast_fusion = f32[256,27,256]{2,0,1:T(8,128)} fusion(f32[640,27,256]{2,0,1:T(8,128)} %constant_dynamic-update-slice_fusion.3, f32[640,256,1]{1,0,2:T(8,128)S(1)} %bitcast.77), kind=kOutput, calls=%fused_computation.2 | convolution fusion | flops 6794772480 | bytes 25427968 | tf_op jit(solution)/shard_map/rq,rop->poq/dot_general | solution.py:91
  114.0 2.2 %collective-permute-start.2 = (f32[1,40,8,256]{3,2,1,0:T(8,128)S(1)}, f32[1,40,8,256]{3,2,1,0:T(8,128)S(1)}, u32[]{:S(2)}, u32[]{:S(2)}) collective-permute-start(f32[1,40,8,256]{3,2,1,0:T(8,128)S(1)} %get-tuple-element.68), channel_id=1, source_target_pairs={{0,1},{1,2},{2,3},{3,4},{4,5},{5,6},{6,7},{7,8},{8,9},{9,10},{10,1... | collective-permute-start | bytes 983048 | tf_op jit(solution)/shard_map/ppermute | solution.py:17
  117.8 2.7 %collective-permute-start.5 = (f32[6,256]{1,0:T(8,128)S(1)}, f32[6,256]{1,0:T(8,128)S(1)}, u32[]{:S(2)}, u32[]{:S(2)}) collective-permute-start(f32[6,256]{1,0:T(8,128)S(1)} %fusion.9), channel_id=1, source_target_pairs={{0,2},{1,3},{2,0},{3,1},{4,6},{5,7},{6,4},{7,5},{8,10},{9,11},{10,... | collective-permute-start | bytes 18440 | tf_op jit(solution)/shard_map/ppermute | solution.py:59
  120.5 4.9 %collective-permute-done.5 = f32[6,256]{1,0:T(8,128)S(1)} collective-permute-done((f32[6,256]{1,0:T(8,128)S(1)}, f32[6,256]{1,0:T(8,128)S(1)}, u32[]{:S(2)}, u32[]{:S(2)}) %collective-permute-start.5) | collective-permute-done | bytes 6176 | tf_op jit(solution)/shard_map/ppermute | solution.py:59
  125.4 2.9 %collective-permute-start.6 = (f32[6,256]{1,0:T(8,128)S(1)}, f32[6,256]{1,0:T(8,128)S(1)}, u32[]{:S(2)}, u32[]{:S(2)}) collective-permute-start(f32[6,256]{1,0:T(8,128)S(1)} %add.51), channel_id=1, source_target_pairs={{0,4},{1,5},{2,6},{3,7},{4,0},{5,1},{6,2},{7,3},{8,12},{9,13},{10,... | collective-permute-start | bytes 18440 | tf_op jit(solution)/shard_map/ppermute | solution.py:59
  129.9 2.5 %collective-permute-start.7 = (f32[6,256]{1,0:T(8,128)S(1)}, f32[6,256]{1,0:T(8,128)S(1)}, u32[]{:S(2)}, u32[]{:S(2)}) collective-permute-start(f32[6,256]{1,0:T(8,128)S(1)} %add.52), channel_id=1, source_target_pairs={{0,8},{1,9},{2,10},{3,11},{4,12},{5,13},{6,14},{7,15},{8,0},{9,1},... | collective-permute-start | bytes 18440 | tf_op jit(solution)/shard_map/ppermute | solution.py:59
  132.5 2.0 collective-permute-done.7
  137.1 4.4 %fusion.11 = (f32[2,40,8,256]{3,2,1,0:T(8,128)}, f32[2,40,8,256]{3,2,1,0:T(8,128)}, f32[2,40,8,256]{3,2,1,0:T(8,128)}, f32[2,40,8,256]{3,2,1,0:T(8,128)}, f32[2,...) fusion(f32[4,42,10,256]{3,2,1,0:T(8,128)S(1)} %select_maximum_f, ...), kind=kLoop, calls=%fused_computation.104 | loop fusion | bytes 23592960 | tf_op jit(solution)/shard_map/slice | solution.py:38
  141.6 2.2 %constant_dynamic-update-slice_fusion.56 = f32[640,27,256]{2,0,1:T(8,128)} fusion(f32[640,1,256]{2,0,1:T(8,128)} %bitcast.119), kind=kLoop, calls=%fused_computation.91 | loop fusion | bytes 1310720
  147.1 2.1 %constant_dynamic-update-slice_fusion.54 = f32[640,27,256]{2,0,1:T(8,128)} fusion(f32[640,27,256]{2,0,1:T(8,128)} %constant_dynamic-update-slice_fusion.55, f32[640,1,256]{2,0,1:T(8,128)} %bitcast.115), kind=kLoop, calls=%fused_computation.89 | loop fusion | bytes 1310720
  149.2 2.0 constant_dynamic-update-slice_fusion.53
  173.2 10.7 %fusion.20 = f32[640,256,1]{1,0,2:T(8,128)S(1)} fusion(f32[640,27,256]{2,0,1:T(8,128)} %constant_dynamic-update-slice_fusion.30, f32[256,27,256]{2,0,1:T(8,128)S(1)} %bitcast.80), kind=kOutput, calls=%fused_computation.113 | convolution fusion | flops 6794772480 | bytes 25427968 | tf_op jit(solution)/shard_map/roc,qoc->rq/dot_general | solution.py:50
  184.8 17.1 %reduce-scatter.2.cloned.1.call-done = f32[16,27,256]{2,0,1:T(8,128)} async-done(((f32[256,27,256]{2,0,1:T(8,128)}), f32[16,27,256]{2,0,1:T(8,128)}) %reduce-scatter.2.cloned.1.call-update) | async-done | bytes 442384 | tf_op jit(solution)/shard_map/reduce_scatter | solution.py:90
  (164 shorter events, 63.1 us)
Async XLA Ops:
  7.2 72.4 %all-gather.2.cloned.1.call-start = ((), (), s32[]{:S(2)}) async-start(), calls=%async_computation.1 | async-start | bytes 7520256 | tf_op jit(solution)/shard_map/all_gather | solution.py:71
  7.9 194.0 %reduce-scatter.2.cloned.1.call-start = ((), (), s32[]{:S(2)}) async-start(), calls=%async_computation.2 | async-start | bytes 7520256 | tf_op jit(solution)/shard_map/reduce_scatter | solution.py:90
  9.1 6.7 %collective-permute-start.1 = (f32[1,40,8,256]{3,2,1,0:T(8,128)S(1)}, f32[1,40,8,256]{3,2,1,0:T(8,128)S(1)}, u32[]{:S(2)}, u32[]{:S(2)}) collective-permute-start(f32[1,40,8,256]{3,2,1,0:T(8,128)S(1)} %get-tuple-element.73), channel_id=1, source_target_pairs={{1,0},{2,1},{3,2},{4,3},{5,4},{6,5},{7,6},{8,7},{9,8},{10,9},{11,1... | collective-permute-start | bytes 983048 | tf_op jit(solution)/shard_map/ppermute | solution.py:18
  10.4 5.4 %collective-permute-start = (f32[1,40,8,256]{3,2,1,0:T(8,128)S(1)}, f32[1,40,8,256]{3,2,1,0:T(8,128)S(1)}, u32[]{:S(2)}, u32[]{:S(2)}) collective-permute-start(f32[1,40,8,256]{3,2,1,0:T(8,128)S(1)} %get-tuple-element.74), channel_id=1, source_target_pairs={{0,1},{1,2},{2,3},{3,4},{4,5},{5,6},{6,7},{7,8},{8,9},{9,10},{10,1... | collective-permute-start | bytes 983048 | tf_op jit(solution)/shard_map/ppermute | solution.py:17
  20.0 28.0 %copy-start.3 = (f32[2,40,8,256]{3,2,1,0:T(8,128)S(1)}, f32[2,40,8,256]{3,2,1,0:T(8,128)}, u32[]{:S(2)}) copy-start(f32[2,40,8,256]{3,2,1,0:T(8,128)} %param.8) | copy-start | bytes 1966084
  24.5 27.0 %copy-start.21 = (f32[2,40,8,256]{3,2,1,0:T(8,128)S(1)}, f32[2,40,8,256]{3,2,1,0:T(8,128)}, u32[]{:S(2)}) copy-start(f32[2,40,8,256]{3,2,1,0:T(8,128)} %get-tuple-element.32) | copy-start | bytes 1966084
  24.5 27.9 %copy-start.20 = (f32[2,40,8,256]{3,2,1,0:T(8,128)S(1)}, f32[2,40,8,256]{3,2,1,0:T(8,128)}, u32[]{:S(2)}) copy-start(f32[2,40,8,256]{3,2,1,0:T(8,128)} %get-tuple-element.31) | copy-start | bytes 1966084
  24.5 29.7 %copy-start.17 = (f32[2,40,8,256]{3,2,1,0:T(8,128)S(1)}, f32[2,40,8,256]{3,2,1,0:T(8,128)}, u32[]{:S(2)}) copy-start(f32[2,40,8,256]{3,2,1,0:T(8,128)} %get-tuple-element.30) | copy-start | bytes 1966084
  24.5 30.6 %copy-start.16 = (f32[2,40,8,256]{3,2,1,0:T(8,128)S(1)}, f32[2,40,8,256]{3,2,1,0:T(8,128)}, u32[]{:S(2)}) copy-start(f32[2,40,8,256]{3,2,1,0:T(8,128)} %get-tuple-element.29) | copy-start | bytes 1966084
  24.5 31.5 %copy-start.34 = (f32[2,40,8,256]{3,2,1,0:T(8,128)S(1)}, f32[2,40,8,256]{3,2,1,0:T(8,128)}, u32[]{:S(2)}) copy-start(f32[2,40,8,256]{3,2,1,0:T(8,128)} %get-tuple-element.70) | copy-start | bytes 1966084
  24.5 32.4 %copy-start.13 = (f32[2,40,8,256]{3,2,1,0:T(8,128)S(1)}, f32[2,40,8,256]{3,2,1,0:T(8,128)}, u32[]{:S(2)}) copy-start(f32[2,40,8,256]{3,2,1,0:T(8,128)} %get-tuple-element.28) | copy-start | bytes 1966084
  26.7 31.1 %copy-start.12 = (f32[2,40,8,256]{3,2,1,0:T(8,128)S(1)}, f32[2,40,8,256]{3,2,1,0:T(8,128)}, u32[]{:S(2)}) copy-start(f32[2,40,8,256]{3,2,1,0:T(8,128)} %get-tuple-element.27) | copy-start | bytes 1966084
  29.4 30.2 %copy-start.9 = (f32[2,40,8,256]{3,2,1,0:T(8,128)S(1)}, f32[2,40,8,256]{3,2,1,0:T(8,128)}, u32[]{:S(2)}) copy-start(f32[2,40,8,256]{3,2,1,0:T(8,128)} %get-tuple-element.26) | copy-start | bytes 1966084
  56.0 37.3 %copy-start.32 = (f32[2,40,8,256]{3,2,1,0:T(8,128)S(1)}, f32[2,40,8,256]{3,2,1,0:T(8,128)}, u32[]{:S(2)}) copy-start(f32[2,40,8,256]{3,2,1,0:T(8,128)} %param.9) | copy-start | bytes 1966084
  56.0 37.3 %copy-start.36 = (f32[256]{0:T(256)S(1)}, f32[256]{0:T(256)}, u32[]{:S(2)}) copy-start(f32[256]{0:T(256)} %param.11) | copy-start | bytes 3076
  113.7 4.1 %collective-permute-start.4 = (f32[6,256]{1,0:T(8,128)S(1)}, f32[6,256]{1,0:T(8,128)S(1)}, u32[]{:S(2)}, u32[]{:S(2)}) collective-permute-start(f32[6,256]{1,0:T(8,128)S(1)} %pad_maximum_fusion.10), channel_id=1, source_target_pairs={{0,1},{1,0},{2,3},{3,2},{4,5},{5,4},{6,7},{7,6},{8,9},{9,8},{10,11... | collective-permute-start | bytes 18440 | tf_op jit(solution)/shard_map/ppermute | solution.py:59
  114.0 21.6 %collective-permute-start.2 = (f32[1,40,8,256]{3,2,1,0:T(8,128)S(1)}, f32[1,40,8,256]{3,2,1,0:T(8,128)S(1)}, u32[]{:S(2)}, u32[]{:S(2)}) collective-permute-start(f32[1,40,8,256]{3,2,1,0:T(8,128)S(1)} %get-tuple-element.68), channel_id=1, source_target_pairs={{0,1},{1,2},{2,3},{3,4},{4,5},{5,6},{6,7},{7,8},{8,9},{9,10},{10,1... | collective-permute-start | bytes 983048 | tf_op jit(solution)/shard_map/ppermute | solution.py:17
  116.2 19.4 %collective-permute-start.3 = (f32[1,40,8,256]{3,2,1,0:T(8,128)S(1)}, f32[1,40,8,256]{3,2,1,0:T(8,128)S(1)}, u32[]{:S(2)}, u32[]{:S(2)}) collective-permute-start(f32[1,40,8,256]{3,2,1,0:T(8,128)S(1)} %get-tuple-element.69), channel_id=1, source_target_pairs={{1,0},{2,1},{3,2},{4,3},{5,4},{6,5},{7,6},{8,7},{9,8},{10,9},{11,1... | collective-permute-start | bytes 983048 | tf_op jit(solution)/shard_map/ppermute | solution.py:18
  117.8 7.6 %collective-permute-start.5 = (f32[6,256]{1,0:T(8,128)S(1)}, f32[6,256]{1,0:T(8,128)S(1)}, u32[]{:S(2)}, u32[]{:S(2)}) collective-permute-start(f32[6,256]{1,0:T(8,128)S(1)} %fusion.9), channel_id=1, source_target_pairs={{0,2},{1,3},{2,0},{3,1},{4,6},{5,7},{6,4},{7,5},{8,10},{9,11},{10,... | collective-permute-start | bytes 18440 | tf_op jit(solution)/shard_map/ppermute | solution.py:59
  125.4 4.5 %collective-permute-start.6 = (f32[6,256]{1,0:T(8,128)S(1)}, f32[6,256]{1,0:T(8,128)S(1)}, u32[]{:S(2)}, u32[]{:S(2)}) collective-permute-start(f32[6,256]{1,0:T(8,128)S(1)} %add.51), channel_id=1, source_target_pairs={{0,4},{1,5},{2,6},{3,7},{4,0},{5,1},{6,2},{7,3},{8,12},{9,13},{10,... | collective-permute-start | bytes 18440 | tf_op jit(solution)/shard_map/ppermute | solution.py:59
  129.9 4.5 %collective-permute-start.7 = (f32[6,256]{1,0:T(8,128)S(1)}, f32[6,256]{1,0:T(8,128)S(1)}, u32[]{:S(2)}, u32[]{:S(2)}) collective-permute-start(f32[6,256]{1,0:T(8,128)S(1)} %add.52), channel_id=1, source_target_pairs={{0,8},{1,9},{2,10},{3,11},{4,12},{5,13},{6,14},{7,15},{8,0},{9,1},... | collective-permute-start | bytes 18440 | tf_op jit(solution)/shard_map/ppermute | solution.py:59
  146.2 26.1 %copy-start.6 = (f32[2,40,8,256]{3,2,1,0:T(8,128)S(1)}, f32[2,40,8,256]{3,2,1,0:T(8,128)}, u32[]{:S(2)}) copy-start(f32[2,40,8,256]{3,2,1,0:T(8,128)} %get-tuple-element.8) | copy-start | bytes 1966084
  147.1 26.1 %slice-start = ((s8[7077888]{0:T(1024)(128)(4,1)}), s8[4194304]{0:T(1024)(128)(4,1)S(1)}, s32[]{:S(2)}) async-start(s8[7077888]{0:T(1024)(128)(4,1)} %bitcast.79), calls=%async_computation.3 | async-start | bytes 8388608
  169.6 32.4 %copy-start.1 = (f32[4,256]{1,0:T(4,128)S(1)}, f32[4,256]{1,0:T(4,128)}, u32[]{:S(2)}) copy-start(f32[4,256]{1,0:T(4,128)} %param.13) | copy-start | bytes 12292
  (26 other events, 416.2 us)
Sparse Core Ops, SparseCore 0:
  10.2 69.3 all-gather.1
  113.5 88.4 reduce-scatter.1

commit v5 on v4

--- a/solution.py
+++ b/solution.py
@@ -87,12 +87,10 @@
     local_gain = jnp.dot(one_hot.T, per_level, precision=highest)
     sums = all_sum(jnp.concatenate([local_bias[None], local_land[None], local_gain], axis=0))
     delta_flat = delta.reshape(-1, chans)
-    grad_weight = lax.psum_scatter(
-        jnp.einsum("rq,rop->poq", delta_flat, table_pre, precision=high),
-        "space",
-        scatter_dimension=0,
-        tiled=True,
-    )
+    count = lax.axis_size("space")
+    terms = jnp.einsum("rq,rop->poq", delta_flat, table_pre, precision=high)
+    terms = terms.reshape((count, chans // count) + terms.shape[1:])
+    grad_weight = jnp.sum(lax.all_to_all(terms, "space", 0, 0, tiled=False), axis=0)
     return (grad_field, grad_weight, sums[0], sums[1], sums[2 : 2 + local_gain.shape[0]])
 
 

time: 209 us -> 342 us (1.64)
  waiting for transfers between devices: 45.4 us -> 163 us
  starting transfers between devices: 16.6 us -> 25.1 us
  other arithmetic: 12.4 us -> 16.4 us
  local copies, waits for them, and re-layouts: 74.8 us -> 78.3 us
    ppermute x4, waiting for transfers between devices: 8.53 us -> 143 us  [all_sum(): x = x + lax.ppermute(x, 'space', [(i, i ^ bit) for i in range(count)])]
    reduce_scatter x1 -> x0, waiting for transfers between devices: 17.1 us -> none  [per_device(): lax.psum_scatter(jnp.einsum('rq,rop->poq', delta_flat, table_pre, precisi...]
    all_to_all x0 -> x1, starting transfers between devices: none -> 4.74 us  [per_device(): lax.all_to_all(terms, 'space', 0, 0, tiled=False)]
    reduce_sum x0 -> x1, other arithmetic: none -> 4.61 us  [per_device(): jnp.sum(lax.all_to_all(terms, 'space', 0, 0, tiled=False), axis=0)]
    ppermute x4, starting transfers between devices: 8.5 us -> 12.2 us  [all_sum(): x = x + lax.ppermute(x, 'space', [(i, i ^ bit) for i in range(count)])]
    reshape x0 -> x1, local copies, waits for them, and re-layouts: none -> 3.66 us  [per_device(): terms = terms.reshape((count, chans // count) + terms.shape[1:])]
  transfers between devices with their start and end apart: 10 -> 10, of which waited for: 5 -> 4; matrix products, arithmetic and copies ran while one was open for 46% -> 28% of each run, Pallas kernels for 0% -> 0%
where the time goes in v5:
time: 342 us; the launch traced here: 341 us
  waiting for transfers between devices  163 us (48%)
  local copies, waits for them, and re-layouts  78.3 us (23%)
  matrix products  43.2 us (13%)
  starting transfers between devices  25.1 us (7%)
  other arithmetic  16.4 us (5%)
  between operations  14.5 us (4%)
    ppermute x4, waiting for transfers between devices, all_sum(): x = x + lax.ppermute(x, 'space', [(i, i ^ bit) for i in range(count)])  143 us
    unnamed x133, local copies, waits for them, and re-layouts  61.2 us
    all_gather x1, waiting for transfers between devices, per_device(): full_weight = lax.all_gather(weight, 'space', axis=0, tiled=True)  19.4 us
    dot_general x1, matrix products, per_device(): terms = jnp.einsum('rq,rop->poq', delta_flat, table_pre, precision=high)  17.8 us
    dot_general x1, matrix products, conv_piece(): return jnp.einsum('rop,poc->rc', table, piece, precision=high)  13.7 us
    ppermute x4, starting transfers between devices, all_sum(): x = x + lax.ppermute(x, 'space', [(i, i ^ bit) for i in range(count)])  12.2 us
    dot_general x1, matrix products, back_piece(): return jnp.einsum('roc,qoc->rq', table, piece, precision=high)  10.6 us
    slice x3, local copies, waits for them, and re-layouts, window_table(): grid[lat_off:lat_off + out_rows, lon_off:lon_off + lon_n, lev_off:lev_off...  9.23 us
  transfers between devices with their start and end apart: 10, of which 4 were waited for; matrix products, arithmetic and copies ran while one was open for 28% of the time, Pallas kernels for 0%

profile of v5, /device:TPU:0, one launch (start us, length us, event | category | flops | bytes accessed | tf_op | source)
XLA Modules:
  0.0 340.8 jit_solution(3916459291352299394)
XLA Ops:
  10.3 3.1 collective-permute-start
  15.7 2.5 pad_maximum_fusion.4
  19.8 4.4 %fusion.12 = (f32[2,40,8,256]{3,2,1,0:T(8,128)}, f32[2,40,8,256]{3,2,1,0:T(8,128)}, f32[2,40,8,256]{3,2,1,0:T(8,128)}, f32[2,40,8,256]{3,2,1,0:T(8,128)}, f32[2,...) fusion(f32[4,42,10,256]{3,2,1,0:T(8,128)S(1)} %select_maximum_f, ...), kind=kLoop, calls=%fused_computation.104 | loop fusion | bytes 23592960 | tf_op jit(solution)/shard_map/slice | solution.py:38
  24.4 2.1 constant_dynamic-update-slice_fusion.29
  26.5 2.6 pad_maximum_fusion.3
  30.1 2.0 constant_dynamic-update-slice_fusion.27
  36.0 2.0 constant_dynamic-update-slice_fusion.24
  40.9 2.0 constant_dynamic-update-slice_fusion.21
  60.2 19.4 %all-gather.2.cloned.1.call-done = f32[256,27,256]{2,0,1:T(8,128)} async-done(((f32[16,27,256]{2,0,1:T(8,128)}), f32[256,27,256]{2,0,1:T(8,128)}) %all-gather.2.cloned.1.call-update) | async-done | bytes 7077904 | tf_op jit(solution)/shard_map/all_gather | solution.py:71
  79.6 13.7 %fusion.19 = f32[640,256,1]{1,0,2:T(8,128)S(1)} fusion(f32[640,27,256]{2,0,1:T(8,128)} %constant_dynamic-update-slice_fusion.3, f32[256,27,256]{2,0,1:T(8,128)} %all-gather.2.cloned.1.call-done), kind=kOutput, calls=%fused_computation.111 | convolution fusion | flops 6794772480 | bytes 25427968 | tf_op jit(solution)/shard_map/rop,poc->rc/dot_general | solution.py:46
  93.7 17.8 %fusion.21 = f32[27,256,256]{2,1,0:T(8,128)S(1)} fusion(f32[640,27,256]{2,0,1:T(8,128)} %constant_dynamic-update-slice_fusion.3, f32[640,256,1]{1,0,2:T(8,128)S(1)} %bitcast.78), kind=kOutput, calls=%fused_computation.113 | convolution fusion | flops 6794772480 | bytes 25427968 | tf_op jit(solution)/shard_map/rq,rop->poq/dot_general | solution.py:91
  111.6 3.7 %copy.15 = f32[16,16,27,256]{3,1,2,0:T(8,128)} copy(f32[16,16,27,256]{3,1,0,2:T(8,128)S(1)} %bitcast.82) | data formatting | bytes 14155776 | tf_op jit(solution)/shard_map/reshape | solution.py:92
  115.2 4.7 %all-to-all-start = ((f32[16,16,27,256]{3,1,2,0:T(8,128)}), f32[16,16,27,256]{3,1,2,0:T(8,128)}, u32[]{:S(2)}, u32[]{:S(2)}) async-start(f32[16,16,27,256]{3,1,2,0:T(8,128)} %copy.15), calls=%async_computation | async-start | bytes 14155776 | tf_op jit(solution)/shard_map/all_to_all | solution.py:93
  120.6 2.2 collective-permute-start.2
  124.3 3.8 %collective-permute-start.5 = (f32[6,256]{1,0:T(8,128)S(1)}, f32[6,256]{1,0:T(8,128)S(1)}, u32[]{:S(2)}, u32[]{:S(2)}) collective-permute-start(f32[6,256]{1,0:T(8,128)S(1)} %fusion.9), channel_id=1, source_target_pairs={{0,2},{1,3},{2,0},{3,1},{4,6},{5,7},{6,4},{7,5},{8,10},{9,11},{10,... | collective-permute-start | bytes 18440 | tf_op jit(solution)/shard_map/ppermute | solution.py:59
  128.2 37.4 %collective-permute-done.5 = f32[6,256]{1,0:T(8,128)S(1)} collective-permute-done((f32[6,256]{1,0:T(8,128)S(1)}, f32[6,256]{1,0:T(8,128)S(1)}, u32[]{:S(2)}, u32[]{:S(2)}) %collective-permute-start.5) | collective-permute-done | bytes 6176 | tf_op jit(solution)/shard_map/ppermute | solution.py:59
  165.6 69.4 %collective-permute-done.6 = f32[6,256]{1,0:T(8,128)S(1)} collective-permute-done((f32[6,256]{1,0:T(8,128)S(1)}, f32[6,256]{1,0:T(8,128)S(1)}, u32[]{:S(2)}, u32[]{:S(2)}) %collective-permute-start.6) | collective-permute-done | bytes 6176 | tf_op jit(solution)/shard_map/ppermute | solution.py:59
  235.0 8.1 %collective-permute-start.7 = (f32[6,256]{1,0:T(8,128)S(1)}, f32[6,256]{1,0:T(8,128)S(1)}, u32[]{:S(2)}, u32[]{:S(2)}) collective-permute-start(f32[6,256]{1,0:T(8,128)S(1)} %add.50), channel_id=1, source_target_pairs={{0,8},{1,9},{2,10},{3,11},{4,12},{5,13},{6,14},{7,15},{8,0},{9,1},... | collective-permute-start | bytes 18440 | tf_op jit(solution)/shard_map/ppermute | solution.py:59
  243.1 36.4 %collective-permute-done.7 = f32[6,256]{1,0:T(8,128)S(1)} collective-permute-done((f32[6,256]{1,0:T(8,128)S(1)}, f32[6,256]{1,0:T(8,128)S(1)}, u32[]{:S(2)}, u32[]{:S(2)}) %collective-permute-start.7) | collective-permute-done | bytes 6176 | tf_op jit(solution)/shard_map/ppermute | solution.py:59
  282.1 4.4 %fusion.11 = (f32[2,40,8,256]{3,2,1,0:T(8,128)}, f32[2,40,8,256]{3,2,1,0:T(8,128)}, f32[2,40,8,256]{3,2,1,0:T(8,128)}, f32[2,40,8,256]{3,2,1,0:T(8,128)}, f32[2,...) fusion(f32[4,42,10,256]{3,2,1,0:T(8,128)S(1)} %select_maximum_f, ...), kind=kLoop, calls=%fused_computation.103 | loop fusion | bytes 23592960 | tf_op jit(solution)/shard_map/slice | solution.py:38
  286.6 2.1 constant_dynamic-update-slice_fusion.56
  291.7 2.1 constant_dynamic-update-slice_fusion.54
  317.8 10.6 %fusion.20 = f32[640,256,1]{1,0,2:T(8,128)S(1)} fusion(f32[640,27,256]{2,0,1:T(8,128)} %constant_dynamic-update-slice_fusion.30, f32[256,27,256]{2,0,1:T(8,128)S(1)} %bitcast.81), kind=kOutput, calls=%fused_computation.112 | convolution fusion | flops 6794772480 | bytes 25427968 | tf_op jit(solution)/shard_map/roc,qoc->rq/dot_general | solution.py:50
  329.3 4.6 %reduce_sum.36 = f32[16,27,256]{2,0,1:T(8,128)} reduce(f32[16,16,27,256]{3,1,2,0:T(8,128)} %all-to-all-done, f32[]{:T(128)} %constant.1.clone.1), dimensions={0}, to_apply=%region_0.1 | reduce | flops 1658880 | bytes 7520260 | tf_op jit(solution)/shard_map/reduce_sum | solution.py:93
  (165 shorter events, 65.0 us)
Async XLA Ops:
  7.2 72.4 %all-gather.2.cloned.1.call-start = ((), (), s32[]{:S(2)}) async-start(), calls=%async_computation.1 | async-start | bytes 7520256 | tf_op jit(solution)/shard_map/all_gather | solution.py:71
  9.0 6.7 %collective-permute-start.1 = (f32[1,40,8,256]{3,2,1,0:T(8,128)S(1)}, f32[1,40,8,256]{3,2,1,0:T(8,128)S(1)}, u32[]{:S(2)}, u32[]{:S(2)}) collective-permute-start(f32[1,40,8,256]{3,2,1,0:T(8,128)S(1)} %get-tuple-element.73), channel_id=1, source_target_pairs={{1,0},{2,1},{3,2},{4,3},{5,4},{6,5},{7,6},{8,7},{9,8},{10,9},{11,1... | collective-permute-start | bytes 983048 | tf_op jit(solution)/shard_map/ppermute | solution.py:18
  10.3 5.3 %collective-permute-start = (f32[1,40,8,256]{3,2,1,0:T(8,128)S(1)}, f32[1,40,8,256]{3,2,1,0:T(8,128)S(1)}, u32[]{:S(2)}, u32[]{:S(2)}) collective-permute-start(f32[1,40,8,256]{3,2,1,0:T(8,128)S(1)} %get-tuple-element.74), channel_id=1, source_target_pairs={{0,1},{1,2},{2,3},{3,4},{4,5},{5,6},{6,7},{7,8},{8,9},{9,10},{10,1... | collective-permute-start | bytes 983048 | tf_op jit(solution)/shard_map/ppermute | solution.py:17
  19.8 27.8 %copy-start.3 = (f32[2,40,8,256]{3,2,1,0:T(8,128)S(1)}, f32[2,40,8,256]{3,2,1,0:T(8,128)}, u32[]{:S(2)}) copy-start(f32[2,40,8,256]{3,2,1,0:T(8,128)} %param.8) | copy-start | bytes 1966084
  24.3 25.2 %copy-start.24 = (f32[2,40,8,256]{3,2,1,0:T(8,128)S(1)}, f32[2,40,8,256]{3,2,1,0:T(8,128)}, u32[]{:S(2)}) copy-start(f32[2,40,8,256]{3,2,1,0:T(8,128)} %get-tuple-element.33) | copy-start | bytes 1966084
  24.3 26.9 %copy-start.21 = (f32[2,40,8,256]{3,2,1,0:T(8,128)S(1)}, f32[2,40,8,256]{3,2,1,0:T(8,128)}, u32[]{:S(2)}) copy-start(f32[2,40,8,256]{3,2,1,0:T(8,128)} %get-tuple-element.32) | copy-start | bytes 1966084
  24.3 27.8 %copy-start.20 = (f32[2,40,8,256]{3,2,1,0:T(8,128)S(1)}, f32[2,40,8,256]{3,2,1,0:T(8,128)}, u32[]{:S(2)}) copy-start(f32[2,40,8,256]{3,2,1,0:T(8,128)} %get-tuple-element.31) | copy-start | bytes 1966084
  24.3 29.6 %copy-start.17 = (f32[2,40,8,256]{3,2,1,0:T(8,128)S(1)}, f32[2,40,8,256]{3,2,1,0:T(8,128)}, u32[]{:S(2)}) copy-start(f32[2,40,8,256]{3,2,1,0:T(8,128)} %get-tuple-element.30) | copy-start | bytes 1966084
  24.3 30.5 %copy-start.16 = (f32[2,40,8,256]{3,2,1,0:T(8,128)S(1)}, f32[2,40,8,256]{3,2,1,0:T(8,128)}, u32[]{:S(2)}) copy-start(f32[2,40,8,256]{3,2,1,0:T(8,128)} %get-tuple-element.29) | copy-start | bytes 1966084
  24.3 31.4 %copy-start.34 = (f32[2,40,8,256]{3,2,1,0:T(8,128)S(1)}, f32[2,40,8,256]{3,2,1,0:T(8,128)}, u32[]{:S(2)}) copy-start(f32[2,40,8,256]{3,2,1,0:T(8,128)} %get-tuple-element.70) | copy-start | bytes 1966084
  24.4 32.3 %copy-start.13 = (f32[2,40,8,256]{3,2,1,0:T(8,128)S(1)}, f32[2,40,8,256]{3,2,1,0:T(8,128)}, u32[]{:S(2)}) copy-start(f32[2,40,8,256]{3,2,1,0:T(8,128)} %get-tuple-element.28) | copy-start | bytes 1966084
  26.5 31.0 %copy-start.12 = (f32[2,40,8,256]{3,2,1,0:T(8,128)S(1)}, f32[2,40,8,256]{3,2,1,0:T(8,128)}, u32[]{:S(2)}) copy-start(f32[2,40,8,256]{3,2,1,0:T(8,128)} %get-tuple-element.27) | copy-start | bytes 1966084
  29.2 30.1 %copy-start.9 = (f32[2,40,8,256]{3,2,1,0:T(8,128)S(1)}, f32[2,40,8,256]{3,2,1,0:T(8,128)}, u32[]{:S(2)}) copy-start(f32[2,40,8,256]{3,2,1,0:T(8,128)} %get-tuple-element.26) | copy-start | bytes 1966084
  55.7 37.6 %copy-start.32 = (f32[2,40,8,256]{3,2,1,0:T(8,128)S(1)}, f32[2,40,8,256]{3,2,1,0:T(8,128)}, u32[]{:S(2)}) copy-start(f32[2,40,8,256]{3,2,1,0:T(8,128)} %param.9) | copy-start | bytes 1966084
  55.7 37.6 %copy-start.36 = (f32[256]{0:T(256)S(1)}, f32[256]{0:T(256)}, u32[]{:S(2)}) copy-start(f32[256]{0:T(256)} %param.11) | copy-start | bytes 3076
  115.2 214.1 %all-to-all-start = ((f32[16,16,27,256]{3,1,2,0:T(8,128)}), f32[16,16,27,256]{3,1,2,0:T(8,128)}, u32[]{:S(2)}, u32[]{:S(2)}) async-start(f32[16,16,27,256]{3,1,2,0:T(8,128)} %copy.15), calls=%async_computation | async-start | bytes 14155776 | tf_op jit(solution)/shard_map/all_to_all | solution.py:93
  120.2 4.1 %collective-permute-start.4 = (f32[6,256]{1,0:T(8,128)S(1)}, f32[6,256]{1,0:T(8,128)S(1)}, u32[]{:S(2)}, u32[]{:S(2)}) collective-permute-start(f32[6,256]{1,0:T(8,128)S(1)} %pad_maximum_fusion.10), channel_id=1, source_target_pairs={{0,1},{1,0},{2,3},{3,2},{4,5},{5,4},{6,7},{7,6},{8,9},{9,8},{10,11... | collective-permute-start | bytes 18440 | tf_op jit(solution)/shard_map/ppermute | solution.py:59
  120.6 160.1 %collective-permute-start.2 = (f32[1,40,8,256]{3,2,1,0:T(8,128)S(1)}, f32[1,40,8,256]{3,2,1,0:T(8,128)S(1)}, u32[]{:S(2)}, u32[]{:S(2)}) collective-permute-start(f32[1,40,8,256]{3,2,1,0:T(8,128)S(1)} %get-tuple-element.68), channel_id=1, source_target_pairs={{0,1},{1,2},{2,3},{3,4},{4,5},{5,6},{6,7},{7,8},{8,9},{9,10},{10,1... | collective-permute-start | bytes 983048 | tf_op jit(solution)/shard_map/ppermute | solution.py:17
  122.8 157.9 %collective-permute-start.3 = (f32[1,40,8,256]{3,2,1,0:T(8,128)S(1)}, f32[1,40,8,256]{3,2,1,0:T(8,128)S(1)}, u32[]{:S(2)}, u32[]{:S(2)}) collective-permute-start(f32[1,40,8,256]{3,2,1,0:T(8,128)S(1)} %get-tuple-element.69), channel_id=1, source_target_pairs={{1,0},{2,1},{3,2},{4,3},{5,4},{6,5},{7,6},{8,7},{9,8},{10,9},{11,1... | collective-permute-start | bytes 983048 | tf_op jit(solution)/shard_map/ppermute | solution.py:18
  124.3 41.2 %collective-permute-start.5 = (f32[6,256]{1,0:T(8,128)S(1)}, f32[6,256]{1,0:T(8,128)S(1)}, u32[]{:S(2)}, u32[]{:S(2)}) collective-permute-start(f32[6,256]{1,0:T(8,128)S(1)} %fusion.9), channel_id=1, source_target_pairs={{0,2},{1,3},{2,0},{3,1},{4,6},{5,7},{6,4},{7,5},{8,10},{9,11},{10,... | collective-permute-start | bytes 18440 | tf_op jit(solution)/shard_map/ppermute | solution.py:59
  165.6 69.4 %collective-permute-start.6 = (f32[6,256]{1,0:T(8,128)S(1)}, f32[6,256]{1,0:T(8,128)S(1)}, u32[]{:S(2)}, u32[]{:S(2)}) collective-permute-start(f32[6,256]{1,0:T(8,128)S(1)} %add.49), channel_id=1, source_target_pairs={{0,4},{1,5},{2,6},{3,7},{4,0},{5,1},{6,2},{7,3},{8,12},{9,13},{10,... | collective-permute-start | bytes 18440 | tf_op jit(solution)/shard_map/ppermute | solution.py:59
  235.0 44.6 %collective-permute-start.7 = (f32[6,256]{1,0:T(8,128)S(1)}, f32[6,256]{1,0:T(8,128)S(1)}, u32[]{:S(2)}, u32[]{:S(2)}) collective-permute-start(f32[6,256]{1,0:T(8,128)S(1)} %add.50), channel_id=1, source_target_pairs={{0,8},{1,9},{2,10},{3,11},{4,12},{5,13},{6,14},{7,15},{8,0},{9,1},... | collective-permute-start | bytes 18440 | tf_op jit(solution)/shard_map/ppermute | solution.py:59
  290.8 26.1 %copy-start.6 = (f32[2,40,8,256]{3,2,1,0:T(8,128)S(1)}, f32[2,40,8,256]{3,2,1,0:T(8,128)}, u32[]{:S(2)}) copy-start(f32[2,40,8,256]{3,2,1,0:T(8,128)} %get-tuple-element.8) | copy-start | bytes 1966084
  291.7 26.1 %slice-start = ((s8[7077888]{0:T(1024)(128)(4,1)}), s8[4194304]{0:T(1024)(128)(4,1)S(1)}, s32[]{:S(2)}) async-start(s8[7077888]{0:T(1024)(128)(4,1)} %bitcast.80), calls=%async_computation.2 | async-start | bytes 8388608
  (26 other events, 391.6 us)
Sparse Core Ops, SparseCore 0:
  10.2 69.3 all-gather.1

commit v6 on v4

--- a/solution.py
+++ b/solution.py
@@ -88,11 +88,12 @@
     sums = all_sum(jnp.concatenate([local_bias[None], local_land[None], local_gain], axis=0))
     delta_flat = delta.reshape(-1, chans)
     grad_weight = lax.psum_scatter(
-        jnp.einsum("rq,rop->poq", delta_flat, table_pre, precision=high),
+        jnp.einsum("rq,rop->opq", delta_flat, table_pre, precision=high),
         "space",
-        scatter_dimension=0,
+        scatter_dimension=1,
         tiled=True,
     )
+    grad_weight = jnp.transpose(grad_weight, (1, 0, 2))
     return (grad_field, grad_weight, sums[0], sums[1], sums[2 : 2 + local_gain.shape[0]])
 
 

time: 209 us -> 209 us (level)
  no operation moved by 1% of the time
where the time goes in v6:
time: 209 us
  local copies, waits for them, and re-layouts  74.8 us (36%)
  waiting for transfers between devices  45.4 us (22%)
  matrix products  45.1 us (22%)
  starting transfers between devices  16.6 us (8%)
  between operations  14.5 us (7%)
  other arithmetic  12.4 us (6%)
    unnamed x133, local copies, waits for them, and re-layouts  61.3 us
    dot_general x1, matrix products, per_device(): jnp.einsum('rq,rop->opq', delta_flat, table_pre, precision=high)  19.6 us
    all_gather x1, waiting for transfers between devices, per_device(): full_weight = lax.all_gather(weight, 'space', axis=0, tiled=True)  19.1 us
    reduce_scatter x1, waiting for transfers between devices, per_device(): lax.psum_scatter(jnp.einsum('rq,rop->opq', delta_flat, table_pre, precisi...  17.1 us
    dot_general x1, matrix products, conv_piece(): return jnp.einsum('rop,poc->rc', table, piece, precision=high)  13.7 us
    dot_general x1, matrix products, back_piece(): return jnp.einsum('roc,qoc->rq', table, piece, precision=high)  10.7 us
    slice x3, local copies, waits for them, and re-layouts, window_table(): grid[lat_off:lat_off + out_rows, lon_off:lon_off + lon_n, lev_off:lev_off...  9.27 us
    ppermute x4, waiting for transfers between devices, all_sum(): x = x + lax.ppermute(x, 'space', [(i, i ^ bit) for i in range(count)])  8.53 us
  transfers between devices with their start and end apart: 10, of which 5 were waited for; matrix products, arithmetic and copies ran while one was open for 46% of the time, Pallas kernels for 0%

profile of v6, /device:TPU:0, one launch (start us, length us, event | category | flops | bytes accessed | tf_op | source)
XLA Modules:
  0.0 208.8 jit_solution(12286144815160069324)
XLA Ops:
  10.4 3.1 %collective-permute-start = (f32[1,40,8,256]{3,2,1,0:T(8,128)S(1)}, f32[1,40,8,256]{3,2,1,0:T(8,128)S(1)}, u32[]{:S(2)}, u32[]{:S(2)}) collective-permute-start(f32[1,40,8,256]{3,2,1,0:T(8,128)S(1)} %get-tuple-element.74), channel_id=1, source_target_pairs={{0,1},{1,2},{2,3},{3,4},{4,5},{5,6},{6,7},{7,8},{8,9},{9,10},{10,1... | collective-permute-start | bytes 983048 | tf_op jit(solution)/shard_map/ppermute | solution.py:17
  15.8 2.6 %pad_maximum_fusion.4 = (f32[2,40,8,256]{3,2,1,0:T(8,128)}, f32[4,40,8,256]{3,2,1,0:T(8,128)S(1)}, f32[2,40,8,256]{3,2,1,0:T(8,128)}) fusion(f32[1,40,8,256]{3,2,1,0:T(8,128)S(1)} %collective-permute-done.1, f32[2,40,8,256]{3,2,1,0:T(8,128)} %param.8, f32[4,40,8,256]{3,2,1,0:T(8,128)S(1)} %constant_dynamic-update-slice_fusion.2, ...), kind=kLoop, calls=%fused_computation.26 | loop fusion | flops 327680 | bytes 3276800 | tf_op jit(solution)/shard_map/concatenate | solution.py:19
  20.0 4.5 %fusion.12 = (f32[2,40,8,256]{3,2,1,0:T(8,128)}, f32[2,40,8,256]{3,2,1,0:T(8,128)}, f32[2,40,8,256]{3,2,1,0:T(8,128)}, f32[2,40,8,256]{3,2,1,0:T(8,128)}, f32[2,...) fusion(f32[4,42,10,256]{3,2,1,0:T(8,128)S(1)} %select_maximum_f, ...), kind=kLoop, calls=%fused_computation.104 | loop fusion | bytes 23592960 | tf_op jit(solution)/shard_map/slice | solution.py:38
  24.6 2.1 %constant_dynamic-update-slice_fusion.29 = f32[640,27,256]{2,0,1:T(8,128)} fusion(f32[640,1,256]{2,0,1:T(8,128)} %bitcast.117), kind=kLoop, calls=%fused_computation.63 | loop fusion | bytes 1310720
  26.7 2.7 %pad_maximum_fusion.3 = (f32[2,40,8,256]{3,2,1,0:T(8,128)S(1)}, f32[2,40,8,256]{3,2,1,0:T(8,128)S(1)}, f32[2,40,8,256]{3,2,1,0:T(8,128)S(1)}, f32[2,40,8,256]{3,...) fusion(f32[4,1,8,256]{3,2,1,0:T(8,128)} %copy-done.35, f32[4,40,8,256]{3,2,1,0:T(8,128)} %copy-done.2, ...), kind=kLoop, calls=%fused_computation.25 | loop fusion | flops 983040 | bytes 5308416 | tf_op jit(solution)/shard_map/concatenate | solution.py:24
  30.3 2.0 constant_dynamic-update-slice_fusion.27
  32.2 2.0 constant_dynamic-update-slice_fusion.26
  38.2 2.0 constant_dynamic-update-slice_fusion.23
  43.0 2.1 %constant_dynamic-update-slice_fusion.20 = f32[640,27,256]{2,0,1:T(8,128)} fusion(f32[640,27,256]{2,0,1:T(8,128)} %constant_dynamic-update-slice_fusion.21, f32[640,1,256]{2,0,1:T(8,128)} %bitcast.109), kind=kLoop, calls=%fused_computation.54 | loop fusion | bytes 1310720
  60.5 19.1 %all-gather.2.cloned.1.call-done = f32[256,27,256]{2,0,1:T(8,128)} async-done(((f32[16,27,256]{2,0,1:T(8,128)}), f32[256,27,256]{2,0,1:T(8,128)}) %all-gather.2.cloned.1.call-update) | async-done | bytes 7077904 | tf_op jit(solution)/shard_map/all_gather | solution.py:71
  79.6 13.7 %fusion.19 = f32[640,256,1]{1,0,2:T(8,128)S(1)} fusion(f32[640,27,256]{2,0,1:T(8,128)} %constant_dynamic-update-slice_fusion.3, f32[256,27,256]{2,0,1:T(8,128)} %all-gather.2.cloned.1.call-done), kind=kOutput, calls=%fused_computation.111 | convolution fusion | flops 6794772480 | bytes 25427968 | tf_op jit(solution)/shard_map/rop,poc->rc/dot_general | solution.py:46
  93.8 19.6 %fusion.21 = f32[27,256,256]{2,1,0:T(8,128)} fusion(f32[640,27,256]{2,0,1:T(8,128)} %constant_dynamic-update-slice_fusion.3, f32[640,256,1]{1,0,2:T(8,128)S(1)} %bitcast.76), kind=kOutput, calls=%fused_computation.113 | convolution fusion | flops 6794772480 | bytes 25427968 | tf_op jit(solution)/shard_map/rq,rop->opq/dot_general | solution.py:91
  114.0 2.2 %collective-permute-start.2 = (f32[1,40,8,256]{3,2,1,0:T(8,128)S(1)}, f32[1,40,8,256]{3,2,1,0:T(8,128)S(1)}, u32[]{:S(2)}, u32[]{:S(2)}) collective-permute-start(f32[1,40,8,256]{3,2,1,0:T(8,128)S(1)} %get-tuple-element.68), channel_id=1, source_target_pairs={{0,1},{1,2},{2,3},{3,4},{4,5},{5,6},{6,7},{7,8},{8,9},{9,10},{10,1... | collective-permute-start | bytes 983048 | tf_op jit(solution)/shard_map/ppermute | solution.py:17
  117.8 2.7 %collective-permute-start.5 = (f32[6,256]{1,0:T(8,128)S(1)}, f32[6,256]{1,0:T(8,128)S(1)}, u32[]{:S(2)}, u32[]{:S(2)}) collective-permute-start(f32[6,256]{1,0:T(8,128)S(1)} %fusion.9), channel_id=1, source_target_pairs={{0,2},{1,3},{2,0},{3,1},{4,6},{5,7},{6,4},{7,5},{8,10},{9,11},{10,... | collective-permute-start | bytes 18440 | tf_op jit(solution)/shard_map/ppermute | solution.py:59
  120.5 4.9 %collective-permute-done.5 = f32[6,256]{1,0:T(8,128)S(1)} collective-permute-done((f32[6,256]{1,0:T(8,128)S(1)}, f32[6,256]{1,0:T(8,128)S(1)}, u32[]{:S(2)}, u32[]{:S(2)}) %collective-permute-start.5) | collective-permute-done | bytes 6176 | tf_op jit(solution)/shard_map/ppermute | solution.py:59
  125.4 2.9 %collective-permute-start.6 = (f32[6,256]{1,0:T(8,128)S(1)}, f32[6,256]{1,0:T(8,128)S(1)}, u32[]{:S(2)}, u32[]{:S(2)}) collective-permute-start(f32[6,256]{1,0:T(8,128)S(1)} %add.51), channel_id=1, source_target_pairs={{0,4},{1,5},{2,6},{3,7},{4,0},{5,1},{6,2},{7,3},{8,12},{9,13},{10,... | collective-permute-start | bytes 18440 | tf_op jit(solution)/shard_map/ppermute | solution.py:59
  129.9 2.5 %collective-permute-start.7 = (f32[6,256]{1,0:T(8,128)S(1)}, f32[6,256]{1,0:T(8,128)S(1)}, u32[]{:S(2)}, u32[]{:S(2)}) collective-permute-start(f32[6,256]{1,0:T(8,128)S(1)} %add.52), channel_id=1, source_target_pairs={{0,8},{1,9},{2,10},{3,11},{4,12},{5,13},{6,14},{7,15},{8,0},{9,1},... | collective-permute-start | bytes 18440 | tf_op jit(solution)/shard_map/ppermute | solution.py:59
  132.5 2.0 collective-permute-done.7
  137.1 4.4 %fusion.11 = (f32[2,40,8,256]{3,2,1,0:T(8,128)}, f32[2,40,8,256]{3,2,1,0:T(8,128)}, f32[2,40,8,256]{3,2,1,0:T(8,128)}, f32[2,40,8,256]{3,2,1,0:T(8,128)}, f32[2,...) fusion(f32[4,42,10,256]{3,2,1,0:T(8,128)S(1)} %select_maximum_f, ...), kind=kLoop, calls=%fused_computation.103 | loop fusion | bytes 23592960 | tf_op jit(solution)/shard_map/slice | solution.py:38
  141.6 2.2 %constant_dynamic-update-slice_fusion.56 = f32[640,27,256]{2,0,1:T(8,128)} fusion(f32[640,1,256]{2,0,1:T(8,128)} %bitcast.118), kind=kLoop, calls=%fused_computation.90 | loop fusion | bytes 1310720
  147.1 2.1 %constant_dynamic-update-slice_fusion.54 = f32[640,27,256]{2,0,1:T(8,128)} fusion(f32[640,27,256]{2,0,1:T(8,128)} %constant_dynamic-update-slice_fusion.55, f32[640,1,256]{2,0,1:T(8,128)} %bitcast.114), kind=kLoop, calls=%fused_computation.88 | loop fusion | bytes 1310720
  149.2 2.0 constant_dynamic-update-slice_fusion.53
  173.2 10.7 %fusion.20 = f32[640,256,1]{1,0,2:T(8,128)S(1)} fusion(f32[640,27,256]{2,0,1:T(8,128)} %constant_dynamic-update-slice_fusion.30, f32[256,27,256]{2,0,1:T(8,128)S(1)} %bitcast.79), kind=kOutput, calls=%fused_computation.112 | convolution fusion | flops 6794772480 | bytes 25427968 | tf_op jit(solution)/shard_map/roc,qoc->rq/dot_general | solution.py:50
  184.8 17.1 %reduce-scatter.2.cloned.1.call-done = f32[27,16,256]{2,1,0:T(8,128)} async-done(((f32[27,256,256]{2,1,0:T(8,128)}), f32[27,16,256]{2,1,0:T(8,128)}) %reduce-scatter.2.cloned.1.call-update) | async-done | bytes 442384 | tf_op jit(solution)/shard_map/reduce_scatter | solution.py:90
  (164 shorter events, 63.1 us)
Async XLA Ops:
  7.2 72.4 %all-gather.2.cloned.1.call-start = ((), (), s32[]{:S(2)}) async-start(), calls=%async_computation.1 | async-start | bytes 7520256 | tf_op jit(solution)/shard_map/all_gather | solution.py:71
  7.9 194.0 %reduce-scatter.2.cloned.1.call-start = ((), (), s32[]{:S(2)}) async-start(), calls=%async_computation.2 | async-start | bytes 7520256 | tf_op jit(solution)/shard_map/reduce_scatter | solution.py:90
  9.1 6.7 %collective-permute-start.1 = (f32[1,40,8,256]{3,2,1,0:T(8,128)S(1)}, f32[1,40,8,256]{3,2,1,0:T(8,128)S(1)}, u32[]{:S(2)}, u32[]{:S(2)}) collective-permute-start(f32[1,40,8,256]{3,2,1,0:T(8,128)S(1)} %get-tuple-element.73), channel_id=1, source_target_pairs={{1,0},{2,1},{3,2},{4,3},{5,4},{6,5},{7,6},{8,7},{9,8},{10,9},{11,1... | collective-permute-start | bytes 983048 | tf_op jit(solution)/shard_map/ppermute | solution.py:18
  10.4 5.4 %collective-permute-start = (f32[1,40,8,256]{3,2,1,0:T(8,128)S(1)}, f32[1,40,8,256]{3,2,1,0:T(8,128)S(1)}, u32[]{:S(2)}, u32[]{:S(2)}) collective-permute-start(f32[1,40,8,256]{3,2,1,0:T(8,128)S(1)} %get-tuple-element.74), channel_id=1, source_target_pairs={{0,1},{1,2},{2,3},{3,4},{4,5},{5,6},{6,7},{7,8},{8,9},{9,10},{10,1... | collective-permute-start | bytes 983048 | tf_op jit(solution)/shard_map/ppermute | solution.py:17
  20.0 28.0 %copy-start.3 = (f32[2,40,8,256]{3,2,1,0:T(8,128)S(1)}, f32[2,40,8,256]{3,2,1,0:T(8,128)}, u32[]{:S(2)}) copy-start(f32[2,40,8,256]{3,2,1,0:T(8,128)} %param.8) | copy-start | bytes 1966084
  24.5 27.0 %copy-start.21 = (f32[2,40,8,256]{3,2,1,0:T(8,128)S(1)}, f32[2,40,8,256]{3,2,1,0:T(8,128)}, u32[]{:S(2)}) copy-start(f32[2,40,8,256]{3,2,1,0:T(8,128)} %get-tuple-element.32) | copy-start | bytes 1966084
  24.5 27.9 %copy-start.20 = (f32[2,40,8,256]{3,2,1,0:T(8,128)S(1)}, f32[2,40,8,256]{3,2,1,0:T(8,128)}, u32[]{:S(2)}) copy-start(f32[2,40,8,256]{3,2,1,0:T(8,128)} %get-tuple-element.31) | copy-start | bytes 1966084
  24.5 29.7 %copy-start.17 = (f32[2,40,8,256]{3,2,1,0:T(8,128)S(1)}, f32[2,40,8,256]{3,2,1,0:T(8,128)}, u32[]{:S(2)}) copy-start(f32[2,40,8,256]{3,2,1,0:T(8,128)} %get-tuple-element.30) | copy-start | bytes 1966084
  24.5 30.6 %copy-start.16 = (f32[2,40,8,256]{3,2,1,0:T(8,128)S(1)}, f32[2,40,8,256]{3,2,1,0:T(8,128)}, u32[]{:S(2)}) copy-start(f32[2,40,8,256]{3,2,1,0:T(8,128)} %get-tuple-element.29) | copy-start | bytes 1966084
  24.5 31.5 %copy-start.34 = (f32[2,40,8,256]{3,2,1,0:T(8,128)S(1)}, f32[2,40,8,256]{3,2,1,0:T(8,128)}, u32[]{:S(2)}) copy-start(f32[2,40,8,256]{3,2,1,0:T(8,128)} %get-tuple-element.70) | copy-start | bytes 1966084
  24.5 32.4 %copy-start.13 = (f32[2,40,8,256]{3,2,1,0:T(8,128)S(1)}, f32[2,40,8,256]{3,2,1,0:T(8,128)}, u32[]{:S(2)}) copy-start(f32[2,40,8,256]{3,2,1,0:T(8,128)} %get-tuple-element.28) | copy-start | bytes 1966084
  26.7 31.1 %copy-start.12 = (f32[2,40,8,256]{3,2,1,0:T(8,128)S(1)}, f32[2,40,8,256]{3,2,1,0:T(8,128)}, u32[]{:S(2)}) copy-start(f32[2,40,8,256]{3,2,1,0:T(8,128)} %get-tuple-element.27) | copy-start | bytes 1966084
  29.4 30.2 %copy-start.9 = (f32[2,40,8,256]{3,2,1,0:T(8,128)S(1)}, f32[2,40,8,256]{3,2,1,0:T(8,128)}, u32[]{:S(2)}) copy-start(f32[2,40,8,256]{3,2,1,0:T(8,128)} %get-tuple-element.26) | copy-start | bytes 1966084
  56.0 37.3 %copy-start.32 = (f32[2,40,8,256]{3,2,1,0:T(8,128)S(1)}, f32[2,40,8,256]{3,2,1,0:T(8,128)}, u32[]{:S(2)}) copy-start(f32[2,40,8,256]{3,2,1,0:T(8,128)} %param.9) | copy-start | bytes 1966084
  56.0 37.3 %copy-start.36 = (f32[256]{0:T(256)S(1)}, f32[256]{0:T(256)}, u32[]{:S(2)}) copy-start(f32[256]{0:T(256)} %param.11) | copy-start | bytes 3076
  113.7 4.1 %collective-permute-start.4 = (f32[6,256]{1,0:T(8,128)S(1)}, f32[6,256]{1,0:T(8,128)S(1)}, u32[]{:S(2)}, u32[]{:S(2)}) collective-permute-start(f32[6,256]{1,0:T(8,128)S(1)} %pad_maximum_fusion.10), channel_id=1, source_target_pairs={{0,1},{1,0},{2,3},{3,2},{4,5},{5,4},{6,7},{7,6},{8,9},{9,8},{10,11... | collective-permute-start | bytes 18440 | tf_op jit(solution)/shard_map/ppermute | solution.py:59
  114.0 21.6 %collective-permute-start.2 = (f32[1,40,8,256]{3,2,1,0:T(8,128)S(1)}, f32[1,40,8,256]{3,2,1,0:T(8,128)S(1)}, u32[]{:S(2)}, u32[]{:S(2)}) collective-permute-start(f32[1,40,8,256]{3,2,1,0:T(8,128)S(1)} %get-tuple-element.68), channel_id=1, source_target_pairs={{0,1},{1,2},{2,3},{3,4},{4,5},{5,6},{6,7},{7,8},{8,9},{9,10},{10,1... | collective-permute-start | bytes 983048 | tf_op jit(solution)/shard_map/ppermute | solution.py:17
  116.2 19.4 %collective-permute-start.3 = (f32[1,40,8,256]{3,2,1,0:T(8,128)S(1)}, f32[1,40,8,256]{3,2,1,0:T(8,128)S(1)}, u32[]{:S(2)}, u32[]{:S(2)}) collective-permute-start(f32[1,40,8,256]{3,2,1,0:T(8,128)S(1)} %get-tuple-element.69), channel_id=1, source_target_pairs={{1,0},{2,1},{3,2},{4,3},{5,4},{6,5},{7,6},{8,7},{9,8},{10,9},{11,1... | collective-permute-start | bytes 983048 | tf_op jit(solution)/shard_map/ppermute | solution.py:18
  117.8 7.6 %collective-permute-start.5 = (f32[6,256]{1,0:T(8,128)S(1)}, f32[6,256]{1,0:T(8,128)S(1)}, u32[]{:S(2)}, u32[]{:S(2)}) collective-permute-start(f32[6,256]{1,0:T(8,128)S(1)} %fusion.9), channel_id=1, source_target_pairs={{0,2},{1,3},{2,0},{3,1},{4,6},{5,7},{6,4},{7,5},{8,10},{9,11},{10,... | collective-permute-start | bytes 18440 | tf_op jit(solution)/shard_map/ppermute | solution.py:59
  125.4 4.5 %collective-permute-start.6 = (f32[6,256]{1,0:T(8,128)S(1)}, f32[6,256]{1,0:T(8,128)S(1)}, u32[]{:S(2)}, u32[]{:S(2)}) collective-permute-start(f32[6,256]{1,0:T(8,128)S(1)} %add.51), channel_id=1, source_target_pairs={{0,4},{1,5},{2,6},{3,7},{4,0},{5,1},{6,2},{7,3},{8,12},{9,13},{10,... | collective-permute-start | bytes 18440 | tf_op jit(solution)/shard_map/ppermute | solution.py:59
  129.9 4.5 %collective-permute-start.7 = (f32[6,256]{1,0:T(8,128)S(1)}, f32[6,256]{1,0:T(8,128)S(1)}, u32[]{:S(2)}, u32[]{:S(2)}) collective-permute-start(f32[6,256]{1,0:T(8,128)S(1)} %add.52), channel_id=1, source_target_pairs={{0,8},{1,9},{2,10},{3,11},{4,12},{5,13},{6,14},{7,15},{8,0},{9,1},... | collective-permute-start | bytes 18440 | tf_op jit(solution)/shard_map/ppermute | solution.py:59
  146.2 26.1 %copy-start.6 = (f32[2,40,8,256]{3,2,1,0:T(8,128)S(1)}, f32[2,40,8,256]{3,2,1,0:T(8,128)}, u32[]{:S(2)}) copy-start(f32[2,40,8,256]{3,2,1,0:T(8,128)} %get-tuple-element.8) | copy-start | bytes 1966084
  147.1 26.1 %slice-start = ((s8[7077888]{0:T(1024)(128)(4,1)}), s8[4194304]{0:T(1024)(128)(4,1)S(1)}, s32[]{:S(2)}) async-start(s8[7077888]{0:T(1024)(128)(4,1)} %bitcast.78), calls=%async_computation.3 | async-start | bytes 8388608
  169.6 32.4 %copy-start.1 = (f32[4,256]{1,0:T(4,128)S(1)}, f32[4,256]{1,0:T(4,128)}, u32[]{:S(2)}) copy-start(f32[4,256]{1,0:T(4,128)} %param.13) | copy-start | bytes 12292
  (26 other events, 416.2 us)
Sparse Core Ops, SparseCore 0:
  10.2 69.3 all-gather.1
  113.5 88.4 reduce-scatter.1

commit v7 on v6

--- a/solution.py
+++ b/solution.py
@@ -61,6 +61,17 @@
     return x
 
 
+def split_bf16(x):
+    hi = lax.reduce_precision(x, exponent_bits=8, mantissa_bits=7)
+    return hi.astype(jnp.bfloat16), (x - hi).astype(jnp.bfloat16)
+
+
+def dot3(spec, a_parts, b_parts):
+    (a_hi, a_lo), (b_hi, b_lo) = a_parts, b_parts
+    part = lambda x, y: jnp.einsum(spec, x, y, preferred_element_type=jnp.float32)
+    return part(a_hi, b_hi) + (part(a_hi, b_lo) + part(a_lo, b_hi))
+
+
 def per_device(field, grad_out, weight, bias, land_bias, level_gain, land_mask, level_index):
     rows, lon_n, lev_n, chans = field.shape
     land_float = land_mask.astype(jnp.float32)
@@ -70,8 +81,9 @@
     gains = jnp.dot(one_hot, level_gain, precision=highest)
     full_weight = lax.all_gather(weight, "space", axis=0, tiled=True)
     grid_pre = wrap_levels(with_halo(field, (("space", 0),), 1))
-    table_pre = window_table(grid_pre, rows, False)
-    conv = conv_piece(table_pre, full_weight)
+    grid_hi, grid_lo = split_bf16(grid_pre)
+    table_pre = (window_table(grid_hi, rows, False), window_table(grid_lo, rows, False))
+    conv = dot3("rop,poc->rc", table_pre, split_bf16(full_weight))
     conv = conv.reshape(rows, lon_n, lev_n, chans)
     pre = conv + bias + land_float[:, :, None, None] * land_bias
     sigma = jax.nn.sigmoid(pre)
@@ -88,7 +100,7 @@
     sums = all_sum(jnp.concatenate([local_bias[None], local_land[None], local_gain], axis=0))
     delta_flat = delta.reshape(-1, chans)
     grad_weight = lax.psum_scatter(
-        jnp.einsum("rq,rop->opq", delta_flat, table_pre, precision=high),
+        dot3("rq,rop->opq", split_bf16(delta_flat), table_pre),
         "space",
         scatter_dimension=1,
         tiled=True,

time: 209 us -> 215 us (1.029)
  waiting for transfers between devices: 45.4 us -> 68.8 us
  local copies, waits for them, and re-layouts: 74.8 us -> 58.9 us
  other arithmetic: 12.4 us -> 5.95 us
  matrix products: 45.1 us -> 50.6 us
    all_gather x1, waiting for transfers between devices: 19.1 us -> 37.3 us  [per_device(): full_weight = lax.all_gather(weight, 'space', axis=0, tiled=True)]
    unnamed x133 -> x148, local copies, waits for them, and re-layouts: 61.3 us -> 48 us
    dot_general x2 -> x6, matrix products: 33.3 us -> 39.1 us  [dot3(): jnp.einsum(spec, x, y, preferred_element_type=jnp.float32)]
    reduce_scatter x1, waiting for transfers between devices: 17.1 us -> 21.3 us  [per_device(): lax.psum_scatter(dot3('rq,rop->opq', split_bf16(delta_flat), table_pre),...]
    concatenate x2 -> x1, other arithmetic: 3.87 us -> 0.11 us  [with_halo(): array = jnp.concatenate([before, array, after], axis=dim)]
    concatenate x4 -> x2, other arithmetic: 5.67 us -> 2.17 us  [wrap_levels(): wrapped = jnp.concatenate([field[:, -1:], field, field[:, :1]], axis=1)]
    slice x3 -> x6, local copies, waits for them, and re-layouts: 9.27 us -> 6.78 us  [window_table(): grid[lat_off:lat_off + out_rows, lon_off:lon_off + lon_n, lev_off:lev_off...]
  transfers between devices with their start and end apart: 10 -> 10, of which waited for: 5 -> 6; matrix products, arithmetic and copies ran while one was open for 46% -> 35% of each run, Pallas kernels for 0% -> 0%
where the time goes in v7:
time: 215 us
  waiting for transfers between devices  68.8 us (32%)
  local copies, waits for them, and re-layouts  58.9 us (27%)
  matrix products  50.6 us (24%)
  starting transfers between devices  15.9 us (7%)
  between operations  14.7 us (7%)
  other arithmetic  5.95 us (3%)
    unnamed x148, local copies, waits for them, and re-layouts  48 us
    dot_general x6, matrix products, dot3(): jnp.einsum(spec, x, y, preferred_element_type=jnp.float32)  39.1 us
    all_gather x1, waiting for transfers between devices, per_device(): full_weight = lax.all_gather(weight, 'space', axis=0, tiled=True)  37.3 us
    reduce_scatter x1, waiting for transfers between devices, per_device(): lax.psum_scatter(dot3('rq,rop->opq', split_bf16(delta_flat), table_pre),...  21.3 us
    dot_general x1, matrix products, back_piece(): return jnp.einsum('roc,qoc->rq', table, piece, precision=high)  10.5 us
    ppermute x4, waiting for transfers between devices, all_sum(): x = x + lax.ppermute(x, 'space', [(i, i ^ bit) for i in range(count)])  8.53 us
    ppermute x4, starting transfers between devices, all_sum(): x = x + lax.ppermute(x, 'space', [(i, i ^ bit) for i in range(count)])  8.5 us
    slice x6, local copies, waits for them, and re-layouts, window_table(): grid[lat_off:lat_off + out_rows, lon_off:lon_off + lon_n, lev_off:lev_off...  6.78 us
  transfers between devices with their start and end apart: 10, of which 6 were waited for; matrix products, arithmetic and copies ran while one was open for 35% of the time, Pallas kernels for 0%

profile of v7, /device:TPU:0, one launch (start us, length us, event | category | flops | bytes accessed | tf_op | source)
XLA Modules:
  0.0 214.9 jit_solution(11551516118335637928)
XLA Ops:
  9.1 2.4 %collective-permute-start = (f32[1,40,8,256]{3,2,1,0:T(8,128)S(1)}, f32[1,40,8,256]{3,2,1,0:T(8,128)S(1)}, u32[]{:S(2)}, u32[]{:S(2)}) collective-permute-start(f32[1,40,8,256]{3,2,1,0:T(8,128)S(1)} %get-tuple-element.102), channel_id=1, source_target_pairs={{0,1},{1,2},{2,3},{3,4},{4,5},{5,6},{6,7},{7,8},{8,9},{9,10},{10,1... | collective-permute-start | bytes 983048 | tf_op jit(solution)/shard_map/ppermute | solution.py:17
  11.5 1.3 collective-permute-start.1
  21.5 1.2 constant_dynamic-update-slice_fusion.27
  22.8 1.4 constant_dynamic-update-slice_fusion.26
  42.2 37.3 %all-gather.2.cloned.1.call-done = f32[256,27,256]{2,0,1:T(8,128)} async-done(((f32[16,27,256]{2,0,1:T(8,128)}), f32[256,27,256]{2,0,1:T(8,128)}) %all-gather.2.cloned.1.call-update) | async-done | bytes 7077904 | tf_op jit(solution)/shard_map/all_gather | solution.py:82
  79.6 8.1 %fusion.8 = f32[640,256]{1,0:T(8,128)S(1)} fusion(bf16[640,27,256]{2,0,1:T(8,128)(2,1)} %copy-done.3, f32[256,27,256]{2,0,1:T(8,128)} %all-gather.2.cloned.1.call-done), kind=kOutput, calls=%fused_computation.22 | convolution fusion | flops 2268463104 | bytes 16580608 | tf_op jit(solution)/shard_map/rop,poc->rc/dot_general | solution.py:71
  87.7 6.2 %fusion.7 = f32[640,256]{1,0:T(8,128)S(1)} fusion(bf16[640,27,256]{2,0,1:T(8,128)(2,1)} %constant_dynamic-update-slice_fusion.3, f32[256,27,256]{2,0,1:T(8,128)S(1)} %copy-done.2), kind=kOutput, calls=%fused_computation.21 | convolution fusion | flops 2268463104 | bytes 16580608 | tf_op jit(solution)/shard_map/rop,poc->rc/dot_general | solution.py:71
  94.0 6.2 %fusion.15 = f32[640,256]{1,0:T(8,128)S(1)} fusion(f32[640,256]{1,0:T(8,128)S(1)} %fusion.7, f32[640,256]{1,0:T(8,128)S(1)} %fusion.8, bf16[640,27,256]{2,0,1:T(8,128)(2,1)} %constant_dynamic-update-slice_fusion.3, f32[256,27,256]{2,0,1:T(8,128)S(1)} %copy-done.2), kind=kOutput, calls=%fused_computation.25 | convolution fusion | flops 2270560256 | bytes 17891328 | tf_op jit(solution)/shard_map/rop,poc->rc/dot_general | solution.py:71
  100.8 3.2 %fusion.20 = f32[27,256,256]{2,1,0:T(8,128)S(1)} fusion(bf16[640,27,256]{2,0,1:T(8,128)(2,1)S(1)} %bitcast.125, bf16[640,256]{1,0:T(8,128)(2,1)S(1)} %get-tuple-element.96), kind=kOutput, calls=%fused_computation.37 | convolution fusion | flops 2264924160 | bytes 16252928 | tf_op jit(solution)/shard_map/rq,rop->opq/dot_general | solution.py:71
  103.9 5.5 %fusion.22 = f32[27,256,256]{2,1,0:T(8,128)S(1)} fusion(bf16[640,27,256]{2,0,1:T(8,128)(2,1)} %constant_dynamic-update-slice_fusion.3, bf16[640,256]{1,0:T(8,128)(2,1)S(1)} %get-tuple-element.96), kind=kOutput, calls=%fused_computation.39 | convolution fusion | flops 2264924160 | bytes 16252928 | tf_op jit(solution)/shard_map/rq,rop->opq/dot_general | solution.py:71
  109.5 9.9 %add_add_fusion = f32[27,256,256]{2,1,0:T(8,128)} fusion(f32[27,256,256]{2,1,0:T(8,128)S(1)} %fusion.22, f32[27,256,256]{2,1,0:T(8,128)S(1)} %fusion.20, bf16[640,27,256]{2,0,1:T(8,128)(2,1)} %constant_dynamic-update-slice_fusion.3, bf16[640,256]{1,0:T(8,128)(2,1)S(1)} %get-tuple-element.95), kind=kOutput, calls=%fused_computation.3 | convolution fusion | flops 2268463104 | bytes 30408704 | tf_op jit(solution)/shard_map/rq,rop->opq/dot_general | solution.py:71
  120.1 2.2 %collective-permute-start.2 = (f32[1,40,8,256]{3,2,1,0:T(8,128)S(1)}, f32[1,40,8,256]{3,2,1,0:T(8,128)S(1)}, u32[]{:S(2)}, u32[]{:S(2)}) collective-permute-start(f32[1,40,8,256]{3,2,1,0:T(8,128)S(1)} %get-tuple-element.99), channel_id=1, source_target_pairs={{0,1},{1,2},{2,3},{3,4},{4,5},{5,6},{6,7},{7,8},{8,9},{9,10},{10,1... | collective-permute-start | bytes 983048 | tf_op jit(solution)/shard_map/ppermute | solution.py:17
  122.2 1.5 collective-permute-start.3
  123.8 2.7 %collective-permute-start.5 = (f32[6,256]{1,0:T(8,128)S(1)}, f32[6,256]{1,0:T(8,128)S(1)}, u32[]{:S(2)}, u32[]{:S(2)}) collective-permute-start(f32[6,256]{1,0:T(8,128)S(1)} %fusion.28), channel_id=1, source_target_pairs={{0,2},{1,3},{2,0},{3,1},{4,6},{5,7},{6,4},{7,5},{8,10},{9,11},{10,... | collective-permute-start | bytes 18440 | tf_op jit(solution)/shard_map/ppermute | solution.py:59
  126.5 4.9 %collective-permute-done.5 = f32[6,256]{1,0:T(8,128)S(1)} collective-permute-done((f32[6,256]{1,0:T(8,128)S(1)}, f32[6,256]{1,0:T(8,128)S(1)}, u32[]{:S(2)}, u32[]{:S(2)}) %collective-permute-start.5) | collective-permute-done | bytes 6176 | tf_op jit(solution)/shard_map/ppermute | solution.py:59
  131.4 2.9 %collective-permute-start.6 = (f32[6,256]{1,0:T(8,128)S(1)}, f32[6,256]{1,0:T(8,128)S(1)}, u32[]{:S(2)}, u32[]{:S(2)}) collective-permute-start(f32[6,256]{1,0:T(8,128)S(1)} %add.67), channel_id=1, source_target_pairs={{0,4},{1,5},{2,6},{3,7},{4,0},{5,1},{6,2},{7,3},{8,12},{9,13},{10,... | collective-permute-start | bytes 18440 | tf_op jit(solution)/shard_map/ppermute | solution.py:59
  134.3 1.6 collective-permute-done.6
  135.9 2.5 %collective-permute-start.7 = (f32[6,256]{1,0:T(8,128)S(1)}, f32[6,256]{1,0:T(8,128)S(1)}, u32[]{:S(2)}, u32[]{:S(2)}) collective-permute-start(f32[6,256]{1,0:T(8,128)S(1)} %add.68), channel_id=1, source_target_pairs={{0,8},{1,9},{2,10},{3,11},{4,12},{5,13},{6,14},{7,15},{8,0},{9,1},... | collective-permute-start | bytes 18440 | tf_op jit(solution)/shard_map/ppermute | solution.py:59
  138.5 2.0 collective-permute-done.7
  143.1 4.4 %fusion.30 = (f32[2,40,8,256]{3,2,1,0:T(8,128)}, f32[2,40,8,256]{3,2,1,0:T(8,128)}, f32[2,40,8,256]{3,2,1,0:T(8,128)}, f32[2,40,8,256]{3,2,1,0:T(8,128)}, f32[2,...) fusion(f32[4,42,10,256]{3,2,1,0:T(8,128)S(1)} %select_maximum_f, ...), kind=kLoop, calls=%fused_computation.137 | loop fusion | bytes 23592960 | tf_op jit(solution)/shard_map/slice | solution.py:38
  147.6 2.2 %constant_dynamic-update-slice_fusion.83 = f32[640,27,256]{2,0,1:T(8,128)} fusion(f32[640,1,256]{2,0,1:T(8,128)} %bitcast.144), kind=kLoop, calls=%fused_computation.124 | loop fusion | bytes 1310720
  149.8 1.6 maximum_maximum_fusion
  175.3 10.5 %fusion.41 = f32[640,256,1]{1,0,2:T(8,128)S(1)} fusion(f32[640,27,256]{2,0,1:T(8,128)} %constant_dynamic-update-slice_fusion.57, f32[256,27,256]{2,0,1:T(8,128)S(1)} %bitcast.122), kind=kOutput, calls=%fused_computation.148 | convolution fusion | flops 6794772480 | bytes 25427968 | tf_op jit(solution)/shard_map/roc,qoc->rq/dot_general | solution.py:50
  186.7 21.3 %reduce-scatter.2.cloned.1.call-done = f32[27,16,256]{2,1,0:T(8,128)} async-done(((f32[27,256,256]{2,1,0:T(8,128)}), f32[27,16,256]{2,1,0:T(8,128)}) %reduce-scatter.2.cloned.1.call-update) | async-done | bytes 442384 | tf_op jit(solution)/shard_map/reduce_scatter | solution.py:102
  (187 shorter events, 57.0 us)
Async XLA Ops:
  7.2 72.4 %all-gather.2.cloned.1.call-start = ((), (), s32[]{:S(2)}) async-start(), calls=%async_computation.1 | async-start | bytes 7520256 | tf_op jit(solution)/shard_map/all_gather | solution.py:82
  7.9 200.1 %reduce-scatter.2.cloned.1.call-start = ((), (), s32[]{:S(2)}) async-start(), calls=%async_computation.2 | async-start | bytes 7520256 | tf_op jit(solution)/shard_map/reduce_scatter | solution.py:102
  9.1 6.0 %collective-permute-start = (f32[1,40,8,256]{3,2,1,0:T(8,128)S(1)}, f32[1,40,8,256]{3,2,1,0:T(8,128)S(1)}, u32[]{:S(2)}, u32[]{:S(2)}) collective-permute-start(f32[1,40,8,256]{3,2,1,0:T(8,128)S(1)} %get-tuple-element.102), channel_id=1, source_target_pairs={{0,1},{1,2},{2,3},{3,4},{4,5},{5,6},{6,7},{7,8},{8,9},{9,10},{10,1... | collective-permute-start | bytes 983048 | tf_op jit(solution)/shard_map/ppermute | solution.py:17
  11.5 5.6 %collective-permute-start.1 = (f32[1,40,8,256]{3,2,1,0:T(8,128)S(1)}, f32[1,40,8,256]{3,2,1,0:T(8,128)S(1)}, u32[]{:S(2)}, u32[]{:S(2)}) collective-permute-start(f32[1,40,8,256]{3,2,1,0:T(8,128)S(1)} %get-tuple-element.101), channel_id=1, source_target_pairs={{1,0},{2,1},{3,2},{4,3},{5,4},{6,5},{7,6},{8,7},{9,8},{10,9},{11,1... | collective-permute-start | bytes 983048 | tf_op jit(solution)/shard_map/ppermute | solution.py:18
  87.7 13.0 %slice-start.2 = ((s8[8847360]{0:T(1024)(128)(4,1)}), s8[4194304]{0:T(1024)(128)(4,1)S(1)}, s32[]{:S(2)}) async-start(s8[8847360]{0:T(1024)(128)(4,1)} %bitcast.124), calls=%async_computation.5 | async-start | bytes 8388608
  87.7 13.0 %slice-start.3 = ((s8[8847360]{0:T(1024)(128)(4,1)}), s8[4194304]{0:T(1024)(128)(4,1)S(1)}, s32[]{:S(2)}) async-start(s8[8847360]{0:T(1024)(128)(4,1)} %bitcast.124), calls=%async_computation.6 | async-start | bytes 8388608
  109.5 9.9 %copy-start.28 = (s32[8]{0:T(128)S(1)}, s32[8]{0:T(128)}, u32[]{:S(2)}) copy-start(s32[8]{0:T(128)} %param.15) | copy-start | bytes 100
  119.7 4.1 %collective-permute-start.4 = (f32[6,256]{1,0:T(8,128)S(1)}, f32[6,256]{1,0:T(8,128)S(1)}, u32[]{:S(2)}, u32[]{:S(2)}) collective-permute-start(f32[6,256]{1,0:T(8,128)S(1)} %pad_maximum_fusion.6), channel_id=1, source_target_pairs={{0,1},{1,0},{2,3},{3,2},{4,5},{5,4},{6,7},{7,6},{8,9},{9,8},{10,11... | collective-permute-start | bytes 18440 | tf_op jit(solution)/shard_map/ppermute | solution.py:59
  120.1 21.6 %collective-permute-start.2 = (f32[1,40,8,256]{3,2,1,0:T(8,128)S(1)}, f32[1,40,8,256]{3,2,1,0:T(8,128)S(1)}, u32[]{:S(2)}, u32[]{:S(2)}) collective-permute-start(f32[1,40,8,256]{3,2,1,0:T(8,128)S(1)} %get-tuple-element.99), channel_id=1, source_target_pairs={{0,1},{1,2},{2,3},{3,4},{4,5},{5,6},{6,7},{7,8},{8,9},{9,10},{10,1... | collective-permute-start | bytes 983048 | tf_op jit(solution)/shard_map/ppermute | solution.py:17
  122.2 19.4 %collective-permute-start.3 = (f32[1,40,8,256]{3,2,1,0:T(8,128)S(1)}, f32[1,40,8,256]{3,2,1,0:T(8,128)S(1)}, u32[]{:S(2)}, u32[]{:S(2)}) collective-permute-start(f32[1,40,8,256]{3,2,1,0:T(8,128)S(1)} %get-tuple-element.100), channel_id=1, source_target_pairs={{1,0},{2,1},{3,2},{4,3},{5,4},{6,5},{7,6},{8,7},{9,8},{10,9},{11,1... | collective-permute-start | bytes 983048 | tf_op jit(solution)/shard_map/ppermute | solution.py:18
  123.8 7.6 %collective-permute-start.5 = (f32[6,256]{1,0:T(8,128)S(1)}, f32[6,256]{1,0:T(8,128)S(1)}, u32[]{:S(2)}, u32[]{:S(2)}) collective-permute-start(f32[6,256]{1,0:T(8,128)S(1)} %fusion.28), channel_id=1, source_target_pairs={{0,2},{1,3},{2,0},{3,1},{4,6},{5,7},{6,4},{7,5},{8,10},{9,11},{10,... | collective-permute-start | bytes 18440 | tf_op jit(solution)/shard_map/ppermute | solution.py:59
  131.4 4.5 %collective-permute-start.6 = (f32[6,256]{1,0:T(8,128)S(1)}, f32[6,256]{1,0:T(8,128)S(1)}, u32[]{:S(2)}, u32[]{:S(2)}) collective-permute-start(f32[6,256]{1,0:T(8,128)S(1)} %add.67), channel_id=1, source_target_pairs={{0,4},{1,5},{2,6},{3,7},{4,0},{5,1},{6,2},{7,3},{8,12},{9,13},{10,... | collective-permute-start | bytes 18440 | tf_op jit(solution)/shard_map/ppermute | solution.py:59
  135.9 4.5 %collective-permute-start.7 = (f32[6,256]{1,0:T(8,128)S(1)}, f32[6,256]{1,0:T(8,128)S(1)}, u32[]{:S(2)}, u32[]{:S(2)}) collective-permute-start(f32[6,256]{1,0:T(8,128)S(1)} %add.68), channel_id=1, source_target_pairs={{0,8},{1,9},{2,10},{3,11},{4,12},{5,13},{6,14},{7,15},{8,0},{9,1},... | collective-permute-start | bytes 18440 | tf_op jit(solution)/shard_map/ppermute | solution.py:59
  154.4 9.2 %copy-start.16 = (f32[2,40,8,256]{3,2,1,0:T(8,128)S(1)}, f32[2,40,8,256]{3,2,1,0:T(8,128)}, u32[]{:S(2)}) copy-start(f32[2,40,8,256]{3,2,1,0:T(8,128)} %get-tuple-element.16) | copy-start | bytes 1966084
  155.3 9.2 %copy-start.15 = (f32[2,40,8,256]{3,2,1,0:T(8,128)S(1)}, f32[2,40,8,256]{3,2,1,0:T(8,128)}, u32[]{:S(2)}) copy-start(f32[2,40,8,256]{3,2,1,0:T(8,128)} %get-tuple-element.15) | copy-start | bytes 1966084
  157.1 10.1 %copy-start.13 = (f32[2,40,8,256]{3,2,1,0:T(8,128)S(1)}, f32[2,40,8,256]{3,2,1,0:T(8,128)}, u32[]{:S(2)}) copy-start(f32[2,40,8,256]{3,2,1,0:T(8,128)} %get-tuple-element.13) | copy-start | bytes 1966084
  157.2 11.8 %copy-start.12 = (f32[2,40,8,256]{3,2,1,0:T(8,128)S(1)}, f32[2,40,8,256]{3,2,1,0:T(8,128)}, u32[]{:S(2)}) copy-start(f32[2,40,8,256]{3,2,1,0:T(8,128)} %get-tuple-element.12) | copy-start | bytes 1966084
  158.2 11.7 %copy-start.11 = (f32[2,40,8,256]{3,2,1,0:T(8,128)S(1)}, f32[2,40,8,256]{3,2,1,0:T(8,128)}, u32[]{:S(2)}) copy-start(f32[2,40,8,256]{3,2,1,0:T(8,128)} %get-tuple-element.11) | copy-start | bytes 1966084
  159.9 11.8 %copy-start.10 = (f32[2,40,8,256]{3,2,1,0:T(8,128)S(1)}, f32[2,40,8,256]{3,2,1,0:T(8,128)}, u32[]{:S(2)}) copy-start(f32[2,40,8,256]{3,2,1,0:T(8,128)} %get-tuple-element.10) | copy-start | bytes 1966084
  160.8 11.8 %copy-start.9 = (f32[2,40,8,256]{3,2,1,0:T(8,128)S(1)}, f32[2,40,8,256]{3,2,1,0:T(8,128)}, u32[]{:S(2)}) copy-start(f32[2,40,8,256]{3,2,1,0:T(8,128)} %get-tuple-element.9) | copy-start | bytes 1966084
  162.7 11.6 %copy-start.8 = (f32[2,40,8,256]{3,2,1,0:T(8,128)S(1)}, f32[2,40,8,256]{3,2,1,0:T(8,128)}, u32[]{:S(2)}) copy-start(f32[2,40,8,256]{3,2,1,0:T(8,128)} %get-tuple-element.8) | copy-start | bytes 1966084
  163.6 11.7 %slice-start = ((s8[7077888]{0:T(1024)(128)(4,1)}), s8[4194304]{0:T(1024)(128)(4,1)S(1)}, s32[]{:S(2)}) async-start(s8[7077888]{0:T(1024)(128)(4,1)} %bitcast.121), calls=%async_computation.3 | async-start | bytes 8388608
  174.4 33.7 %copy-start.1 = (f32[4,256]{1,0:T(4,128)S(1)}, f32[4,256]{1,0:T(4,128)}, u32[]{:S(2)}) copy-start(f32[4,256]{1,0:T(4,128)} %param.13) | copy-start | bytes 12292
  175.3 10.5 %copy-start.26 = (f32[2,40,8,256]{3,2,1,0:T(8,128)S(1)}, f32[2,40,8,256]{3,2,1,0:T(8,128)}, u32[]{:S(2)}) copy-start(f32[2,40,8,256]{3,2,1,0:T(8,128)} %param.9) | copy-start | bytes 1966084
  (20 other events, 126.0 us)
Sparse Core Ops, SparseCore 0:
  10.2 69.3 all-gather.1
  119.5 88.4 reduce-scatter.1

commit v8 on v6

--- a/solution.py
+++ b/solution.py
@@ -50,6 +50,14 @@
     return jnp.einsum("roc,qoc->rq", table, piece, precision=high)
 
 
+def stacked_product(delta_flat, table):
+    d_hi, d_lo = split_bf16(delta_flat)
+    t_hi, t_lo = split_bf16(table)
+    lhs = jnp.concatenate([d_hi, d_hi, d_lo], axis=0)
+    rhs = jnp.concatenate([t_hi, t_lo, t_hi], axis=0)
+    return jnp.einsum("rq,rop->opq", lhs, rhs, preferred_element_type=jnp.float32)
+
+
 def all_sum(x):
     count = lax.axis_size("space")
     if count & (count - 1):
@@ -59,6 +67,11 @@
         x = x + lax.ppermute(x, "space", [(i, i ^ bit) for i in range(count)])
         bit *= 2
     return x
+
+
+def split_bf16(x):
+    hi = lax.reduce_precision(x, exponent_bits=8, mantissa_bits=7)
+    return hi.astype(jnp.bfloat16), (x - hi).astype(jnp.bfloat16)
 
 
 def per_device(field, grad_out, weight, bias, land_bias, level_gain, land_mask, level_index):
@@ -88,7 +101,7 @@
     sums = all_sum(jnp.concatenate([local_bias[None], local_land[None], local_gain], axis=0))
     delta_flat = delta.reshape(-1, chans)
     grad_weight = lax.psum_scatter(
-        jnp.einsum("rq,rop->opq", delta_flat, table_pre, precision=high),
+        stacked_product(delta_flat, table_pre),
         "space",
         scatter_dimension=1,
         tiled=True,

time: 209 us -> 207 us (level)
  local copies, waits for them, and re-layouts: 74.8 us -> 58.4 us
  waiting for transfers between devices: 45.4 us -> 54 us
  other arithmetic: 12.4 us -> 20.1 us
  matrix products: 45.1 us -> 42.2 us
    unnamed x133 -> x135, local copies, waits for them, and re-layouts: 61.3 us -> 45.8 us
    all_gather x1, waiting for transfers between devices: 19.1 us -> 27.6 us  [per_device(): full_weight = lax.all_gather(weight, 'space', axis=0, tiled=True)]
    convert_element_type x0 -> x2, other arithmetic: none -> 7.44 us  [split_bf16(): return (hi.astype(jnp.bfloat16), (x - hi).astype(jnp.bfloat16))]
    dot_general x1, matrix products: 19.6 us -> 16.7 us  [stacked_product(): jnp.einsum('rq,rop->opq', lhs, rhs, preferred_element_type=jnp.float32)]
  transfers between devices with their start and end apart: 10 -> 10, of which waited for: 5 -> 5; matrix products, arithmetic and copies ran while one was open for 46% -> 39% of each run, Pallas kernels for 0% -> 0%
where the time goes in v8:
time: 207 us; the launch traced here: 206 us
  local copies, waits for them, and re-layouts  58.4 us (28%)
  waiting for transfers between devices  54 us (26%)
  matrix products  42.2 us (20%)
  other arithmetic  20.1 us (10%)
  starting transfers between devices  16.6 us (8%)
  between operations  14.8 us (7%)
    unnamed x135, local copies, waits for them, and re-layouts  45.8 us
    all_gather x1, waiting for transfers between devices, per_device(): full_weight = lax.all_gather(weight, 'space', axis=0, tiled=True)  27.6 us
    reduce_scatter x1, waiting for transfers between devices, per_device(): lax.psum_scatter(stacked_product(delta_flat, table_pre), 'space', scatter...  17.1 us
    dot_general x1, matrix products, stacked_product(): jnp.einsum('rq,rop->opq', lhs, rhs, preferred_element_type=jnp.float32)  16.7 us
    dot_general x1, matrix products, conv_piece(): return jnp.einsum('rop,poc->rc', table, piece, precision=high)  13.7 us
    dot_general x1, matrix products, back_piece(): return jnp.einsum('roc,qoc->rq', table, piece, precision=high)  10.7 us
    slice x3, local copies, waits for them, and re-layouts, window_table(): grid[lat_off:lat_off + out_rows, lon_off:lon_off + lon_n, lev_off:lev_off...  9.24 us
    ppermute x4, waiting for transfers between devices, all_sum(): x = x + lax.ppermute(x, 'space', [(i, i ^ bit) for i in range(count)])  8.57 us
  transfers between devices with their start and end apart: 10, of which 5 were waited for; matrix products, arithmetic and copies ran while one was open for 39% of the time, Pallas kernels for 0%

profile of v8, /device:TPU:0, one launch (start us, length us, event | category | flops | bytes accessed | tf_op | source)
XLA Modules:
  0.0 206.0 jit_solution(803695057500846920)
XLA Ops:
  10.4 3.1 %collective-permute-start = (f32[1,40,8,256]{3,2,1,0:T(8,128)S(1)}, f32[1,40,8,256]{3,2,1,0:T(8,128)S(1)}, u32[]{:S(2)}, u32[]{:S(2)}) collective-permute-start(f32[1,40,8,256]{3,2,1,0:T(8,128)S(1)} %get-tuple-element.78), channel_id=1, source_target_pairs={{0,1},{1,2},{2,3},{3,4},{4,5},{5,6},{6,7},{7,8},{8,9},{9,10},{10,1... | collective-permute-start | bytes 983048 | tf_op jit(solution)/shard_map/ppermute | solution.py:17
  15.8 2.5 %pad_maximum_fusion.4 = (f32[2,40,8,256]{3,2,1,0:T(8,128)}, f32[4,40,8,256]{3,2,1,0:T(8,128)S(1)}, f32[2,40,8,256]{3,2,1,0:T(8,128)}) fusion(f32[1,40,8,256]{3,2,1,0:T(8,128)S(1)} %collective-permute-done.1, f32[2,40,8,256]{3,2,1,0:T(8,128)} %param.8, f32[4,40,8,256]{3,2,1,0:T(8,128)S(1)} %constant_dynamic-update-slice_fusion.2, ...), kind=kLoop, calls=%fused_computation.43 | loop fusion | flops 327680 | bytes 3276800 | tf_op jit(solution)/shard_map/concatenate | solution.py:19
  19.8 4.4 %fusion.25 = (f32[2,40,8,256]{3,2,1,0:T(8,128)}, f32[2,40,8,256]{3,2,1,0:T(8,128)}, f32[2,40,8,256]{3,2,1,0:T(8,128)}, f32[2,40,8,256]{3,2,1,0:T(8,128)}, f32[2,...) fusion(f32[4,42,10,256]{3,2,1,0:T(8,128)S(1)} %select_maximum_f, ...), kind=kLoop, calls=%fused_computation.122 | loop fusion | bytes 23592960 | tf_op jit(solution)/shard_map/slice | solution.py:38
  25.7 3.1 %pad_maximum_fusion.3 = (f32[2,40,8,256]{3,2,1,0:T(8,128)S(1)}, f32[2,40,8,256]{3,2,1,0:T(8,128)S(1)}, f32[2,40,8,256]{3,2,1,0:T(8,128)S(1)}, f32[2,40,8,256]{3,...) fusion(f32[4,1,8,256]{3,2,1,0:T(8,128)} %copy-done.36, f32[4,40,8,256]{3,2,1,0:T(8,128)} %copy-done.3, ...), kind=kLoop, calls=%fused_computation.42 | loop fusion | flops 983040 | bytes 5308416 | tf_op jit(solution)/shard_map/concatenate | solution.py:24
  38.0 6.6 %copy-done.2 = f32[640,27,256]{2,0,1:T(8,128)} copy-done((f32[640,27,256]{2,0,1:T(8,128)}, f32[640,27,256]{2,0,1:T(8,128)S(1)}, u32[]{:S(2)}) %copy-start.2) | copy-done | bytes 17694744
  44.6 7.4 %fusion.6 = (bf16[640,27,256]{2,0,1:T(8,128)(2,1)}, bf16[640,27,256]{2,0,1:T(8,128)(2,1)}) fusion(f32[640,27,256]{2,0,1:T(8,128)S(1)} %constant_dynamic-update-slice_fusion.3), kind=kLoop, calls=%fused_computation.8 | loop fusion | flops 17694720 | bytes 35389440 | tf_op jit(solution)/shard_map/convert_element_type | solution.py:74
  52.0 27.6 %all-gather.2.cloned.1.call-done = f32[256,27,256]{2,0,1:T(8,128)} async-done(((f32[16,27,256]{2,0,1:T(8,128)}), f32[256,27,256]{2,0,1:T(8,128)}) %all-gather.2.cloned.1.call-update) | async-done | bytes 7077904 | tf_op jit(solution)/shard_map/all_gather | solution.py:84
  79.6 13.7 %fusion.32 = f32[640,256,1]{1,0,2:T(8,128)S(1)} fusion(f32[640,27,256]{2,0,1:T(8,128)} %copy-done.2, f32[256,27,256]{2,0,1:T(8,128)} %all-gather.2.cloned.1.call-done), kind=kOutput, calls=%fused_computation.129 | convolution fusion | flops 6794772480 | bytes 25427968 | tf_op jit(solution)/shard_map/rop,poc->rc/dot_general | solution.py:46
  93.9 16.7 %fusion = f32[27,256,256]{2,1,0:T(8,128)} fusion(bf16[640,27,256]{2,0,1:T(8,128)(2,1)} %get-tuple-element.9, bf16[640,27,256]{2,0,1:T(8,128)(2,1)} %get-tuple-element.8, bf16[640,256]{1,0:T(8,128)(2,1)S(1)} %get-tuple-element.69, bf16[640,256]{1,0:T(8,128)(2,1)S(1)} %get-tuple-element.68), kind=kOutput, calls=%fused_computation | convolution fusion | flops 6877347840 | bytes 25427968 | tf_op jit(solution)/shard_map/rq,rop->opq/dot_general | solution.py:58
  111.3 2.2 %collective-permute-start.2 = (f32[1,40,8,256]{3,2,1,0:T(8,128)S(1)}, f32[1,40,8,256]{3,2,1,0:T(8,128)S(1)}, u32[]{:S(2)}, u32[]{:S(2)}) collective-permute-start(f32[1,40,8,256]{3,2,1,0:T(8,128)S(1)} %get-tuple-element.72), channel_id=1, source_target_pairs={{0,1},{1,2},{2,3},{3,4},{4,5},{5,6},{6,7},{7,8},{8,9},{9,10},{10,1... | collective-permute-start | bytes 983048 | tf_op jit(solution)/shard_map/ppermute | solution.py:17
  113.5 1.5 collective-permute-start.3
  115.0 2.7 %collective-permute-start.5 = (f32[6,256]{1,0:T(8,128)S(1)}, f32[6,256]{1,0:T(8,128)S(1)}, u32[]{:S(2)}, u32[]{:S(2)}) collective-permute-start(f32[6,256]{1,0:T(8,128)S(1)} %fusion.22), channel_id=1, source_target_pairs={{0,2},{1,3},{2,0},{3,1},{4,6},{5,7},{6,4},{7,5},{8,10},{9,11},{10,... | collective-permute-start | bytes 18440 | tf_op jit(solution)/shard_map/ppermute | solution.py:67
  117.7 4.9 %collective-permute-done.5 = f32[6,256]{1,0:T(8,128)S(1)} collective-permute-done((f32[6,256]{1,0:T(8,128)S(1)}, f32[6,256]{1,0:T(8,128)S(1)}, u32[]{:S(2)}, u32[]{:S(2)}) %collective-permute-start.5) | collective-permute-done | bytes 6176 | tf_op jit(solution)/shard_map/ppermute | solution.py:67
  122.6 2.9 %collective-permute-start.6 = (f32[6,256]{1,0:T(8,128)S(1)}, f32[6,256]{1,0:T(8,128)S(1)}, u32[]{:S(2)}, u32[]{:S(2)}) collective-permute-start(f32[6,256]{1,0:T(8,128)S(1)} %add.51), channel_id=1, source_target_pairs={{0,4},{1,5},{2,6},{3,7},{4,0},{5,1},{6,2},{7,3},{8,12},{9,13},{10,... | collective-permute-start | bytes 18440 | tf_op jit(solution)/shard_map/ppermute | solution.py:67
  125.5 1.6 collective-permute-done.6
  127.2 2.5 %collective-permute-start.7 = (f32[6,256]{1,0:T(8,128)S(1)}, f32[6,256]{1,0:T(8,128)S(1)}, u32[]{:S(2)}, u32[]{:S(2)}) collective-permute-start(f32[6,256]{1,0:T(8,128)S(1)} %add.52), channel_id=1, source_target_pairs={{0,8},{1,9},{2,10},{3,11},{4,12},{5,13},{6,14},{7,15},{8,0},{9,1},... | collective-permute-start | bytes 18440 | tf_op jit(solution)/shard_map/ppermute | solution.py:67
  129.7 2.0 collective-permute-done.7
  134.4 4.4 %fusion.24 = (f32[2,40,8,256]{3,2,1,0:T(8,128)}, f32[2,40,8,256]{3,2,1,0:T(8,128)}, f32[2,40,8,256]{3,2,1,0:T(8,128)}, f32[2,40,8,256]{3,2,1,0:T(8,128)}, f32[2,...) fusion(f32[4,42,10,256]{3,2,1,0:T(8,128)S(1)} %select_maximum_f, ...), kind=kLoop, calls=%fused_computation.121 | loop fusion | bytes 23592960 | tf_op jit(solution)/shard_map/slice | solution.py:38
  138.9 2.3 %constant_dynamic-update-slice_fusion.56 = f32[640,27,256]{2,0,1:T(8,128)} fusion(f32[640,1,256]{2,0,1:T(8,128)} %bitcast.118), kind=kLoop, calls=%fused_computation.107 | loop fusion | bytes 1310720
  141.1 1.9 maximum_maximum_fusion
  144.4 2.1 %constant_dynamic-update-slice_fusion.54 = f32[640,27,256]{2,0,1:T(8,128)} fusion(f32[640,27,256]{2,0,1:T(8,128)} %constant_dynamic-update-slice_fusion.55, f32[640,1,256]{2,0,1:T(8,128)} %bitcast.114), kind=kLoop, calls=%fused_computation.105 | loop fusion | bytes 1310720
  146.5 2.0 constant_dynamic-update-slice_fusion.53
  170.5 10.7 %fusion.33 = f32[640,256,1]{1,0,2:T(8,128)S(1)} fusion(f32[640,27,256]{2,0,1:T(8,128)} %constant_dynamic-update-slice_fusion.30, f32[256,27,256]{2,0,1:T(8,128)S(1)} %bitcast.79), kind=kOutput, calls=%fused_computation.130 | convolution fusion | flops 6794772480 | bytes 25427968 | tf_op jit(solution)/shard_map/roc,qoc->rq/dot_general | solution.py:50
  182.1 17.1 %reduce-scatter.2.cloned.1.call-done = f32[27,16,256]{2,1,0:T(8,128)} async-done(((f32[27,256,256]{2,1,0:T(8,128)}), f32[27,16,256]{2,1,0:T(8,128)}) %reduce-scatter.2.cloned.1.call-update) | async-done | bytes 442384 | tf_op jit(solution)/shard_map/reduce_scatter | solution.py:103
  (168 shorter events, 45.3 us)
Async XLA Ops:
  7.2 72.4 %all-gather.2.cloned.1.call-start = ((), (), s32[]{:S(2)}) async-start(), calls=%async_computation.1 | async-start | bytes 7520256 | tf_op jit(solution)/shard_map/all_gather | solution.py:84
  7.9 191.2 %reduce-scatter.2.cloned.1.call-start = ((), (), s32[]{:S(2)}) async-start(), calls=%async_computation.2 | async-start | bytes 7520256 | tf_op jit(solution)/shard_map/reduce_scatter | solution.py:103
  9.1 6.7 %collective-permute-start.1 = (f32[1,40,8,256]{3,2,1,0:T(8,128)S(1)}, f32[1,40,8,256]{3,2,1,0:T(8,128)S(1)}, u32[]{:S(2)}, u32[]{:S(2)}) collective-permute-start(f32[1,40,8,256]{3,2,1,0:T(8,128)S(1)} %get-tuple-element.77), channel_id=1, source_target_pairs={{1,0},{2,1},{3,2},{4,3},{5,4},{6,5},{7,6},{8,7},{9,8},{10,9},{11,1... | collective-permute-start | bytes 983048 | tf_op jit(solution)/shard_map/ppermute | solution.py:18
  10.4 5.4 %collective-permute-start = (f32[1,40,8,256]{3,2,1,0:T(8,128)S(1)}, f32[1,40,8,256]{3,2,1,0:T(8,128)S(1)}, u32[]{:S(2)}, u32[]{:S(2)}) collective-permute-start(f32[1,40,8,256]{3,2,1,0:T(8,128)S(1)} %get-tuple-element.78), channel_id=1, source_target_pairs={{0,1},{1,2},{2,3},{3,4},{4,5},{5,6},{6,7},{7,8},{8,9},{9,10},{10,1... | collective-permute-start | bytes 983048 | tf_op jit(solution)/shard_map/ppermute | solution.py:17
  52.0 41.4 %copy-start.33 = (f32[2,40,8,256]{3,2,1,0:T(8,128)S(1)}, f32[2,40,8,256]{3,2,1,0:T(8,128)}, u32[]{:S(2)}) copy-start(f32[2,40,8,256]{3,2,1,0:T(8,128)} %param.9) | copy-start | bytes 1966084
  52.0 41.4 %copy-start.37 = (f32[256]{0:T(256)S(1)}, f32[256]{0:T(256)}, u32[]{:S(2)}) copy-start(f32[256]{0:T(256)} %param.11) | copy-start | bytes 3076
  110.9 4.0 %collective-permute-start.4 = (f32[6,256]{1,0:T(8,128)S(1)}, f32[6,256]{1,0:T(8,128)S(1)}, u32[]{:S(2)}, u32[]{:S(2)}) collective-permute-start(f32[6,256]{1,0:T(8,128)S(1)} %pad_maximum_fusion.10), channel_id=1, source_target_pairs={{0,1},{1,0},{2,3},{3,2},{4,5},{5,4},{6,7},{7,6},{8,9},{9,8},{10,11... | collective-permute-start | bytes 18440 | tf_op jit(solution)/shard_map/ppermute | solution.py:67
  111.3 21.6 %collective-permute-start.2 = (f32[1,40,8,256]{3,2,1,0:T(8,128)S(1)}, f32[1,40,8,256]{3,2,1,0:T(8,128)S(1)}, u32[]{:S(2)}, u32[]{:S(2)}) collective-permute-start(f32[1,40,8,256]{3,2,1,0:T(8,128)S(1)} %get-tuple-element.72), channel_id=1, source_target_pairs={{0,1},{1,2},{2,3},{3,4},{4,5},{5,6},{6,7},{7,8},{8,9},{9,10},{10,1... | collective-permute-start | bytes 983048 | tf_op jit(solution)/shard_map/ppermute | solution.py:17
  113.5 19.4 %collective-permute-start.3 = (f32[1,40,8,256]{3,2,1,0:T(8,128)S(1)}, f32[1,40,8,256]{3,2,1,0:T(8,128)S(1)}, u32[]{:S(2)}, u32[]{:S(2)}) collective-permute-start(f32[1,40,8,256]{3,2,1,0:T(8,128)S(1)} %get-tuple-element.73), channel_id=1, source_target_pairs={{1,0},{2,1},{3,2},{4,3},{5,4},{6,5},{7,6},{8,7},{9,8},{10,9},{11,1... | collective-permute-start | bytes 983048 | tf_op jit(solution)/shard_map/ppermute | solution.py:18
  115.0 7.6 %collective-permute-start.5 = (f32[6,256]{1,0:T(8,128)S(1)}, f32[6,256]{1,0:T(8,128)S(1)}, u32[]{:S(2)}, u32[]{:S(2)}) collective-permute-start(f32[6,256]{1,0:T(8,128)S(1)} %fusion.22), channel_id=1, source_target_pairs={{0,2},{1,3},{2,0},{3,1},{4,6},{5,7},{6,4},{7,5},{8,10},{9,11},{10,... | collective-permute-start | bytes 18440 | tf_op jit(solution)/shard_map/ppermute | solution.py:67
  122.6 4.5 %collective-permute-start.6 = (f32[6,256]{1,0:T(8,128)S(1)}, f32[6,256]{1,0:T(8,128)S(1)}, u32[]{:S(2)}, u32[]{:S(2)}) collective-permute-start(f32[6,256]{1,0:T(8,128)S(1)} %add.51), channel_id=1, source_target_pairs={{0,4},{1,5},{2,6},{3,7},{4,0},{5,1},{6,2},{7,3},{8,12},{9,13},{10,... | collective-permute-start | bytes 18440 | tf_op jit(solution)/shard_map/ppermute | solution.py:67
  127.2 4.5 %collective-permute-start.7 = (f32[6,256]{1,0:T(8,128)S(1)}, f32[6,256]{1,0:T(8,128)S(1)}, u32[]{:S(2)}, u32[]{:S(2)}) collective-permute-start(f32[6,256]{1,0:T(8,128)S(1)} %add.52), channel_id=1, source_target_pairs={{0,8},{1,9},{2,10},{3,11},{4,12},{5,13},{6,14},{7,15},{8,0},{9,1},... | collective-permute-start | bytes 18440 | tf_op jit(solution)/shard_map/ppermute | solution.py:67
  138.8 18.1 %copy-start.23 = (f32[2,40,8,256]{3,2,1,0:T(8,128)S(1)}, f32[2,40,8,256]{3,2,1,0:T(8,128)}, u32[]{:S(2)}) copy-start(f32[2,40,8,256]{3,2,1,0:T(8,128)} %get-tuple-element.19) | copy-start | bytes 1966084
  138.8 20.0 %copy-start.20 = (f32[2,40,8,256]{3,2,1,0:T(8,128)S(1)}, f32[2,40,8,256]{3,2,1,0:T(8,128)}, u32[]{:S(2)}) copy-start(f32[2,40,8,256]{3,2,1,0:T(8,128)} %get-tuple-element.18) | copy-start | bytes 1966084
  138.9 20.9 %copy-start.19 = (f32[2,40,8,256]{3,2,1,0:T(8,128)S(1)}, f32[2,40,8,256]{3,2,1,0:T(8,128)}, u32[]{:S(2)}) copy-start(f32[2,40,8,256]{3,2,1,0:T(8,128)} %get-tuple-element.17) | copy-start | bytes 1966084
  141.1 20.4 %copy-start.16 = (f32[2,40,8,256]{3,2,1,0:T(8,128)S(1)}, f32[2,40,8,256]{3,2,1,0:T(8,128)}, u32[]{:S(2)}) copy-start(f32[2,40,8,256]{3,2,1,0:T(8,128)} %get-tuple-element.16) | copy-start | bytes 1966084
  141.1 21.3 %copy-start.15 = (f32[2,40,8,256]{3,2,1,0:T(8,128)S(1)}, f32[2,40,8,256]{3,2,1,0:T(8,128)}, u32[]{:S(2)}) copy-start(f32[2,40,8,256]{3,2,1,0:T(8,128)} %get-tuple-element.15) | copy-start | bytes 1966084
  143.1 21.1 %copy-start.12 = (f32[2,40,8,256]{3,2,1,0:T(8,128)S(1)}, f32[2,40,8,256]{3,2,1,0:T(8,128)}, u32[]{:S(2)}) copy-start(f32[2,40,8,256]{3,2,1,0:T(8,128)} %get-tuple-element.14) | copy-start | bytes 1966084
  143.1 22.0 %copy-start.11 = (f32[2,40,8,256]{3,2,1,0:T(8,128)S(1)}, f32[2,40,8,256]{3,2,1,0:T(8,128)}, u32[]{:S(2)}) copy-start(f32[2,40,8,256]{3,2,1,0:T(8,128)} %get-tuple-element.13) | copy-start | bytes 1966084
  143.5 23.4 %copy-start.9 = (f32[2,40,8,256]{3,2,1,0:T(8,128)S(1)}, f32[2,40,8,256]{3,2,1,0:T(8,128)}, u32[]{:S(2)}) copy-start(f32[2,40,8,256]{3,2,1,0:T(8,128)} %get-tuple-element.12) | copy-start | bytes 1966084
  143.5 24.3 %copy-start.8 = (f32[2,40,8,256]{3,2,1,0:T(8,128)S(1)}, f32[2,40,8,256]{3,2,1,0:T(8,128)}, u32[]{:S(2)}) copy-start(f32[2,40,8,256]{3,2,1,0:T(8,128)} %get-tuple-element.11) | copy-start | bytes 1966084
  143.5 26.1 %copy-start.7 = (f32[2,40,8,256]{3,2,1,0:T(8,128)S(1)}, f32[2,40,8,256]{3,2,1,0:T(8,128)}, u32[]{:S(2)}) copy-start(f32[2,40,8,256]{3,2,1,0:T(8,128)} %get-tuple-element.10) | copy-start | bytes 1966084
  144.4 26.1 %slice-start = ((s8[7077888]{0:T(1024)(128)(4,1)}), s8[4194304]{0:T(1024)(128)(4,1)S(1)}, s32[]{:S(2)}) async-start(s8[7077888]{0:T(1024)(128)(4,1)} %bitcast.78), calls=%async_computation.3 | async-start | bytes 8388608
  166.9 32.3 %copy-start.1 = (f32[4,256]{1,0:T(4,128)S(1)}, f32[4,256]{1,0:T(4,128)}, u32[]{:S(2)}) copy-start(f32[4,256]{1,0:T(4,128)} %param.13) | copy-start | bytes 12292
  (27 other events, 303.6 us)
Sparse Core Ops, SparseCore 0:
  10.2 69.3 all-gather.1
  110.7 88.3 reduce-scatter.1

commit v9 on v8

--- a/solution.py
+++ b/solution.py
@@ -50,6 +50,14 @@
     return jnp.einsum("roc,qoc->rq", table, piece, precision=high)
 
 
+def stacked_conv(table, weight):
+    t_hi, t_lo = split_bf16(table)
+    w_hi, w_lo = split_bf16(weight)
+    lhs = jnp.concatenate([t_hi, t_hi, t_lo], axis=2)
+    rhs = jnp.concatenate([w_hi, w_lo, w_hi], axis=0)
+    return jnp.einsum("rop,poc->rc", lhs, rhs, preferred_element_type=jnp.float32)
+
+
 def stacked_product(delta_flat, table):
     d_hi, d_lo = split_bf16(delta_flat)
     t_hi, t_lo = split_bf16(table)
@@ -84,7 +92,7 @@
     full_weight = lax.all_gather(weight, "space", axis=0, tiled=True)
     grid_pre = wrap_levels(with_halo(field, (("space", 0),), 1))
     table_pre = window_table(grid_pre, rows, False)
-    conv = conv_piece(table_pre, full_weight)
+    conv = stacked_conv(table_pre, full_weight)
     conv = conv.reshape(rows, lon_n, lev_n, chans)
     pre = conv + bias + land_float[:, :, None, None] * land_bias
     sigma = jax.nn.sigmoid(pre)

time: 207 us -> 215 us (1.039)
  waiting for transfers between devices: 54 us -> 61.1 us
  local copies, waits for them, and re-layouts: 58.4 us -> 51.6 us
  other arithmetic: 20.1 us -> 26.1 us
  matrix products: 42.2 us -> 44.8 us
    unnamed x135 -> x133, local copies, waits for them, and re-layouts: 45.8 us -> 39.1 us
    all_gather x1, waiting for transfers between devices: 27.6 us -> 32.6 us  [per_device(): full_weight = lax.all_gather(weight, 'space', axis=0, tiled=True)]
    convert_element_type x2 -> x3, other arithmetic: 7.44 us -> 12.2 us  [split_bf16(): return (hi.astype(jnp.bfloat16), (x - hi).astype(jnp.bfloat16))]
    dot_general x1, matrix products: 13.7 us -> 16.9 us  [stacked_conv(): jnp.einsum('rop,poc->rc', lhs, rhs, preferred_element_type=jnp.float32)]
  transfers between devices with their start and end apart: 10 -> 10, of which waited for: 5 -> 6; matrix products, arithmetic and copies ran while one was open for 39% -> 38% of each run, Pallas kernels for 0% -> 0%
where the time goes in v9:
time: 215 us; the launch traced here: 214 us
  waiting for transfers between devices  61.1 us (28%)
  local copies, waits for them, and re-layouts  51.6 us (24%)
  matrix products  44.8 us (21%)
  other arithmetic  26.1 us (12%)
  starting transfers between devices  15.9 us (7%)
  between operations  14.8 us (7%)
    unnamed x133, local copies, waits for them, and re-layouts  39.1 us
    all_gather x1, waiting for transfers between devices, per_device(): full_weight = lax.all_gather(weight, 'space', axis=0, tiled=True)  32.6 us
    reduce_scatter x1, waiting for transfers between devices, per_device(): lax.psum_scatter(stacked_product(delta_flat, table_pre), 'space', scatter...  17.3 us
    dot_general x1, matrix products, stacked_conv(): jnp.einsum('rop,poc->rc', lhs, rhs, preferred_element_type=jnp.float32)  16.9 us
    dot_general x1, matrix products, stacked_product(): jnp.einsum('rq,rop->opq', lhs, rhs, preferred_element_type=jnp.float32)  16.1 us
    convert_element_type x3, other arithmetic, split_bf16(): return (hi.astype(jnp.bfloat16), (x - hi).astype(jnp.bfloat16))  12.2 us
    dot_general x1, matrix products, back_piece(): return jnp.einsum('roc,qoc->rq', table, piece, precision=high)  10.7 us
    slice x3, local copies, waits for them, and re-layouts, window_table(): grid[lat_off:lat_off + out_rows, lon_off:lon_off + lon_n, lev_off:lev_off...  9.2 us
  transfers between devices with their start and end apart: 10, of which 6 were waited for; matrix products, arithmetic and copies ran while one was open for 38% of the time, Pallas kernels for 0%

profile of v9, /device:TPU:0, one launch (start us, length us, event | category | flops | bytes accessed | tf_op | source)
XLA Modules:
  0.0 214.3 jit_solution(11030249365054954580)
XLA Ops:
  9.1 2.4 %collective-permute-start = (f32[1,40,8,256]{3,2,1,0:T(8,128)S(1)}, f32[1,40,8,256]{3,2,1,0:T(8,128)S(1)}, u32[]{:S(2)}, u32[]{:S(2)}) collective-permute-start(f32[1,40,8,256]{3,2,1,0:T(8,128)S(1)} %get-tuple-element.80), channel_id=1, source_target_pairs={{0,1},{1,2},{2,3},{3,4},{4,5},{5,6},{6,7},{7,8},{8,9},{9,10},{10,1... | collective-permute-start | bytes 983048 | tf_op jit(solution)/shard_map/ppermute | solution.py:17
  15.1 2.0 collective-permute-done.1
  17.1 2.6 %pad_maximum_fusion.4 = (f32[2,40,8,256]{3,2,1,0:T(8,128)}, f32[4,40,8,256]{3,2,1,0:T(8,128)S(1)}, f32[2,40,8,256]{3,2,1,0:T(8,128)}) fusion(f32[1,40,8,256]{3,2,1,0:T(8,128)S(1)} %collective-permute-done.1, f32[2,40,8,256]{3,2,1,0:T(8,128)} %param.8, f32[4,40,8,256]{3,2,1,0:T(8,128)S(1)} %constant_dynamic-update-slice_fusion.2, ...), kind=kLoop, calls=%fused_computation.57 | loop fusion | flops 327680 | bytes 3276800 | tf_op jit(solution)/shard_map/concatenate | solution.py:19
  21.3 4.4 %fusion.38 = (f32[2,40,8,256]{3,2,1,0:T(8,128)}, f32[2,40,8,256]{3,2,1,0:T(8,128)}, f32[2,40,8,256]{3,2,1,0:T(8,128)}, f32[2,40,8,256]{3,2,1,0:T(8,128)}, f32[2,...) fusion(f32[4,42,10,256]{3,2,1,0:T(8,128)S(1)} %select_maximum_f, ...), kind=kLoop, calls=%fused_computation.137 | loop fusion | bytes 23592960 | tf_op jit(solution)/shard_map/slice | solution.py:38
  27.1 3.2 %pad_maximum_fusion.3 = (f32[2,40,8,256]{3,2,1,0:T(8,128)S(1)}, f32[2,40,8,256]{3,2,1,0:T(8,128)S(1)}, f32[2,40,8,256]{3,2,1,0:T(8,128)S(1)}, f32[2,40,8,256]{3,...) fusion(f32[4,1,8,256]{3,2,1,0:T(8,128)} %copy-done.35, f32[4,40,8,256]{3,2,1,0:T(8,128)} %copy-done.2, ...), kind=kLoop, calls=%fused_computation.56 | loop fusion | flops 983040 | bytes 5308416 | tf_op jit(solution)/shard_map/concatenate | solution.py:24
  39.4 7.5 %reduce-precision_convert_fusion = (bf16[640,27,256]{2,0,1:T(8,128)(2,1)}, bf16[640,27,256]{2,0,1:T(8,128)(2,1)}) fusion(f32[640,27,256]{2,0,1:T(8,128)S(1)} %constant_dynamic-update-slice_fusion.3), kind=kLoop, calls=%fused_computation.13 | loop fusion | flops 17694720 | bytes 35389440 | tf_op jit(solution)/shard_map/convert_element_type | solution.py:82
  47.0 32.6 %all-gather.2.cloned.1.call-done = f32[256,27,256]{2,0,1:T(8,128)} async-done(((f32[16,27,256]{2,0,1:T(8,128)}), f32[256,27,256]{2,0,1:T(8,128)}) %all-gather.2.cloned.1.call-update) | async-done | bytes 7077904 | tf_op jit(solution)/shard_map/all_gather | solution.py:92
  79.6 4.5 %fusion.18 = (bf16[256,27,256]{2,0,1:T(8,128)(2,1)S(1)}, bf16[256,27,256]{2,0,1:T(8,128)(2,1)S(1)}) fusion(f32[256,27,256]{2,0,1:T(8,128)} %all-gather.2.cloned.1.call-done), kind=kLoop, calls=%fused_computation.22 | loop fusion | flops 7077888 | bytes 14155776 | tf_op jit(solution)/shard_map/convert_element_type | solution.py:82
  84.1 16.9 %fusion = f32[640,256,1]{1,0,2:T(8,128)} fusion(bf16[640,27,256]{2,0,1:T(8,128)(2,1)} %get-tuple-element.9, bf16[640,27,256]{2,0,1:T(8,128)(2,1)} %get-tuple-element.8, bf16[256,27,256]{2,0,1:T(8,128)(2,1)S(1)} %get-tuple-element.11, bf16[256,27,256]{2,0,1:T(8,128)(2,1)S(1)} %get-tuple-element.10), kind=kOutput, calls=%fused_computation | convolution fusion | flops 6906249216 | bytes 25427968 | tf_op jit(solution)/shard_map/rop,poc->rc/dot_general | solution.py:58
  102.7 16.1 %fusion.6 = f32[27,256,256]{2,1,0:T(8,128)} fusion(bf16[640,27,256]{2,0,1:T(8,128)(2,1)} %get-tuple-element.8, bf16[640,27,256]{2,0,1:T(8,128)(2,1)} %get-tuple-element.9, bf16[640,256]{1,0:T(8,128)(2,1)S(1)} %get-tuple-element.71, bf16[640,256]{1,0:T(8,128)(2,1)S(1)} %get-tuple-element.70), kind=kOutput, calls=%fused_computation.6 | convolution fusion | flops 6877347840 | bytes 25427968 | tf_op jit(solution)/shard_map/rq,rop->opq/dot_general | solution.py:66
  119.4 2.2 %collective-permute-start.2 = (f32[1,40,8,256]{3,2,1,0:T(8,128)S(1)}, f32[1,40,8,256]{3,2,1,0:T(8,128)S(1)}, u32[]{:S(2)}, u32[]{:S(2)}) collective-permute-start(f32[1,40,8,256]{3,2,1,0:T(8,128)S(1)} %get-tuple-element.74), channel_id=1, source_target_pairs={{0,1},{1,2},{2,3},{3,4},{4,5},{5,6},{6,7},{7,8},{8,9},{9,10},{10,1... | collective-permute-start | bytes 983048 | tf_op jit(solution)/shard_map/ppermute | solution.py:17
  123.1 2.7 %collective-permute-start.5 = (f32[6,256]{1,0:T(8,128)S(1)}, f32[6,256]{1,0:T(8,128)S(1)}, u32[]{:S(2)}, u32[]{:S(2)}) collective-permute-start(f32[6,256]{1,0:T(8,128)S(1)} %fusion.35), channel_id=1, source_target_pairs={{0,2},{1,3},{2,0},{3,1},{4,6},{5,7},{6,4},{7,5},{8,10},{9,11},{10,... | collective-permute-start | bytes 18440 | tf_op jit(solution)/shard_map/ppermute | solution.py:75
  125.8 4.9 %collective-permute-done.5 = f32[6,256]{1,0:T(8,128)S(1)} collective-permute-done((f32[6,256]{1,0:T(8,128)S(1)}, f32[6,256]{1,0:T(8,128)S(1)}, u32[]{:S(2)}, u32[]{:S(2)}) %collective-permute-start.5) | collective-permute-done | bytes 6176 | tf_op jit(solution)/shard_map/ppermute | solution.py:75
  130.8 2.9 %collective-permute-start.6 = (f32[6,256]{1,0:T(8,128)S(1)}, f32[6,256]{1,0:T(8,128)S(1)}, u32[]{:S(2)}, u32[]{:S(2)}) collective-permute-start(f32[6,256]{1,0:T(8,128)S(1)} %add.51), channel_id=1, source_target_pairs={{0,4},{1,5},{2,6},{3,7},{4,0},{5,1},{6,2},{7,3},{8,12},{9,13},{10,... | collective-permute-start | bytes 18440 | tf_op jit(solution)/shard_map/ppermute | solution.py:75
  133.7 1.6 collective-permute-done.6
  135.3 2.5 %collective-permute-start.7 = (f32[6,256]{1,0:T(8,128)S(1)}, f32[6,256]{1,0:T(8,128)S(1)}, u32[]{:S(2)}, u32[]{:S(2)}) collective-permute-start(f32[6,256]{1,0:T(8,128)S(1)} %add.52), channel_id=1, source_target_pairs={{0,8},{1,9},{2,10},{3,11},{4,12},{5,13},{6,14},{7,15},{8,0},{9,1},... | collective-permute-start | bytes 18440 | tf_op jit(solution)/shard_map/ppermute | solution.py:75
  137.9 2.0 collective-permute-done.7
  142.5 4.4 %fusion.37 = (f32[2,40,8,256]{3,2,1,0:T(8,128)}, f32[2,40,8,256]{3,2,1,0:T(8,128)}, f32[2,40,8,256]{3,2,1,0:T(8,128)}, f32[2,40,8,256]{3,2,1,0:T(8,128)}, f32[2,...) fusion(f32[4,42,10,256]{3,2,1,0:T(8,128)S(1)} %select_maximum_f, ...), kind=kLoop, calls=%fused_computation.136 | loop fusion | bytes 23592960 | tf_op jit(solution)/shard_map/slice | solution.py:38
  147.0 2.2 %constant_dynamic-update-slice_fusion.56 = f32[640,27,256]{2,0,1:T(8,128)} fusion(f32[640,1,256]{2,0,1:T(8,128)} %bitcast.115), kind=kLoop, calls=%fused_computation.121 | loop fusion | bytes 1310720
  149.2 2.0 maximum_maximum_fusion
  152.5 2.1 constant_dynamic-update-slice_fusion.54
  154.6 2.0 constant_dynamic-update-slice_fusion.53
  178.6 10.7 %fusion.45 = f32[640,256,1]{1,0,2:T(8,128)S(1)} fusion(f32[640,27,256]{2,0,1:T(8,128)} %constant_dynamic-update-slice_fusion.30, f32[256,27,256]{2,0,1:T(8,128)S(1)} %bitcast.77), kind=kOutput, calls=%fused_computation.144 | convolution fusion | flops 6794772480 | bytes 25427968 | tf_op jit(solution)/shard_map/roc,qoc->rq/dot_general | solution.py:50
  190.2 17.3 %reduce-scatter.2.cloned.1.call-done = f32[27,16,256]{2,1,0:T(8,128)} async-done(((f32[27,256,256]{2,1,0:T(8,128)}), f32[27,16,256]{2,1,0:T(8,128)}) %reduce-scatter.2.cloned.1.call-update) | async-done | bytes 442384 | tf_op jit(solution)/shard_map/reduce_scatter | solution.py:111
  (167 shorter events, 47.8 us)
Async XLA Ops:
  7.2 72.4 %all-gather.2.cloned.1.call-start = ((), (), s32[]{:S(2)}) async-start(), calls=%async_computation.1 | async-start | bytes 7520256 | tf_op jit(solution)/shard_map/all_gather | solution.py:92
  7.9 199.5 %reduce-scatter.2.cloned.1.call-start = ((), (), s32[]{:S(2)}) async-start(), calls=%async_computation.2 | async-start | bytes 7520256 | tf_op jit(solution)/shard_map/reduce_scatter | solution.py:111
  9.1 6.0 %collective-permute-start = (f32[1,40,8,256]{3,2,1,0:T(8,128)S(1)}, f32[1,40,8,256]{3,2,1,0:T(8,128)S(1)}, u32[]{:S(2)}, u32[]{:S(2)}) collective-permute-start(f32[1,40,8,256]{3,2,1,0:T(8,128)S(1)} %get-tuple-element.80), channel_id=1, source_target_pairs={{0,1},{1,2},{2,3},{3,4},{4,5},{5,6},{6,7},{7,8},{8,9},{9,10},{10,1... | collective-permute-start | bytes 983048 | tf_op jit(solution)/shard_map/ppermute | solution.py:17
  11.5 5.6 %collective-permute-start.1 = (f32[1,40,8,256]{3,2,1,0:T(8,128)S(1)}, f32[1,40,8,256]{3,2,1,0:T(8,128)S(1)}, u32[]{:S(2)}, u32[]{:S(2)}) collective-permute-start(f32[1,40,8,256]{3,2,1,0:T(8,128)S(1)} %get-tuple-element.79), channel_id=1, source_target_pairs={{1,0},{2,1},{3,2},{4,3},{5,4},{6,5},{7,6},{8,7},{9,8},{10,9},{11,1... | collective-permute-start | bytes 983048 | tf_op jit(solution)/shard_map/ppermute | solution.py:18
  21.3 17.3 %copy-start.3 = (f32[2,40,8,256]{3,2,1,0:T(8,128)S(1)}, f32[2,40,8,256]{3,2,1,0:T(8,128)}, u32[]{:S(2)}) copy-start(f32[2,40,8,256]{3,2,1,0:T(8,128)} %param.8) | copy-start | bytes 1966084
  119.0 4.0 %collective-permute-start.4 = (f32[6,256]{1,0:T(8,128)S(1)}, f32[6,256]{1,0:T(8,128)S(1)}, u32[]{:S(2)}, u32[]{:S(2)}) collective-permute-start(f32[6,256]{1,0:T(8,128)S(1)} %pad_maximum_fusion.10), channel_id=1, source_target_pairs={{0,1},{1,0},{2,3},{3,2},{4,5},{5,4},{6,7},{7,6},{8,9},{9,8},{10,11... | collective-permute-start | bytes 18440 | tf_op jit(solution)/shard_map/ppermute | solution.py:75
  119.4 21.6 %collective-permute-start.2 = (f32[1,40,8,256]{3,2,1,0:T(8,128)S(1)}, f32[1,40,8,256]{3,2,1,0:T(8,128)S(1)}, u32[]{:S(2)}, u32[]{:S(2)}) collective-permute-start(f32[1,40,8,256]{3,2,1,0:T(8,128)S(1)} %get-tuple-element.74), channel_id=1, source_target_pairs={{0,1},{1,2},{2,3},{3,4},{4,5},{5,6},{6,7},{7,8},{8,9},{9,10},{10,1... | collective-permute-start | bytes 983048 | tf_op jit(solution)/shard_map/ppermute | solution.py:17
  121.6 19.4 %collective-permute-start.3 = (f32[1,40,8,256]{3,2,1,0:T(8,128)S(1)}, f32[1,40,8,256]{3,2,1,0:T(8,128)S(1)}, u32[]{:S(2)}, u32[]{:S(2)}) collective-permute-start(f32[1,40,8,256]{3,2,1,0:T(8,128)S(1)} %get-tuple-element.75), channel_id=1, source_target_pairs={{1,0},{2,1},{3,2},{4,3},{5,4},{6,5},{7,6},{8,7},{9,8},{10,9},{11,1... | collective-permute-start | bytes 983048 | tf_op jit(solution)/shard_map/ppermute | solution.py:18
  123.1 7.6 %collective-permute-start.5 = (f32[6,256]{1,0:T(8,128)S(1)}, f32[6,256]{1,0:T(8,128)S(1)}, u32[]{:S(2)}, u32[]{:S(2)}) collective-permute-start(f32[6,256]{1,0:T(8,128)S(1)} %fusion.35), channel_id=1, source_target_pairs={{0,2},{1,3},{2,0},{3,1},{4,6},{5,7},{6,4},{7,5},{8,10},{9,11},{10,... | collective-permute-start | bytes 18440 | tf_op jit(solution)/shard_map/ppermute | solution.py:75
  130.8 4.5 %collective-permute-start.6 = (f32[6,256]{1,0:T(8,128)S(1)}, f32[6,256]{1,0:T(8,128)S(1)}, u32[]{:S(2)}, u32[]{:S(2)}) collective-permute-start(f32[6,256]{1,0:T(8,128)S(1)} %add.51), channel_id=1, source_target_pairs={{0,4},{1,5},{2,6},{3,7},{4,0},{5,1},{6,2},{7,3},{8,12},{9,13},{10,... | collective-permute-start | bytes 18440 | tf_op jit(solution)/shard_map/ppermute | solution.py:75
  135.3 4.5 %collective-permute-start.7 = (f32[6,256]{1,0:T(8,128)S(1)}, f32[6,256]{1,0:T(8,128)S(1)}, u32[]{:S(2)}, u32[]{:S(2)}) collective-permute-start(f32[6,256]{1,0:T(8,128)S(1)} %add.52), channel_id=1, source_target_pairs={{0,8},{1,9},{2,10},{3,11},{4,12},{5,13},{6,14},{7,15},{8,0},{9,1},... | collective-permute-start | bytes 18440 | tf_op jit(solution)/shard_map/ppermute | solution.py:75
  146.9 17.2 %copy-start.23 = (f32[2,40,8,256]{3,2,1,0:T(8,128)S(1)}, f32[2,40,8,256]{3,2,1,0:T(8,128)}, u32[]{:S(2)}) copy-start(f32[2,40,8,256]{3,2,1,0:T(8,128)} %get-tuple-element.22) | copy-start | bytes 1966084
  146.9 18.1 %copy-start.22 = (f32[2,40,8,256]{3,2,1,0:T(8,128)S(1)}, f32[2,40,8,256]{3,2,1,0:T(8,128)}, u32[]{:S(2)}) copy-start(f32[2,40,8,256]{3,2,1,0:T(8,128)} %get-tuple-element.21) | copy-start | bytes 1966084
  146.9 20.0 %copy-start.19 = (f32[2,40,8,256]{3,2,1,0:T(8,128)S(1)}, f32[2,40,8,256]{3,2,1,0:T(8,128)}, u32[]{:S(2)}) copy-start(f32[2,40,8,256]{3,2,1,0:T(8,128)} %get-tuple-element.20) | copy-start | bytes 1966084
  146.9 20.9 %copy-start.18 = (f32[2,40,8,256]{3,2,1,0:T(8,128)S(1)}, f32[2,40,8,256]{3,2,1,0:T(8,128)}, u32[]{:S(2)}) copy-start(f32[2,40,8,256]{3,2,1,0:T(8,128)} %get-tuple-element.19) | copy-start | bytes 1966084
  149.2 20.4 %copy-start.15 = (f32[2,40,8,256]{3,2,1,0:T(8,128)S(1)}, f32[2,40,8,256]{3,2,1,0:T(8,128)}, u32[]{:S(2)}) copy-start(f32[2,40,8,256]{3,2,1,0:T(8,128)} %get-tuple-element.18) | copy-start | bytes 1966084
  149.2 21.3 %copy-start.14 = (f32[2,40,8,256]{3,2,1,0:T(8,128)S(1)}, f32[2,40,8,256]{3,2,1,0:T(8,128)}, u32[]{:S(2)}) copy-start(f32[2,40,8,256]{3,2,1,0:T(8,128)} %get-tuple-element.17) | copy-start | bytes 1966084
  151.2 21.1 %copy-start.11 = (f32[2,40,8,256]{3,2,1,0:T(8,128)S(1)}, f32[2,40,8,256]{3,2,1,0:T(8,128)}, u32[]{:S(2)}) copy-start(f32[2,40,8,256]{3,2,1,0:T(8,128)} %get-tuple-element.16) | copy-start | bytes 1966084
  151.2 22.0 %copy-start.10 = (f32[2,40,8,256]{3,2,1,0:T(8,128)S(1)}, f32[2,40,8,256]{3,2,1,0:T(8,128)}, u32[]{:S(2)}) copy-start(f32[2,40,8,256]{3,2,1,0:T(8,128)} %get-tuple-element.15) | copy-start | bytes 1966084
  151.6 23.4 %copy-start.8 = (f32[2,40,8,256]{3,2,1,0:T(8,128)S(1)}, f32[2,40,8,256]{3,2,1,0:T(8,128)}, u32[]{:S(2)}) copy-start(f32[2,40,8,256]{3,2,1,0:T(8,128)} %get-tuple-element.14) | copy-start | bytes 1966084
  151.6 24.3 %copy-start.7 = (f32[2,40,8,256]{3,2,1,0:T(8,128)S(1)}, f32[2,40,8,256]{3,2,1,0:T(8,128)}, u32[]{:S(2)}) copy-start(f32[2,40,8,256]{3,2,1,0:T(8,128)} %get-tuple-element.13) | copy-start | bytes 1966084
  151.6 26.1 %copy-start.6 = (f32[2,40,8,256]{3,2,1,0:T(8,128)S(1)}, f32[2,40,8,256]{3,2,1,0:T(8,128)}, u32[]{:S(2)}) copy-start(f32[2,40,8,256]{3,2,1,0:T(8,128)} %get-tuple-element.12) | copy-start | bytes 1966084
  152.5 26.1 %slice-start = ((s8[7077888]{0:T(1024)(128)(4,1)}), s8[4194304]{0:T(1024)(128)(4,1)S(1)}, s32[]{:S(2)}) async-start(s8[7077888]{0:T(1024)(128)(4,1)} %bitcast.76), calls=%async_computation.3 | async-start | bytes 8388608
  175.0 32.5 %copy-start.1 = (f32[4,256]{1,0:T(4,128)S(1)}, f32[4,256]{1,0:T(4,128)}, u32[]{:S(2)}) copy-start(f32[4,256]{1,0:T(4,128)} %param.13) | copy-start | bytes 12292
  (26 other events, 295.1 us)
Sparse Core Ops, SparseCore 0:
  10.2 69.3 all-gather.1
  118.9 88.5 reduce-scatter.1

commit v10 on v8

--- a/solution.py
+++ b/solution.py
@@ -58,6 +58,14 @@
     return jnp.einsum("rq,rop->opq", lhs, rhs, preferred_element_type=jnp.float32)
 
 
+def stacked_back(table, weight):
+    t_hi, t_lo = split_bf16(table)
+    w_hi, w_lo = split_bf16(weight)
+    lhs = jnp.concatenate([t_hi, t_hi, t_lo], axis=2)
+    rhs = jnp.concatenate([w_hi, w_lo, w_hi], axis=2)
+    return jnp.einsum("roc,qoc->rq", lhs, rhs, preferred_element_type=jnp.float32)
+
+
 def all_sum(x):
     count = lax.axis_size("space")
     if count & (count - 1):
@@ -92,7 +100,7 @@
     delta = grad_out * gains * sigma * (1.0 + pre * (1.0 - sigma))
     delta_pad = with_halo(delta, (("space", 0),), 1)
     delta_table = window_table(wrap_levels(delta_pad), rows, True)
-    back = back_piece(delta_table, full_weight)
+    back = stacked_back(delta_table, full_weight)
     grad_field = grad_out + back.reshape(rows, lon_n, lev_n, chans)
     local_bias = jnp.sum(delta, axis=(0, 1, 2))
     local_land = jnp.sum(land_float[:, :, None, None] * delta, axis=(0, 1, 2))

time: 207 us -> 211 us (1.019)
  local copies, waits for them, and re-layouts: 58.4 us -> 35.2 us
  other arithmetic: 20.1 us -> 35.8 us
  waiting for transfers between devices: 54 us -> 61.6 us
  matrix products: 42.2 us -> 49 us
  starting transfers between devices: 16.6 us -> 13.9 us
    unnamed x135 -> x133, local copies, waits for them, and re-layouts: 45.8 us -> 23.6 us
    convert_element_type x2 -> x4, other arithmetic: 7.44 us -> 23.1 us  [split_bf16(): return (hi.astype(jnp.bfloat16), (x - hi).astype(jnp.bfloat16))]
    reduce_scatter x1, waiting for transfers between devices: 17.1 us -> 31.8 us  [per_device(): lax.psum_scatter(stacked_product(delta_flat, table_pre), 'space', scatter...]
    ppermute x4, waiting for transfers between devices: 8.57 us -> 0.82 us  [all_sum(): x = x + lax.ppermute(x, 'space', [(i, i ^ bit) for i in range(count)])]
    dot_general x1, matrix products: 10.7 us -> 17.5 us  [stacked_back(): jnp.einsum('roc,qoc->rq', lhs, rhs, preferred_element_type=jnp.float32)]
  transfers between devices with their start and end apart: 10 -> 10, of which waited for: 5 -> 4; matrix products, arithmetic and copies ran while one was open for 39% -> 46% of each run, Pallas kernels for 0% -> 0%
where the time goes in v10:
time: 211 us
  waiting for transfers between devices  61.6 us (29%)
  matrix products  49 us (23%)
  other arithmetic  35.8 us (17%)
  local copies, waits for them, and re-layouts  35.2 us (17%)
  between operations  15.1 us (7%)
  starting transfers between devices  13.9 us (7%)
    reduce_scatter x1, waiting for transfers between devices, per_device(): lax.psum_scatter(stacked_product(delta_flat, table_pre), 'space', scatter...  31.8 us
    all_gather x1, waiting for transfers between devices, per_device(): full_weight = lax.all_gather(weight, 'space', axis=0, tiled=True)  26.2 us
    unnamed x133, local copies, waits for them, and re-layouts  23.6 us
    convert_element_type x4, other arithmetic, split_bf16(): return (hi.astype(jnp.bfloat16), (x - hi).astype(jnp.bfloat16))  23.1 us
    dot_general x1, matrix products, stacked_back(): jnp.einsum('roc,qoc->rq', lhs, rhs, preferred_element_type=jnp.float32)  17.5 us
    dot_general x1, matrix products, stacked_product(): jnp.einsum('rq,rop->opq', lhs, rhs, preferred_element_type=jnp.float32)  16.7 us
    dot_general x1, matrix products, conv_piece(): return jnp.einsum('rop,poc->rc', table, piece, precision=high)  13.7 us
    slice x3, local copies, waits for them, and re-layouts, window_table(): grid[lat_off:lat_off + out_rows, lon_off:lon_off + lon_n, lev_off:lev_off...  9.19 us
  transfers between devices with their start and end apart: 10, of which 4 were waited for; matrix products, arithmetic and copies ran while one was open for 46% of the time, Pallas kernels for 0%

profile of v10, /device:TPU:0, one launch (start us, length us, event | category | flops | bytes accessed | tf_op | source)
XLA Modules:
  0.0 210.6 jit_solution(1743325610506453593)
XLA Ops:
  9.1 2.4 %collective-permute-start = (f32[1,40,8,256]{3,2,1,0:T(8,128)S(1)}, f32[1,40,8,256]{3,2,1,0:T(8,128)S(1)}, u32[]{:S(2)}, u32[]{:S(2)}) collective-permute-start(f32[1,40,8,256]{3,2,1,0:T(8,128)S(1)} %get-tuple-element.82), channel_id=1, source_target_pairs={{0,1},{1,2},{2,3},{3,4},{4,5},{5,6},{6,7},{7,8},{8,9},{9,10},{10,1... | collective-permute-start | bytes 983048 | tf_op jit(solution)/shard_map/ppermute | solution.py:17
  11.5 1.3 collective-permute-start.1
  15.1 2.0 collective-permute-done.1
  17.1 2.5 %pad_maximum_fusion.4 = (f32[2,40,8,256]{3,2,1,0:T(8,128)}, f32[4,40,8,256]{3,2,1,0:T(8,128)S(1)}, f32[2,40,8,256]{3,2,1,0:T(8,128)}) fusion(f32[1,40,8,256]{3,2,1,0:T(8,128)S(1)} %collective-permute-done.1, f32[2,40,8,256]{3,2,1,0:T(8,128)} %param.8, f32[4,40,8,256]{3,2,1,0:T(8,128)S(1)} %constant_dynamic-update-slice_fusion.2, ...), kind=kLoop, calls=%fused_computation.60 | loop fusion | flops 327680 | bytes 3276800 | tf_op jit(solution)/shard_map/concatenate | solution.py:19
  21.1 4.4 %fusion.39 = (f32[2,40,8,256]{3,2,1,0:T(8,128)}, f32[2,40,8,256]{3,2,1,0:T(8,128)}, f32[2,40,8,256]{3,2,1,0:T(8,128)}, f32[2,40,8,256]{3,2,1,0:T(8,128)}, f32[2,...) fusion(f32[4,42,10,256]{3,2,1,0:T(8,128)S(1)} %select_maximum_f, ...), kind=kLoop, calls=%fused_computation.140 | loop fusion | bytes 23592960 | tf_op jit(solution)/shard_map/slice | solution.py:38
  25.7 1.3 constant_dynamic-update-slice_fusion.29
  26.9 3.2 %pad_maximum_fusion.3 = (f32[2,40,8,256]{3,2,1,0:T(8,128)S(1)}, f32[2,40,8,256]{3,2,1,0:T(8,128)S(1)}, f32[2,40,8,256]{3,2,1,0:T(8,128)S(1)}, f32[2,40,8,256]{3,...) fusion(f32[4,1,8,256]{3,2,1,0:T(8,128)} %copy-done.37, f32[4,40,8,256]{3,2,1,0:T(8,128)} %copy-done.3, ...), kind=kLoop, calls=%fused_computation.59 | loop fusion | flops 983040 | bytes 5308416 | tf_op jit(solution)/shard_map/concatenate | solution.py:24
  39.3 6.7 %copy-done.2 = f32[640,27,256]{2,0,1:T(8,128)} copy-done((f32[640,27,256]{2,0,1:T(8,128)}, f32[640,27,256]{2,0,1:T(8,128)S(1)}, u32[]{:S(2)}) %copy-start.2) | copy-done | bytes 17694744
  46.0 7.4 %fusion.13 = (bf16[640,27,256]{2,0,1:T(8,128)(2,1)}, bf16[640,27,256]{2,0,1:T(8,128)(2,1)}) fusion(f32[640,27,256]{2,0,1:T(8,128)S(1)} %constant_dynamic-update-slice_fusion.3), kind=kLoop, calls=%fused_computation.17 | loop fusion | flops 17694720 | bytes 35389440 | tf_op jit(solution)/shard_map/convert_element_type | solution.py:82
  53.4 26.2 %all-gather.2.cloned.1.call-done = f32[256,27,256]{2,0,1:T(8,128)} async-done(((f32[16,27,256]{2,0,1:T(8,128)}), f32[256,27,256]{2,0,1:T(8,128)}) %all-gather.2.cloned.1.call-update) | async-done | bytes 7077904 | tf_op jit(solution)/shard_map/all_gather | solution.py:92
  79.6 13.7 %fusion.46 = f32[640,256,1]{1,0,2:T(8,128)S(1)} fusion(f32[640,27,256]{2,0,1:T(8,128)} %copy-done.2, f32[256,27,256]{2,0,1:T(8,128)} %all-gather.2.cloned.1.call-done), kind=kOutput, calls=%fused_computation.147 | convolution fusion | flops 6794772480 | bytes 25427968 | tf_op jit(solution)/shard_map/rop,poc->rc/dot_general | solution.py:46
  95.9 16.7 %fusion.6 = f32[27,256,256]{2,1,0:T(8,128)} fusion(bf16[640,27,256]{2,0,1:T(8,128)(2,1)} %get-tuple-element.9, bf16[640,27,256]{2,0,1:T(8,128)(2,1)} %get-tuple-element.8, bf16[640,256]{1,0:T(8,128)(2,1)S(1)} %get-tuple-element.73, bf16[640,256]{1,0:T(8,128)(2,1)S(1)} %get-tuple-element.72), kind=kOutput, calls=%fused_computation.6 | convolution fusion | flops 6877347840 | bytes 25427968 | tf_op jit(solution)/shard_map/rq,rop->opq/dot_general | solution.py:58
  112.6 1.3 collective-permute-start.6
  114.1 1.6 collective-permute-start.2
  115.7 1.5 collective-permute-start.3
  117.2 4.7 %collective-permute-start.7 = (f32[6,256]{1,0:T(8,128)S(1)}, f32[6,256]{1,0:T(8,128)S(1)}, u32[]{:S(2)}, u32[]{:S(2)}) collective-permute-start(f32[6,256]{1,0:T(8,128)S(1)} %add.52), channel_id=1, source_target_pairs={{0,8},{1,9},{2,10},{3,11},{4,12},{5,13},{6,14},{7,15},{8,0},{9,1},... | collective-permute-start | bytes 18440 | tf_op jit(solution)/shard_map/ppermute | solution.py:75
  121.9 8.2 %fusion.19 = (bf16[256,27,256]{2,0,1:T(8,128)(2,1)}, bf16[256,27,256]{2,0,1:T(8,128)(2,1)}) fusion(f32[256,27,256]{2,0,1:T(8,128)} %all-gather.2.cloned.1.call-done), kind=kLoop, calls=%fused_computation.25 | loop fusion | flops 7077888 | bytes 14155776 | tf_op jit(solution)/shard_map/convert_element_type | solution.py:82
  132.7 4.4 %fusion.38 = (f32[2,40,8,256]{3,2,1,0:T(8,128)}, f32[2,40,8,256]{3,2,1,0:T(8,128)}, f32[2,40,8,256]{3,2,1,0:T(8,128)}, f32[2,40,8,256]{3,2,1,0:T(8,128)}, f32[2,...) fusion(f32[4,42,10,256]{3,2,1,0:T(8,128)S(1)} %select_maximum_f, ...), kind=kLoop, calls=%fused_computation.139 | loop fusion | bytes 23592960 | tf_op jit(solution)/shard_map/slice | solution.py:38
  137.2 1.3 constant_dynamic-update-slice_fusion.56
  138.5 1.9 maximum_maximum_fusion
  140.9 1.3 constant_dynamic-update-slice_fusion.54
  145.9 7.5 %reduce-precision_convert_fusion.1 = (bf16[640,27,256]{2,0,1:T(8,128)(2,1)}, bf16[640,27,256]{2,0,1:T(8,128)(2,1)}) fusion(f32[640,27,256]{2,0,1:T(8,128)S(1)} %constant_dynamic-update-slice_fusion.30), kind=kLoop, calls=%fused_computation.15 | loop fusion | flops 17694720 | bytes 35389440 | tf_op jit(solution)/shard_map/convert_element_type | solution.py:82
  153.4 17.5 %fusion = f32[640,256,1]{1,0,2:T(8,128)S(1)} fusion(bf16[640,27,256]{2,0,1:T(8,128)(2,1)} %get-tuple-element.11, bf16[640,27,256]{2,0,1:T(8,128)(2,1)} %get-tuple-element.10, bf16[256,27,256]{2,0,1:T(8,128)(2,1)} %get-tuple-element.13, bf16[256,27,256]{2,0,1:T(8,128)(2,1)S(1)} %copy-done.7), kind=kOutput, calls=%fused_computation | convolution fusion | flops 6906249216 | bytes 25427968 | tf_op jit(solution)/shard_map/roc,qoc->rq/dot_general | solution.py:66
  171.9 31.8 %reduce-scatter.2.cloned.1.call-done = f32[27,16,256]{2,1,0:T(8,128)} async-done(((f32[27,256,256]{2,1,0:T(8,128)}), f32[27,16,256]{2,1,0:T(8,128)}) %reduce-scatter.2.cloned.1.call-update) | async-done | bytes 442384 | tf_op jit(solution)/shard_map/reduce_scatter | solution.py:111
  (167 shorter events, 24.7 us)
Async XLA Ops:
  7.2 72.4 %all-gather.2.cloned.1.call-start = ((), (), s32[]{:S(2)}) async-start(), calls=%async_computation.1 | async-start | bytes 7520256 | tf_op jit(solution)/shard_map/all_gather | solution.py:92
  7.9 195.8 %reduce-scatter.2.cloned.1.call-start = ((), (), s32[]{:S(2)}) async-start(), calls=%async_computation.2 | async-start | bytes 7520256 | tf_op jit(solution)/shard_map/reduce_scatter | solution.py:111
  9.1 6.0 %collective-permute-start = (f32[1,40,8,256]{3,2,1,0:T(8,128)S(1)}, f32[1,40,8,256]{3,2,1,0:T(8,128)S(1)}, u32[]{:S(2)}, u32[]{:S(2)}) collective-permute-start(f32[1,40,8,256]{3,2,1,0:T(8,128)S(1)} %get-tuple-element.82), channel_id=1, source_target_pairs={{0,1},{1,2},{2,3},{3,4},{4,5},{5,6},{6,7},{7,8},{8,9},{9,10},{10,1... | collective-permute-start | bytes 983048 | tf_op jit(solution)/shard_map/ppermute | solution.py:17
  11.5 5.6 %collective-permute-start.1 = (f32[1,40,8,256]{3,2,1,0:T(8,128)S(1)}, f32[1,40,8,256]{3,2,1,0:T(8,128)S(1)}, u32[]{:S(2)}, u32[]{:S(2)}) collective-permute-start(f32[1,40,8,256]{3,2,1,0:T(8,128)S(1)} %get-tuple-element.81), channel_id=1, source_target_pairs={{1,0},{2,1},{3,2},{4,3},{5,4},{6,5},{7,6},{8,7},{9,8},{10,9},{11,1... | collective-permute-start | bytes 983048 | tf_op jit(solution)/shard_map/ppermute | solution.py:18
  21.1 17.3 %copy-start.4 = (f32[2,40,8,256]{3,2,1,0:T(8,128)S(1)}, f32[2,40,8,256]{3,2,1,0:T(8,128)}, u32[]{:S(2)}) copy-start(f32[2,40,8,256]{3,2,1,0:T(8,128)} %param.8) | copy-start | bytes 1966084
  25.6 12.9 %copy-start.27 = (f32[2,40,8,256]{3,2,1,0:T(8,128)S(1)}, f32[2,40,8,256]{3,2,1,0:T(8,128)}, u32[]{:S(2)}) copy-start(f32[2,40,8,256]{3,2,1,0:T(8,128)} %get-tuple-element.40) | copy-start | bytes 1966084
  25.6 13.0 %copy-start.26 = (f32[2,40,8,256]{3,2,1,0:T(8,128)S(1)}, f32[2,40,8,256]{3,2,1,0:T(8,128)}, u32[]{:S(2)}) copy-start(f32[2,40,8,256]{3,2,1,0:T(8,128)} %get-tuple-element.39) | copy-start | bytes 1966084
  25.6 13.1 %copy-start.23 = (f32[2,40,8,256]{3,2,1,0:T(8,128)S(1)}, f32[2,40,8,256]{3,2,1,0:T(8,128)}, u32[]{:S(2)}) copy-start(f32[2,40,8,256]{3,2,1,0:T(8,128)} %get-tuple-element.38) | copy-start | bytes 1966084
  25.6 13.1 %copy-start.22 = (f32[2,40,8,256]{3,2,1,0:T(8,128)S(1)}, f32[2,40,8,256]{3,2,1,0:T(8,128)}, u32[]{:S(2)}) copy-start(f32[2,40,8,256]{3,2,1,0:T(8,128)} %get-tuple-element.37) | copy-start | bytes 1966084
  25.6 13.2 %copy-start.19 = (f32[2,40,8,256]{3,2,1,0:T(8,128)S(1)}, f32[2,40,8,256]{3,2,1,0:T(8,128)}, u32[]{:S(2)}) copy-start(f32[2,40,8,256]{3,2,1,0:T(8,128)} %get-tuple-element.36) | copy-start | bytes 1966084
  25.6 13.3 %copy-start.18 = (f32[2,40,8,256]{3,2,1,0:T(8,128)S(1)}, f32[2,40,8,256]{3,2,1,0:T(8,128)}, u32[]{:S(2)}) copy-start(f32[2,40,8,256]{3,2,1,0:T(8,128)} %get-tuple-element.35) | copy-start | bytes 1966084
  25.6 13.4 %copy-start.36 = (f32[2,40,8,256]{3,2,1,0:T(8,128)S(1)}, f32[2,40,8,256]{3,2,1,0:T(8,128)}, u32[]{:S(2)}) copy-start(f32[2,40,8,256]{3,2,1,0:T(8,128)} %get-tuple-element.78) | copy-start | bytes 1966084
  25.6 13.4 %copy-start.15 = (f32[2,40,8,256]{3,2,1,0:T(8,128)S(1)}, f32[2,40,8,256]{3,2,1,0:T(8,128)}, u32[]{:S(2)}) copy-start(f32[2,40,8,256]{3,2,1,0:T(8,128)} %get-tuple-element.34) | copy-start | bytes 1966084
  53.4 40.0 %copy-start.34 = (f32[2,40,8,256]{3,2,1,0:T(8,128)S(1)}, f32[2,40,8,256]{3,2,1,0:T(8,128)}, u32[]{:S(2)}) copy-start(f32[2,40,8,256]{3,2,1,0:T(8,128)} %param.9) | copy-start | bytes 1966084
  53.4 40.0 %copy-start.38 = (f32[256]{0:T(256)S(1)}, f32[256]{0:T(256)}, u32[]{:S(2)}) copy-start(f32[256]{0:T(256)} %param.11) | copy-start | bytes 3076
  53.4 40.4 %copy-start.39 = (s32[8]{0:T(128)S(1)}, s32[8]{0:T(128)}, u32[]{:S(2)}) copy-start(s32[8]{0:T(128)} %param.15) | copy-start | bytes 100
  94.0 1.2 collective-permute-start.4
  95.3 17.3 %collective-permute-start.5 = (f32[6,256]{1,0:T(8,128)S(1)}, f32[6,256]{1,0:T(8,128)S(1)}, u32[]{:S(2)}, u32[]{:S(2)}) collective-permute-start(f32[6,256]{1,0:T(8,128)S(1)} %fusion.36), channel_id=1, source_target_pairs={{0,2},{1,3},{2,0},{3,1},{4,6},{5,7},{6,4},{7,5},{8,10},{9,11},{10,... | collective-permute-start | bytes 18440 | tf_op jit(solution)/shard_map/ppermute | solution.py:75
  112.6 4.5 %collective-permute-start.6 = (f32[6,256]{1,0:T(8,128)S(1)}, f32[6,256]{1,0:T(8,128)S(1)}, u32[]{:S(2)}, u32[]{:S(2)}) collective-permute-start(f32[6,256]{1,0:T(8,128)S(1)} %add.51), channel_id=1, source_target_pairs={{0,4},{1,5},{2,6},{3,7},{4,0},{5,1},{6,2},{7,3},{8,12},{9,13},{10,... | collective-permute-start | bytes 18440 | tf_op jit(solution)/shard_map/ppermute | solution.py:75
  114.1 17.2 %collective-permute-start.2 = (f32[1,40,8,256]{3,2,1,0:T(8,128)S(1)}, f32[1,40,8,256]{3,2,1,0:T(8,128)S(1)}, u32[]{:S(2)}, u32[]{:S(2)}) collective-permute-start(f32[1,40,8,256]{3,2,1,0:T(8,128)S(1)} %get-tuple-element.76), channel_id=1, source_target_pairs={{0,1},{1,2},{2,3},{3,4},{4,5},{5,6},{6,7},{7,8},{8,9},{9,10},{10,1... | collective-permute-start | bytes 983048 | tf_op jit(solution)/shard_map/ppermute | solution.py:17
  115.7 15.6 %collective-permute-start.3 = (f32[1,40,8,256]{3,2,1,0:T(8,128)S(1)}, f32[1,40,8,256]{3,2,1,0:T(8,128)S(1)}, u32[]{:S(2)}, u32[]{:S(2)}) collective-permute-start(f32[1,40,8,256]{3,2,1,0:T(8,128)S(1)} %get-tuple-element.77), channel_id=1, source_target_pairs={{1,0},{2,1},{3,2},{4,3},{5,4},{6,5},{7,6},{8,7},{9,8},{10,9},{11,1... | collective-permute-start | bytes 983048 | tf_op jit(solution)/shard_map/ppermute | solution.py:18
  117.2 12.9 %collective-permute-start.7 = (f32[6,256]{1,0:T(8,128)S(1)}, f32[6,256]{1,0:T(8,128)S(1)}, u32[]{:S(2)}, u32[]{:S(2)}) collective-permute-start(f32[6,256]{1,0:T(8,128)S(1)} %add.52), channel_id=1, source_target_pairs={{0,8},{1,9},{2,10},{3,11},{4,12},{5,13},{6,14},{7,15},{8,0},{9,1},... | collective-permute-start | bytes 18440 | tf_op jit(solution)/shard_map/ppermute | solution.py:75
  153.4 17.5 %copy-start.35 = (f32[2,40,8,256]{3,2,1,0:T(8,128)S(1)}, f32[2,40,8,256]{3,2,1,0:T(8,128)}, u32[]{:S(2)}) copy-start(f32[2,40,8,256]{3,2,1,0:T(8,128)} %param.9) | copy-start | bytes 1966084
  153.4 50.3 %copy-start.1 = (f32[4,256]{1,0:T(4,128)S(1)}, f32[4,256]{1,0:T(4,128)}, u32[]{:S(2)}) copy-start(f32[4,256]{1,0:T(4,128)} %param.13) | copy-start | bytes 12292
  (26 other events, 172.8 us)
Sparse Core Ops, SparseCore 0:
  10.2 69.3 all-gather.1
  114.2 89.5 reduce-scatter.1
